TPU v7x, 32 devices: a whole 2x2x4 slice. The times are simulated.
32 devices in a mesh: gy: 16 (over z, y, core), gz: 2 (over x).
Axes of the slice: x: 2, y: 2, z: 4, core: 2. Of those that a mesh axis runs over, the one named last changes fastest.
Arguments:
- mag_start: float32 [2, 256, 256, 256], P(None, 'gy', 'gz'), may hold values from -3 to 3
- mag_middle: float32 [2, 256, 256, 256], P(None, 'gy', 'gz'), may hold values from -3 to 3
- adjoint_end: float32 [2, 256, 256, 256], P(None, 'gy', 'gz'), may hold values from -3 to 3
- phase: float32 [256, 256, 256], P('gy', 'gz'), may hold values from -4 to 4
- labels: int32 [256, 256, 256], P('gy', 'gz'), may hold values from 0 to 3
Outputs:
- adjoint_start: float32 [2, 256, 256, 256], P(None, 'gy', 'gz')
- chi_grad: float32 [256, 256, 256], P('gy', 'gz')
All inputs are finite; a program needn't handle non-finite values.
Results may differ from a plain program's by a relative error of at most 0.0003.
Values sent between devices are 32-bit elements; how exact they have to be, the bound alone decides.
No kernel may reach another device: no remote copies, remote signals or barrier semaphores. Data moves between devices by JAX's collectives and lax.ppermute only.
A program may use at most 192 MiB of HBM per device.

v0:
```python
import functools
import math

import jax
import jax.numpy as jnp
from jax import lax
from jax.experimental import pallas as pl
from jax.experimental.pallas import tpu as pltpu
from jax.sharding import PartitionSpec as P


def signed_freq(index, length):
    return jnp.where(index < length // 2, index, index - length)


def dipole_block(freq_y, freq_z, freq_x):
    square_z = freq_z * freq_z
    total = freq_y * freq_y + square_z + freq_x * freq_x
    ratio = square_z.astype(jnp.float32) / jnp.maximum(total, 1).astype(jnp.float32)
    return jnp.where(total == 0, jnp.float32(0.0), jnp.float32(1.0 / 3.0) - ratio)


def cas_table(length):
    index = jnp.arange(length, dtype=jnp.int32)
    product = index[:, None] * index[None, :] % length
    angle = product.astype(jnp.float32) * (2.0 * math.pi / length)
    return jnp.cos(angle) + jnp.sin(angle)


def along(spec, table, values):
    return jnp.einsum(spec, table, values, precision=lax.Precision.HIGH)


def plane_update(centre, below, above, z_low, z_high):
    length_z, length_x = centre.shape
    row = lax.broadcasted_iota(jnp.int32, centre.shape, 0)
    up = jnp.where(row == 0, z_low, pltpu.roll(centre, 1, 0))
    down = jnp.where(row == length_z - 1, z_high, pltpu.roll(centre, length_z - 1, 0))
    total = below + above + up + down
    total = total + pltpu.roll(centre, 1, 1) + pltpu.roll(centre, length_x - 1, 1)
    return centre + 0.15 * (total - 6.0 * centre)


def neighbour_planes(cur_ref, prev_ref, next_ref, y_low_ref, y_high_ref, rows, field, comp, r, step, last):
    below = cur_ref[comp, jnp.maximum(r - 1, 0)]
    below = jnp.where(r == 0, jnp.where(step == 0, y_low_ref[field], prev_ref[comp, 0]), below)
    above = cur_ref[comp, jnp.minimum(r + 1, rows - 1)]
    above = jnp.where(r == rows - 1, jnp.where(step == last, y_high_ref[field], next_ref[comp, 0]), above)
    return below, above


def write_edges(step, last, rows, r, values, y_first_ref, y_last_ref, z_first_ref, z_last_ref):
    for c, value in enumerate(values):
        z_first_ref[c, r] = value[0:1]
        z_last_ref[c, r] = value[value.shape[0] - 1:]

    @pl.when(jnp.logical_and(r == 0, step == 0))
    def _():
        for c, value in enumerate(values):
            y_first_ref[c] = value

    @pl.when(jnp.logical_and(r == rows - 1, step == last))
    def _():
        for c, value in enumerate(values):
            y_last_ref[c] = value


def for_rows(rows, body):
    def loop_body(r, carry):
        body(r)
        return carry
    lax.fori_loop(0, rows, loop_body, 0)


def step_factor(labels, phase):
    rate = jnp.where(labels == 1, 0.3, 0.02)
    rate = jnp.where(labels == 2, 0.6, rate)
    rate = jnp.where(labels == 3, 1.2, rate).astype(jnp.float32)
    decay = jnp.exp(-rate)
    return decay * jnp.cos(phase), decay * jnp.sin(phase)


def first_w(lam_real, lam_imag, labels, phase):
    f_real, f_imag = step_factor(labels, phase)
    return (f_real * lam_real - f_imag * lam_imag, f_real * lam_imag + f_imag * lam_real), (f_real, f_imag)


def factor_kernel(lam_ref, phase_ref, labels_ref, factor_ref, w_ref, *, rows):
    def body(r, carry):
        (w_real, w_imag), (f_real, f_imag) = first_w(lam_ref[0, r], lam_ref[1, r], labels_ref[r], phase_ref[r])
        factor_ref[0, r] = f_real
        factor_ref[1, r] = f_imag
        w_ref[0, r] = w_real
        w_ref[1, r] = w_imag
        return carry
    lax.fori_loop(0, rows, body, 0)


def edges_kernel(*refs, rows):
    (mm_y0, mm_y1, mm_z0, mm_z1, ms_y0, ms_y1, ms_z0, ms_z1, lam_y0, lam_y1, lam_z0, lam_z1,
     ph_y0, ph_y1, ph_z0, ph_z1, lb_y0, lb_y1, lb_z0, lb_z1,
     y_first_ref, y_last_ref, z_first_ref, z_last_ref) = refs

    @pl.when(pl.program_id(0) == 0)
    def _():
        for out_ref, m1, m2, lam, ph, lb in ((y_first_ref, mm_y0, ms_y0, lam_y0, ph_y0, lb_y0),
                                           (y_last_ref, mm_y1, ms_y1, lam_y1, ph_y1, lb_y1)):
            (w_real, w_imag), _ = first_w(lam[0, 0], lam[1, 0], lb[0], ph[0])
            planes = [m1[0, 0], m1[1, 0], m2[0, 0], m2[1, 0], w_real, w_imag]
            for c, value in enumerate(planes):
                out_ref[c] = value

    def body(r, carry):
        for out_ref, m1, m2, lam, ph, lb, at in ((z_first_ref, mm_z0, ms_z0, lam_z0, ph_z0, lb_z0, 0),
                                               (z_last_ref, mm_z1, ms_z1, lam_z1, ph_z1, lb_z1, 7)):
            (w_real, w_imag), _ = first_w(lam[0, r], lam[1, r], lb[r], ph[r])
            tiles = [m1[0, r], m1[1, r], m2[0, r], m2[1, r], w_real, w_imag]
            for c, value in enumerate(tiles):
                out_ref[c, r] = value[at:at + 1]
        return carry
    lax.fori_loop(0, rows, body, 0)


def edge_specs_of(ndim, length_y, length_z, length_x, rows):
    lead = (2,) if ndim == 4 else ()
    zero = (0,) * len(lead)
    tiles = length_z // 8
    return [
        pl.BlockSpec(lead + (1, length_z, length_x), lambda i: zero + (0, 0, 0)),
        pl.BlockSpec(lead + (1, length_z, length_x), lambda i: zero + (length_y - 1, 0, 0)),
        pl.BlockSpec(lead + (rows, 8, length_x), lambda i: zero + (i, 0, 0)),
        pl.BlockSpec(lead + (rows, 8, length_x), lambda i: zero + (i, tiles - 1, 0)),
    ]


def edge_outputs(comps, length_y, length_z, length_x, rows):
    plane = jax.ShapeDtypeStruct((comps, length_z, length_x), jnp.float32)
    row = jax.ShapeDtypeStruct((comps, length_y, 1, length_x), jnp.float32)
    plane_spec = pl.BlockSpec((comps, length_z, length_x), lambda i: (0, 0, 0))
    row_spec = pl.BlockSpec((comps, rows, 1, length_x), lambda i: (0, i, 0, 0))
    return [plane, plane, row, row], [plane_spec, plane_spec, row_spec, row_spec]


def first_kernel(*refs, rows):
    (mm_ref, mm_prev, mm_next, ms_ref, ms_prev, ms_next, w_ref, w_prev, w_next,
     factor_ref, y_low_ref, y_high_ref, z_low_ref, z_high_ref, pg_ref, w2_ref) = refs[:16]
    step = pl.program_id(0)
    last = pl.num_programs(0) - 1
    fields = ((mm_ref, mm_prev, mm_next), (ms_ref, ms_prev, ms_next), (w_ref, w_prev, w_next))

    def body(r):
        new = []
        for f, (cur, prev, nxt) in enumerate(fields):
            pair = []
            for comp in range(2):
                below, above = neighbour_planes(cur, prev, nxt, y_low_ref, y_high_ref, rows, 2 * f + comp, comp, r,
                                                step, last)
                pair.append(plane_update(cur[comp, r], below, above,
                                         z_low_ref[2 * f + comp, r], z_high_ref[2 * f + comp, r]))
            new.append(pair)
        (u1_real, u1_imag), (u2_real, u2_imag), (lam_real, lam_imag) = new
        w_real = w_ref[0, r]
        w_imag = w_ref[1, r]
        f_real = factor_ref[0, r]
        f_imag = factor_ref[1, r]
        w2_real = f_real * lam_real - f_imag * lam_imag
        w2_imag = f_real * lam_imag + f_imag * lam_real
        grad = w_real * u1_imag - w_imag * u1_real
        pg_ref[r] = grad + (w2_real * u2_imag - w2_imag * u2_real)
        w2_ref[0, r] = w2_real
        w2_ref[1, r] = w2_imag
        write_edges(step, last, rows, r, [w2_real, w2_imag], *refs[16:])

    for_rows(rows, body)


def second_kernel(w_ref, w_prev, w_next, y_low_ref, y_high_ref, z_low_ref, z_high_ref, out_ref, *, rows):
    step = pl.program_id(0)
    last = pl.num_programs(0) - 1

    def body(r):
        for comp in range(2):
            below, above = neighbour_planes(w_ref, w_prev, w_next, y_low_ref, y_high_ref, rows, comp, comp, r,
                                            step, last)
            out_ref[comp, r] = plane_update(w_ref[comp, r], below, above,
                                            z_low_ref[comp, r], z_high_ref[comp, r])

    for_rows(rows, body)


def block_rows(length_y):
    rows = 8
    while length_y % rows:
        rows //= 2
    return rows


def field_specs(shape, rows):
    comps, length_y, length_z, length_x = shape
    cur = pl.BlockSpec((comps, rows, length_z, length_x), lambda i: (0, i, 0, 0))
    prev = pl.BlockSpec((comps, 1, length_z, length_x),
                        lambda i: (0, jnp.maximum(i * rows - 1, 0), 0, 0))
    nxt = pl.BlockSpec((comps, 1, length_z, length_x),
                       lambda i: (0, jnp.minimum(i * rows + rows, length_y - 1), 0, 0))
    return [cur, prev, nxt]


def send_edges(y_first, y_last, z_first, z_last):
    results = []
    for axis, first, last in (("gy", y_first, y_last), ("gz", z_first, z_last)):
        count = lax.axis_size(axis)
        up = [(i, (i + 1) % count) for i in range(count)]
        down = [(j, i) for i, j in up]
        if count == 2:
            both = lax.ppermute(jnp.stack([last, first]), axis, up)
            results.extend([both[0], both[1]])
        else:
            results.extend([lax.ppermute(last, axis, up), lax.ppermute(first, axis, down)])
    return results


def backward_sections(mag_start, mag_middle, adjoint_end, phase, labels):
    _, length_y, length_z, length_x = mag_start.shape
    rows = block_rows(length_y)
    grid = (length_y // rows,)
    plane = jax.ShapeDtypeStruct((length_y, length_z, length_x), jnp.float32)
    pair = jax.ShapeDtypeStruct((2, length_y, length_z, length_x), jnp.float32)
    cur = pl.BlockSpec((2, rows, length_z, length_x), lambda i: (0, i, 0, 0))
    cur_plane = pl.BlockSpec((rows, length_z, length_x), lambda i: (i, 0, 0))
    whole = lambda shape: pl.BlockSpec(shape, lambda i: (0,) * len(shape))
    zspec = lambda comps: pl.BlockSpec((comps, rows, 1, length_x), lambda i: (0, i, 0, 0))
    edge_shapes, edge_specs = edge_outputs(2, length_y, length_z, length_x, rows)
    six_shapes, six_specs = edge_outputs(6, length_y, length_z, length_x, rows)
    inputs = (mag_middle, mag_start, adjoint_end, phase, labels)
    edges = pl.pallas_call(
        functools.partial(edges_kernel, rows=rows),
        grid=grid,
        in_specs=[s for a in inputs for s in edge_specs_of(a.ndim, length_y, length_z, length_x, rows)],
        out_specs=six_specs,
        out_shape=six_shapes,
    )(*[a for a in inputs for _ in range(4)])
    halos = send_edges(*edges)
    factor, w_first = pl.pallas_call(
        functools.partial(factor_kernel, rows=rows),
        grid=grid,
        in_specs=[cur, cur_plane, cur_plane],
        out_specs=[cur, cur],
        out_shape=[pair, pair],
    )(adjoint_end, phase, labels)
    phase_grad, w_second, *w2_edges = pl.pallas_call(
        functools.partial(first_kernel, rows=rows),
        grid=grid,
        in_specs=field_specs(mag_middle.shape, rows) + field_specs(mag_start.shape, rows)
        + field_specs(w_first.shape, rows)
        + [cur, whole((6, length_z, length_x)), whole((6, length_z, length_x)), zspec(6), zspec(6)],
        out_specs=[cur_plane, cur] + edge_specs,
        out_shape=[plane, pair] + edge_shapes,
    )(mag_middle, mag_middle, mag_middle, mag_start, mag_start, mag_start,
      w_first, w_first, w_first, factor, *halos)
    halos = send_edges(*w2_edges)
    lam = pl.pallas_call(
        functools.partial(second_kernel, rows=rows),
        grid=grid,
        in_specs=field_specs(w_second.shape, rows)
        + [whole((2, length_z, length_x)), whole((2, length_z, length_x)), zspec(2), zspec(2)],
        out_specs=cur,
        out_shape=pair,
    )(w_second, w_second, w_second, *halos)
    return (lam, phase_grad)


def dipole_adjoint(phase_grad):
    count_y = lax.axis_size("gy")
    count_z = lax.axis_size("gz")
    parts = count_y * count_z
    block_y, block_z, length_x = phase_grad.shape
    length_y = block_y * count_y
    length_z = block_z * count_z
    block_x = length_x // parts
    pieces = 2 if block_x % 2 == 0 else 1
    piece_x = block_x // pieces
    table_x = cas_table(length_x).reshape(parts, pieces, piece_x, length_x)
    table_y = cas_table(length_y)
    table_z = cas_table(length_z)
    scale = 1.0 / (float(length_y) * float(length_z) * float(length_x))
    freq_y = signed_freq(jnp.arange(length_y, dtype=jnp.int32), length_y)
    freq_z = signed_freq(jnp.arange(length_z, dtype=jnp.int32), length_z)
    index = lax.axis_index("gy") * count_z + lax.axis_index("gz")
    sent = []
    for p in range(pieces):
        spec = along("sxn,yzn->sxyz", table_x[:, p], phase_grad)
        sent.append(lax.all_to_all(spec, ("gy", "gz"), 0, 0, tiled=True))
    result = None
    for p in range(pieces):
        spec = sent[p].reshape(count_y, count_z, piece_x, block_y, block_z)
        spec = spec.transpose(2, 0, 3, 1, 4).reshape(piece_x, length_y, length_z)
        spec = along("kz,xyz->xyk", table_z, spec)
        spec = along("ky,xyz->xkz", table_y, spec)
        first_x = index * block_x + p * piece_x
        freq_x = signed_freq(first_x + jnp.arange(piece_x, dtype=jnp.int32), length_x)
        kernel = dipole_block(freq_y[None, :, None], freq_z[None, None, :], freq_x[:, None, None])
        spec = spec * kernel
        spec = along("ky,xyz->xkz", table_y, spec)
        spec = along("kz,xyz->xyk", table_z, spec)
        spec = spec.reshape(piece_x, count_y, block_y, count_z, block_z)
        spec = spec.transpose(1, 3, 0, 2, 4).reshape(parts, piece_x, block_y, block_z)
        spec = lax.all_to_all(spec, ("gy", "gz"), 0, 0, tiled=True)
        part = along("sxn,sxyz->yzn", table_x[:, p], spec)
        result = part if result is None else result + part
    return result * scale


def per_device(mag_start, mag_middle, adjoint_end, phase, labels):
    lam, phase_grad = backward_sections(mag_start, mag_middle, adjoint_end, phase, labels)
    chi_grad = dipole_adjoint(phase_grad)
    return (lam, chi_grad)


def solution(mesh):
    return jax.shard_map(
        per_device,
        mesh=mesh,
        in_specs=(
            P(None, "gy", "gz", None),
            P(None, "gy", "gz", None),
            P(None, "gy", "gz", None),
            P("gy", "gz", None),
            P("gy", "gz", None),
        ),
        out_specs=(P(None, "gy", "gz", None), P("gy", "gz", None)),
        check_vma=False,
    )
```

profile of v0, /device:TPU:16, one launch (start us, length us, event | category | flops | bytes accessed | tf_op | source)
XLA Modules:
  0.0 186.3 jit_solution(12672258959493704738)
XLA Ops:
  0.6 5.9 %shard_map.69 = (f32[6,128,256]{2,1,0:T(8,128)}, f32[6,128,256]{2,1,0:T(8,128)}, f32[6,16,1,256]{3,2,1,0:T(1,128)}, f32[6,16,1,256]{3,2,1,0:T(1,128)}) custom-call(f32[2,16,128,256]{3,2,1,0:T(8,128)} %refs_2_.3, f32[2,16,128,256]{3,2,1,0:T(8,128)} %refs_2_.3, f32[2,16,128,256]{3,2,1,0:T(8,128)} %refs_2_.3, f32[2,16,128,256]{3,2,1,0:T(8,128)} %refs_2_.3, ...), custom_call_target="tpu_custom_call" | custom-call | tf_op jit(solution)/shard_map/pallas_call | solution.py:235
  6.6 2.6 %collective-permute-start.1 = (f32[6,128,256]{2,1,0:T(8,128)}, f32[6,128,256]{2,1,0:T(8,128)S(1)}, u32[]{:S(2)}, u32[]{:S(2)}) collective-permute-start(f32[6,128,256]{2,1,0:T(8,128)} %get-tuple-element.17), channel_id=1, source_target_pairs={{2,0},{4,2},{6,4},{8,6},{10,8},{12,10},{14,12},{16,14},{18,16},{20... | collective-permute-start | bytes 2359304 | tf_op jit(solution)/shard_map/ppermute | solution.py:218
  9.3 1.1 pad_maximum_fusion
  10.4 1.6 collective-permute-start.2
  12.0 13.2 %shard_map.68 = (f32[2,16,128,256]{3,2,1,0:T(8,128)}, f32[2,16,128,256]{3,2,1,0:T(8,128)}) custom-call(f32[2,16,128,256]{3,2,1,0:T(8,128)} %refs_11_.1, f32[16,128,256]{2,1,0:T(8,128)} %refs_15_.1, s32[16,128,256]{2,1,0:T(8,128)} %refs_19_.1), custom_call_target="tpu_custom_call" | custom-call | tf_op jit(solution)/shard_map/pallas_call | solution.py:243
  25.2 1.1 sine_add_fusion.1
  26.3 0.8 slice_bitcast_fusion
  27.1 1.0 copy-done.1
  28.1 0.2 copy-done.2
  28.3 17.1 %shard_map.70 = (f32[16,128,256]{2,1,0:T(8,128)}, f32[2,16,128,256]{3,2,1,0:T(8,128)}, f32[2,128,256]{2,1,0:T(8,128)}, f32[2,128,256]{2,1,0:T(8,128)}, f32[2,16,...) custom-call(f32[2,16,128,256]{3,2,1,0:T(8,128)} %refs_2_.3, f32[2,16,128,256]{3,2,1,0:T(8,128)} %refs_2_.3, ...), custom_call_target="tpu_custom_call" | custom-call | tf_op jit(solution)/shard_map/pallas_call | solution.py:250
  45.4 2.8 %fusion.3 = f32[32,4,16,128]{3,0,2,1:T(8,128)S(1)} fusion(f32[16,128,256]{2,1,0:T(8,128)} %get-tuple-element.25, f32[32,2,4,256]{3,0,2,1:T(8,128)S(1)} %sine_add_fusion.1), kind=kOutput, calls=%fused_computation.4 | convolution fusion | flops 402653184 | bytes 3276800 | tf_op jit(solution)/shard_map/sxn,yzn->sxyz/dot_general | solution.py:31
  48.2 1.6 copy.13
  49.8 5.5 %all-to-all-start = ((f32[32,4,16,128]{3,2,1,0:T(8,128)}), f32[32,4,16,128]{3,2,1,0:T(8,128)S(1)}, u32[]{:S(2)}, u32[]{:S(2)}) async-start(f32[32,4,16,128]{3,2,1,0:T(8,128)} %copy.13), calls=%async_computation | async-start | bytes 2097152 | tf_op jit(solution)/shard_map/all_to_all | solution.py:292
  55.3 1.2 fusion.1
  56.5 1.6 copy.19
  58.1 22.5 %all-to-all-done = f32[32,4,16,128]{3,2,1,0:T(8,128)S(1)} async-done(((f32[32,4,16,128]{3,2,1,0:T(8,128)}), f32[32,4,16,128]{3,2,1,0:T(8,128)S(1)}, u32[]{:S(2)}, u32[]{:S(2)}) %all-to-all-start) | async-done | bytes 1048608 | tf_op jit(solution)/shard_map/all_to_all | solution.py:292
  80.6 4.6 %all-to-all-start.2 = ((f32[32,4,16,128]{3,2,1,0:T(8,128)}), f32[32,4,16,128]{3,2,1,0:T(8,128)S(1)}, u32[]{:S(2)}, u32[]{:S(2)}) async-start(f32[32,4,16,128]{3,2,1,0:T(8,128)} %copy.19), calls=%async_computation.2 | async-start | bytes 2097152 | tf_op jit(solution)/shard_map/all_to_all | solution.py:292
  85.2 0.8 broadcast_add_fusion
  86.0 0.8 copy.40
  86.8 0.8 reshape.120
  87.7 1.6 fusion.34
  89.3 1.8 fusion.5
  91.1 1.6 convolution_bitcast_fusion.2
  92.8 1.9 %fusion.30 = f32[4,256,256]{2,1,0:T(8,128)S(1)} fusion(f32[4,256,256]{1,2,0:T(8,128)S(1)} %convolution_bitcast_fusion.2), kind=kOutput, calls=%fused_computation.47 | convolution fusion | flops 403636224 | bytes 2097152 | tf_op jit(solution)/shard_map/kz,xyz->xyk/dot_general | solution.py:31
  94.7 0.5 reshape.121
  95.2 1.7 copy.17
  96.9 13.5 %all-to-all-done.2 = f32[32,4,16,128]{3,2,1,0:T(8,128)S(1)} async-done(((f32[32,4,16,128]{3,2,1,0:T(8,128)}), f32[32,4,16,128]{3,2,1,0:T(8,128)S(1)}, u32[]{:S(2)}, u32[]{:S(2)}) %all-to-all-start.2) | async-done | bytes 1048608 | tf_op jit(solution)/shard_map/all_to_all | solution.py:292
  110.4 4.6 %all-to-all-start.1 = ((f32[32,4,16,128]{3,1,2,0:T(4,128)}), f32[32,4,16,128]{3,1,2,0:T(4,128)S(1)}, u32[]{:S(2)}, u32[]{:S(2)}) async-start(f32[32,4,16,128]{3,1,2,0:T(4,128)} %bitcast.18), calls=%async_computation.1 | async-start | bytes 2097152 | tf_op jit(solution)/shard_map/all_to_all | solution.py:307
  115.0 0.8 copy.39
  115.9 0.8 reshape.124
  116.7 1.6 fusion.28
  118.4 1.8 fusion.6
  120.2 1.6 convolution_bitcast_fusion
  121.8 1.9 %fusion.24 = f32[4,256,256]{2,1,0:T(8,128)S(1)} fusion(f32[4,256,256]{1,2,0:T(8,128)S(1)} %convolution_bitcast_fusion), kind=kOutput, calls=%fused_computation.41 | convolution fusion | flops 403636224 | bytes 2097152 | tf_op jit(solution)/shard_map/kz,xyz->xyk/dot_general | solution.py:31
  123.7 0.5 reshape.125
  124.3 1.7 copy.23
  126.0 14.3 %all-to-all-done.1 = f32[32,4,16,128]{3,1,2,0:T(4,128)S(1)} async-done(((f32[32,4,16,128]{3,1,2,0:T(4,128)}), f32[32,4,16,128]{3,1,2,0:T(4,128)S(1)}, u32[]{:S(2)}, u32[]{:S(2)}) %all-to-all-start.1) | async-done | bytes 1048608 | tf_op jit(solution)/shard_map/all_to_all | solution.py:307
  140.3 4.7 %all-to-all-start.3 = ((f32[32,4,16,128]{3,1,2,0:T(4,128)}), f32[32,4,16,128]{3,1,2,0:T(4,128)}, u32[]{:S(2)}, u32[]{:S(2)}) async-start(f32[32,4,16,128]{3,1,2,0:T(4,128)} %bitcast.29), calls=%async_computation.3 | async-start | bytes 2097152 | tf_op jit(solution)/shard_map/all_to_all | solution.py:307
  145.0 1.5 collective-permute-start.5
  146.6 2.6 %collective-permute-start.4 = (f32[2,128,256]{2,1,0:T(8,128)S(1)}, f32[2,128,256]{2,1,0:T(8,128)S(1)}, u32[]{:S(2)}, u32[]{:S(2)}) collective-permute-start(f32[2,128,256]{2,1,0:T(8,128)S(1)} %copy-done.9), channel_id=1, source_target_pairs={{2,0},{4,2},{6,4},{8,6},{10,8},{12,10},{14,12},{16,14},{18,16},{20... | collective-permute-start | bytes 786440 | tf_op jit(solution)/shard_map/ppermute | solution.py:218
  149.2 5.7 %collective-permute-done.5 = f32[2,2,16,1,256]{4,3,2,1,0:T(1,128)S(1)} collective-permute-done((f32[2,2,16,1,256]{4,3,2,1,0:T(1,128)S(1)}, f32[2,2,16,1,256]{4,3,2,1,0:T(1,128)S(1)}, u32[]{:S(2)}, u32[]{:S(2)}) %collective-permute-start.5) | collective-permute-done | bytes 65568 | tf_op jit(solution)/shard_map/ppermute | solution.py:215
  154.9 0.6 slice_bitcast_fusion.2
  155.5 17.4 %collective-permute-done.3.y_low_ref = f32[2,128,256]{2,1,0:T(8,128)S(1)} collective-permute-done((f32[2,128,256]{2,1,0:T(8,128)}, f32[2,128,256]{2,1,0:T(8,128)S(1)}, u32[]{:S(2)}, u32[]{:S(2)}) %collective-permute-start.3) | collective-permute-done | bytes 262176 | tf_op jit(solution)/shard_map/ppermute | solution.py:218
  173.0 0.7 copy-done.3
  173.7 0.1 copy-done.4
  173.7 7.1 %shard_map.71 = f32[2,16,128,256]{3,2,1,0:T(8,128)} custom-call(f32[2,16,128,256]{3,2,1,0:T(8,128)} %get-tuple-element.20.w_ref.w_prev.w_next, f32[2,16,128,256]{3,2,1,0:T(8,128)} %get-tuple-element.20.w_ref.w_prev.w_next, f32[2,16,128,256]{3,2,1,0:T(8,128)} %get-tuple-element.20.w_ref.w_prev.w_next, f32[2,128,256]{2,1,0:T(8,128)} %copy-done.3, ...), custom_call_target="tpu_custom_call" | custom-call | tf_op jit(solution)/shard_map/pallas_call | solution.py:261
  180.8 1.5 fusion.16
  182.3 4.0 %fusion = f32[16,128,256]{2,1,0:T(8,128)} fusion(f32[16,128,256,1]{2,1,3,0:T(8,128)S(1)} %fusion.16, f32[32,4,16,128]{3,1,2,0:T(4,128)} %all-to-all-done.3, f32[32,2,4,256]{3,0,2,1:T(8,128)S(1)} %sine_add_fusion.1), kind=kOutput, calls=%fused_computation.1 | convolution fusion | flops 403701760 | bytes 5373952 | tf_op jit(solution)/shard_map/sxn,sxyz->yzn/dot_general | solution.py:31
  (29 shorter events, 0.2 us)
Async XLA Ops:
  6.6 20.6 %collective-permute-start = (f32[6,128,256]{2,1,0:T(8,128)}, f32[6,128,256]{2,1,0:T(8,128)S(1)}, u32[]{:S(2)}, u32[]{:S(2)}) collective-permute-start(f32[6,128,256]{2,1,0:T(8,128)} %get-tuple-element.16), channel_id=1, source_target_pairs={{0,2},{2,4},{4,6},{6,8},{8,10},{10,12},{12,14},{14,16},{16,18},{18... | collective-permute-start | bytes 2359304 | tf_op jit(solution)/shard_map/ppermute | solution.py:218
  6.6 20.5 %collective-permute-start.1 = (f32[6,128,256]{2,1,0:T(8,128)}, f32[6,128,256]{2,1,0:T(8,128)S(1)}, u32[]{:S(2)}, u32[]{:S(2)}) collective-permute-start(f32[6,128,256]{2,1,0:T(8,128)} %get-tuple-element.17), channel_id=1, source_target_pairs={{2,0},{4,2},{6,4},{8,6},{10,8},{12,10},{14,12},{16,14},{18,16},{20... | collective-permute-start | bytes 2359304 | tf_op jit(solution)/shard_map/ppermute | solution.py:218
  10.4 15.9 %collective-permute-start.2 = (f32[2,6,16,1,256]{4,3,2,1,0:T(1,128)S(1)}, f32[2,6,16,1,256]{4,3,2,1,0:T(1,128)S(1)}, u32[]{:S(2)}, u32[]{:S(2)}) collective-permute-start(f32[2,6,16,1,256]{4,3,2,1,0:T(1,128)S(1)} %pad_maximum_fusion), channel_id=1, source_target_pairs={{0,1},{1,0},{2,3},{3,2},{4,5},{5,4},{6,7},{7,6},{8,9},{9,8},{10,11... | collective-permute-start | bytes 589832 | tf_op jit(solution)/shard_map/ppermute | solution.py:215
  27.1 1.0 copy-start.1
  27.1 1.2 copy-start.2
  48.2 7.1 %copy-start = (f32[16,128,256]{2,1,0:T(8,128)S(1)}, f32[16,128,256]{2,1,0:T(8,128)}, u32[]{:S(2)}) copy-start(f32[16,128,256]{2,1,0:T(8,128)} %get-tuple-element.25) | copy-start | bytes 6291460
  49.8 30.7 %all-to-all-start = ((f32[32,4,16,128]{3,2,1,0:T(8,128)}), f32[32,4,16,128]{3,2,1,0:T(8,128)S(1)}, u32[]{:S(2)}, u32[]{:S(2)}) async-start(f32[32,4,16,128]{3,2,1,0:T(8,128)} %copy.13), calls=%async_computation | async-start | bytes 2097152 | tf_op jit(solution)/shard_map/all_to_all | solution.py:292
  80.6 29.9 %all-to-all-start.2 = ((f32[32,4,16,128]{3,2,1,0:T(8,128)}), f32[32,4,16,128]{3,2,1,0:T(8,128)S(1)}, u32[]{:S(2)}, u32[]{:S(2)}) async-start(f32[32,4,16,128]{3,2,1,0:T(8,128)} %copy.19), calls=%async_computation.2 | async-start | bytes 2097152 | tf_op jit(solution)/shard_map/all_to_all | solution.py:292
  87.7 1.7 copy-start.5
  110.4 29.9 %all-to-all-start.1 = ((f32[32,4,16,128]{3,1,2,0:T(4,128)}), f32[32,4,16,128]{3,1,2,0:T(4,128)S(1)}, u32[]{:S(2)}, u32[]{:S(2)}) async-start(f32[32,4,16,128]{3,1,2,0:T(4,128)} %bitcast.18), calls=%async_computation.1 | async-start | bytes 2097152 | tf_op jit(solution)/shard_map/all_to_all | solution.py:307
  116.7 1.7 copy-start.6
  124.3 20.7 %copy-start.7 = (f32[2,16,1,256]{3,2,1,0:T(1,128)S(1)}, f32[2,16,1,256]{3,2,1,0:T(1,128)}, u32[]{:S(2)}) copy-start(f32[2,16,1,256]{3,2,1,0:T(1,128)} %get-tuple-element.24) | copy-start | bytes 98308
  124.3 20.7 %copy-start.8 = (f32[2,16,1,256]{3,2,1,0:T(1,128)S(1)}, f32[2,16,1,256]{3,2,1,0:T(1,128)}, u32[]{:S(2)}) copy-start(f32[2,16,1,256]{3,2,1,0:T(1,128)} %get-tuple-element.23) | copy-start | bytes 98308
  124.3 22.3 %copy-start.9 = (f32[2,128,256]{2,1,0:T(8,128)S(1)}, f32[2,128,256]{2,1,0:T(8,128)}, u32[]{:S(2)}) copy-start(f32[2,128,256]{2,1,0:T(8,128)} %get-tuple-element.22) | copy-start | bytes 786436
  140.3 42.0 %all-to-all-start.3 = ((f32[32,4,16,128]{3,1,2,0:T(4,128)}), f32[32,4,16,128]{3,1,2,0:T(4,128)}, u32[]{:S(2)}, u32[]{:S(2)}) async-start(f32[32,4,16,128]{3,1,2,0:T(4,128)} %bitcast.29), calls=%async_computation.3 | async-start | bytes 2097152 | tf_op jit(solution)/shard_map/all_to_all | solution.py:307
  145.0 9.9 %collective-permute-start.5 = (f32[2,2,16,1,256]{4,3,2,1,0:T(1,128)S(1)}, f32[2,2,16,1,256]{4,3,2,1,0:T(1,128)S(1)}, u32[]{:S(2)}, u32[]{:S(2)}) collective-permute-start(f32[2,2,16,1,256]{4,3,2,1,0:T(1,128)S(1)} %pad_maximum_fusion.1), channel_id=1, source_target_pairs={{0,1},{1,0},{2,3},{3,2},{4,5},{5,4},{6,7},{7,6},{8,9},{9,8},{10,11... | collective-permute-start | bytes 196616 | tf_op jit(solution)/shard_map/ppermute | solution.py:215
  146.6 26.4 %collective-permute-start.3 = (f32[2,128,256]{2,1,0:T(8,128)}, f32[2,128,256]{2,1,0:T(8,128)S(1)}, u32[]{:S(2)}, u32[]{:S(2)}) collective-permute-start(f32[2,128,256]{2,1,0:T(8,128)} %get-tuple-element.21), channel_id=1, source_target_pairs={{0,2},{2,4},{4,6},{6,8},{8,10},{10,12},{12,14},{14,16},{16,18},{18... | collective-permute-start | bytes 786440 | tf_op jit(solution)/shard_map/ppermute | solution.py:218
  146.6 26.4 %collective-permute-start.4 = (f32[2,128,256]{2,1,0:T(8,128)S(1)}, f32[2,128,256]{2,1,0:T(8,128)S(1)}, u32[]{:S(2)}, u32[]{:S(2)}) collective-permute-start(f32[2,128,256]{2,1,0:T(8,128)S(1)} %copy-done.9), channel_id=1, source_target_pairs={{2,0},{4,2},{6,4},{8,6},{10,8},{12,10},{14,12},{16,14},{18,16},{20... | collective-permute-start | bytes 786440 | tf_op jit(solution)/shard_map/ppermute | solution.py:218
  173.0 0.7 copy-start.3
  173.0 0.8 copy-start.4
where the time goes:
time: 187 us; the launch traced here: 186 us
  waiting for transfers between devices  73.5 us (39%)
  Pallas kernels  43.3 us (23%)
  starting transfers between devices  27.8 us (15%)
  matrix products  23.2 us (12%)
  local copies, waits for them, and re-layouts  14.4 us (8%)
  other arithmetic  3.15 us (2%)
    all_to_all x2, waiting for transfers between devices, dipole_adjoint(): sent.append(lax.all_to_all(spec, ('gy', 'gz'), 0, 0, tiled=True))  36 us
    dot_general x12, matrix products, along(): return jnp.einsum(spec, table, values, precision=lax.Precision.HIGH)  23.2 us
    ppermute x2, waiting for transfers between devices, send_edges(): lax.ppermute(last, axis, up)  17.4 us
    pallas_call x1, Pallas kernels, backward_sections(): pl.pallas_call(functools.partial(first_kernel, rows=rows), grid=grid, in_...  17.1 us
    all_to_all x2, waiting for transfers between devices, dipole_adjoint(): spec = lax.all_to_all(spec, ('gy', 'gz'), 0, 0, tiled=True)  14.3 us
    pallas_call x1, Pallas kernels, backward_sections(): pl.pallas_call(functools.partial(factor_kernel, rows=rows), grid=grid, in...  13.2 us
    all_to_all x2, starting transfers between devices, dipole_adjoint(): sent.append(lax.all_to_all(spec, ('gy', 'gz'), 0, 0, tiled=True))  10.1 us
    all_to_all x2, starting transfers between devices, dipole_adjoint(): spec = lax.all_to_all(spec, ('gy', 'gz'), 0, 0, tiled=True)  9.25 us
  transfers between devices with their start and end apart: 10, of which 5 were waited for; matrix products, arithmetic and copies ran while one was open for 16% of the time, Pallas kernels for 11%

commit v1 on v0

--- a/solution.py
+++ b/solution.py
@@ -2,6 +2,7 @@
 import math
 
 import jax
+import numpy as np
 import jax.numpy as jnp
 from jax import lax
 from jax.experimental import pallas as pl
@@ -72,12 +73,29 @@
     lax.fori_loop(0, rows, loop_body, 0)
 
 
+def sin_cos(x):
+    k = jnp.floor(x * (2.0 / math.pi) + 0.5)
+    r = (x - k * 1.5707963705062866) - k * (-4.371139000186243e-08)
+    r2 = r * r
+    s = r + r * r2 * (-1.0 / 6.0 + r2 * (1.0 / 120.0 + r2 * (-1.0 / 5040.0 + r2 * (1.0 / 362880.0))))
+    c = 1.0 + r2 * (-0.5 + r2 * (1.0 / 24.0 + r2 * (-1.0 / 720.0 + r2 * (1.0 / 40320.0
+                                                                        + r2 * (-1.0 / 3628800.0)))))
+    quadrant = k.astype(jnp.int32) & 3
+    swap = (quadrant & 1) == 1
+    sin_x = jnp.where(swap, c, s)
+    cos_x = jnp.where(swap, s, c)
+    sin_x = jnp.where(quadrant >= 2, -sin_x, sin_x)
+    cos_x = jnp.where((quadrant == 1) | (quadrant == 2), -cos_x, cos_x)
+    return sin_x, cos_x
+
+
 def step_factor(labels, phase):
-    rate = jnp.where(labels == 1, 0.3, 0.02)
-    rate = jnp.where(labels == 2, 0.6, rate)
-    rate = jnp.where(labels == 3, 1.2, rate).astype(jnp.float32)
-    decay = jnp.exp(-rate)
-    return decay * jnp.cos(phase), decay * jnp.sin(phase)
+    decays = [float(np.exp(-np.float32(rate))) for rate in (0.02, 0.3, 0.6, 1.2)]
+    decay = jnp.where(labels == 1, decays[1], decays[0])
+    decay = jnp.where(labels == 2, decays[2], decay)
+    decay = jnp.where(labels == 3, decays[3], decay).astype(jnp.float32)
+    sin_p, cos_p = sin_cos(phase)
+    return decay * cos_p, decay * sin_p
 
 
 def first_w(lam_real, lam_imag, labels, phase):

time: 187 us -> 186 us (level)
  Pallas kernels: 43.3 us -> 37.3 us
  starting transfers between devices: 27.8 us -> 32.4 us
    all_to_all x2, starting transfers between devices: 10.1 us -> 14.7 us  [dipole_adjoint(): sent.append(lax.all_to_all(spec, ('gy', 'gz'), 0, 0, tiled=True))]
    pallas_call x1, Pallas kernels: 13.2 us -> 8.56 us  [backward_sections(): pl.pallas_call(functools.partial(factor_kernel, rows=rows), grid=grid, in...]
  transfers between devices with their start and end apart: 10 -> 10, of which waited for: 5 -> 5; matrix products, arithmetic and copies ran while one was open for 16% -> 16% of each run, Pallas kernels for 11% -> 8%
where the time goes in v1:
time: 186 us; the launch traced here: 185 us
  waiting for transfers between devices  73.5 us (40%)
  Pallas kernels  37.3 us (20%)
  starting transfers between devices  32.4 us (17%)
  matrix products  23.2 us (12%)
  local copies, waits for them, and re-layouts  14.4 us (8%)
  other arithmetic  3.15 us (2%)
    all_to_all x2, waiting for transfers between devices, dipole_adjoint(): sent.append(lax.all_to_all(spec, ('gy', 'gz'), 0, 0, tiled=True))  36 us
    dot_general x12, matrix products, along(): return jnp.einsum(spec, table, values, precision=lax.Precision.HIGH)  23.2 us
    ppermute x2, waiting for transfers between devices, send_edges(): lax.ppermute(last, axis, up)  17.4 us
    pallas_call x1, Pallas kernels, backward_sections(): pl.pallas_call(functools.partial(first_kernel, rows=rows), grid=grid, in_...  17.1 us
    all_to_all x2, starting transfers between devices, dipole_adjoint(): sent.append(lax.all_to_all(spec, ('gy', 'gz'), 0, 0, tiled=True))  14.7 us
    all_to_all x2, waiting for transfers between devices, dipole_adjoint(): spec = lax.all_to_all(spec, ('gy', 'gz'), 0, 0, tiled=True)  14.3 us
    all_to_all x2, starting transfers between devices, dipole_adjoint(): spec = lax.all_to_all(spec, ('gy', 'gz'), 0, 0, tiled=True)  9.25 us
    pallas_call x1, Pallas kernels, backward_sections(): pl.pallas_call(functools.partial(factor_kernel, rows=rows), grid=grid, in...  8.56 us
  transfers between devices with their start and end apart: 10, of which 5 were waited for; matrix products, arithmetic and copies ran while one was open for 16% of the time, Pallas kernels for 8%

profile of v1, /device:TPU:16, one launch (start us, length us, event | category | flops | bytes accessed | tf_op | source)
XLA Modules:
  0.0 184.9 jit_solution(12785280663741681724)
XLA Ops:
  0.6 4.5 %shard_map.69 = (f32[6,128,256]{2,1,0:T(8,128)}, f32[6,128,256]{2,1,0:T(8,128)}, f32[6,16,1,256]{3,2,1,0:T(1,128)}, f32[6,16,1,256]{3,2,1,0:T(1,128)}) custom-call(f32[2,16,128,256]{3,2,1,0:T(8,128)} %refs_2_.3, f32[2,16,128,256]{3,2,1,0:T(8,128)} %refs_2_.3, f32[2,16,128,256]{3,2,1,0:T(8,128)} %refs_2_.3, f32[2,16,128,256]{3,2,1,0:T(8,128)} %refs_2_.3, ...), custom_call_target="tpu_custom_call" | custom-call | tf_op jit(solution)/shard_map/pallas_call | solution.py:253
  5.2 2.6 %collective-permute-start.1 = (f32[6,128,256]{2,1,0:T(8,128)}, f32[6,128,256]{2,1,0:T(8,128)S(1)}, u32[]{:S(2)}, u32[]{:S(2)}) collective-permute-start(f32[6,128,256]{2,1,0:T(8,128)} %get-tuple-element.17), channel_id=1, source_target_pairs={{2,0},{4,2},{6,4},{8,6},{10,8},{12,10},{14,12},{16,14},{18,16},{20... | collective-permute-start | bytes 2359304 | tf_op jit(solution)/shard_map/ppermute | solution.py:236
  7.9 1.1 pad_maximum_fusion
  9.0 1.6 collective-permute-start.2
  10.6 8.6 %shard_map.68 = (f32[2,16,128,256]{3,2,1,0:T(8,128)}, f32[2,16,128,256]{3,2,1,0:T(8,128)}) custom-call(f32[2,16,128,256]{3,2,1,0:T(8,128)} %refs_11_.1, f32[16,128,256]{2,1,0:T(8,128)} %refs_15_.1, s32[16,128,256]{2,1,0:T(8,128)} %refs_19_.1), custom_call_target="tpu_custom_call" | custom-call | tf_op jit(solution)/shard_map/pallas_call | solution.py:261
  19.1 1.1 sine_add_fusion.1
  20.3 0.8 slice_bitcast_fusion
  21.1 1.0 copy-done.1
  22.1 0.2 copy-done.2
  22.3 17.1 %shard_map.70 = (f32[16,128,256]{2,1,0:T(8,128)}, f32[2,16,128,256]{3,2,1,0:T(8,128)}, f32[2,128,256]{2,1,0:T(8,128)}, f32[2,128,256]{2,1,0:T(8,128)}, f32[2,16,...) custom-call(f32[2,16,128,256]{3,2,1,0:T(8,128)} %refs_2_.3, f32[2,16,128,256]{3,2,1,0:T(8,128)} %refs_2_.3, ...), custom_call_target="tpu_custom_call" | custom-call | tf_op jit(solution)/shard_map/pallas_call | solution.py:268
  39.4 2.8 %fusion.3 = f32[32,4,16,128]{3,0,2,1:T(8,128)S(1)} fusion(f32[16,128,256]{2,1,0:T(8,128)} %get-tuple-element.25, f32[32,2,4,256]{3,0,2,1:T(8,128)S(1)} %sine_add_fusion.1), kind=kOutput, calls=%fused_computation.4 | convolution fusion | flops 402653184 | bytes 3276800 | tf_op jit(solution)/shard_map/sxn,yzn->sxyz/dot_general | solution.py:32
  42.2 1.6 copy.13
  43.8 10.1 %all-to-all-start = ((f32[32,4,16,128]{3,2,1,0:T(8,128)}), f32[32,4,16,128]{3,2,1,0:T(8,128)S(1)}, u32[]{:S(2)}, u32[]{:S(2)}) async-start(f32[32,4,16,128]{3,2,1,0:T(8,128)} %copy.13), calls=%async_computation | async-start | bytes 2097152 | tf_op jit(solution)/shard_map/all_to_all | solution.py:310
  53.9 1.2 fusion.1
  55.1 1.6 copy.19
  56.7 22.5 %all-to-all-done = f32[32,4,16,128]{3,2,1,0:T(8,128)S(1)} async-done(((f32[32,4,16,128]{3,2,1,0:T(8,128)}), f32[32,4,16,128]{3,2,1,0:T(8,128)S(1)}, u32[]{:S(2)}, u32[]{:S(2)}) %all-to-all-start) | async-done | bytes 1048608 | tf_op jit(solution)/shard_map/all_to_all | solution.py:310
  79.2 4.6 %all-to-all-start.2 = ((f32[32,4,16,128]{3,2,1,0:T(8,128)}), f32[32,4,16,128]{3,2,1,0:T(8,128)S(1)}, u32[]{:S(2)}, u32[]{:S(2)}) async-start(f32[32,4,16,128]{3,2,1,0:T(8,128)} %copy.19), calls=%async_computation.2 | async-start | bytes 2097152 | tf_op jit(solution)/shard_map/all_to_all | solution.py:310
  83.8 0.8 broadcast_add_fusion
  84.6 0.8 copy.40
  85.4 0.8 reshape.120
  86.3 1.6 fusion.34
  88.0 1.8 fusion.5
  89.7 1.6 convolution_bitcast_fusion.2
  91.4 1.9 %fusion.30 = f32[4,256,256]{2,1,0:T(8,128)S(1)} fusion(f32[4,256,256]{1,2,0:T(8,128)S(1)} %convolution_bitcast_fusion.2), kind=kOutput, calls=%fused_computation.47 | convolution fusion | flops 403636224 | bytes 2097152 | tf_op jit(solution)/shard_map/kz,xyz->xyk/dot_general | solution.py:32
  93.3 0.5 reshape.121
  93.8 1.7 copy.17
  95.5 13.5 %all-to-all-done.2 = f32[32,4,16,128]{3,2,1,0:T(8,128)S(1)} async-done(((f32[32,4,16,128]{3,2,1,0:T(8,128)}), f32[32,4,16,128]{3,2,1,0:T(8,128)S(1)}, u32[]{:S(2)}, u32[]{:S(2)}) %all-to-all-start.2) | async-done | bytes 1048608 | tf_op jit(solution)/shard_map/all_to_all | solution.py:310
  109.0 4.6 %all-to-all-start.1 = ((f32[32,4,16,128]{3,1,2,0:T(4,128)}), f32[32,4,16,128]{3,1,2,0:T(4,128)S(1)}, u32[]{:S(2)}, u32[]{:S(2)}) async-start(f32[32,4,16,128]{3,1,2,0:T(4,128)} %bitcast.18), calls=%async_computation.1 | async-start | bytes 2097152 | tf_op jit(solution)/shard_map/all_to_all | solution.py:325
  113.7 0.8 copy.39
  114.5 0.8 reshape.124
  115.3 1.6 fusion.28
  117.0 1.8 fusion.6
  118.8 1.6 convolution_bitcast_fusion
  120.4 1.9 %fusion.24 = f32[4,256,256]{2,1,0:T(8,128)S(1)} fusion(f32[4,256,256]{1,2,0:T(8,128)S(1)} %convolution_bitcast_fusion), kind=kOutput, calls=%fused_computation.41 | convolution fusion | flops 403636224 | bytes 2097152 | tf_op jit(solution)/shard_map/kz,xyz->xyk/dot_general | solution.py:32
  122.3 0.5 reshape.125
  122.9 1.7 copy.23
  124.6 14.3 %all-to-all-done.1 = f32[32,4,16,128]{3,1,2,0:T(4,128)S(1)} async-done(((f32[32,4,16,128]{3,1,2,0:T(4,128)}), f32[32,4,16,128]{3,1,2,0:T(4,128)S(1)}, u32[]{:S(2)}, u32[]{:S(2)}) %all-to-all-start.1) | async-done | bytes 1048608 | tf_op jit(solution)/shard_map/all_to_all | solution.py:325
  138.9 4.7 %all-to-all-start.3 = ((f32[32,4,16,128]{3,1,2,0:T(4,128)}), f32[32,4,16,128]{3,1,2,0:T(4,128)}, u32[]{:S(2)}, u32[]{:S(2)}) async-start(f32[32,4,16,128]{3,1,2,0:T(4,128)} %bitcast.29), calls=%async_computation.3 | async-start | bytes 2097152 | tf_op jit(solution)/shard_map/all_to_all | solution.py:325
  143.6 1.5 collective-permute-start.5
  145.2 2.6 %collective-permute-start.4 = (f32[2,128,256]{2,1,0:T(8,128)S(1)}, f32[2,128,256]{2,1,0:T(8,128)S(1)}, u32[]{:S(2)}, u32[]{:S(2)}) collective-permute-start(f32[2,128,256]{2,1,0:T(8,128)S(1)} %copy-done.9), channel_id=1, source_target_pairs={{2,0},{4,2},{6,4},{8,6},{10,8},{12,10},{14,12},{16,14},{18,16},{20... | collective-permute-start | bytes 786440 | tf_op jit(solution)/shard_map/ppermute | solution.py:236
  147.8 5.7 %collective-permute-done.5 = f32[2,2,16,1,256]{4,3,2,1,0:T(1,128)S(1)} collective-permute-done((f32[2,2,16,1,256]{4,3,2,1,0:T(1,128)S(1)}, f32[2,2,16,1,256]{4,3,2,1,0:T(1,128)S(1)}, u32[]{:S(2)}, u32[]{:S(2)}) %collective-permute-start.5) | collective-permute-done | bytes 65568 | tf_op jit(solution)/shard_map/ppermute | solution.py:233
  153.5 0.6 slice_bitcast_fusion.2
  154.1 17.4 %collective-permute-done.3.y_low_ref = f32[2,128,256]{2,1,0:T(8,128)S(1)} collective-permute-done((f32[2,128,256]{2,1,0:T(8,128)}, f32[2,128,256]{2,1,0:T(8,128)S(1)}, u32[]{:S(2)}, u32[]{:S(2)}) %collective-permute-start.3) | collective-permute-done | bytes 262176 | tf_op jit(solution)/shard_map/ppermute | solution.py:236
  171.6 0.7 copy-done.3
  172.3 0.1 copy-done.4
  172.4 7.1 %shard_map.71 = f32[2,16,128,256]{3,2,1,0:T(8,128)} custom-call(f32[2,16,128,256]{3,2,1,0:T(8,128)} %get-tuple-element.20.w_ref.w_prev.w_next, f32[2,16,128,256]{3,2,1,0:T(8,128)} %get-tuple-element.20.w_ref.w_prev.w_next, f32[2,16,128,256]{3,2,1,0:T(8,128)} %get-tuple-element.20.w_ref.w_prev.w_next, f32[2,128,256]{2,1,0:T(8,128)} %copy-done.3, ...), custom_call_target="tpu_custom_call" | custom-call | tf_op jit(solution)/shard_map/pallas_call | solution.py:279
  179.4 1.5 fusion.16
  180.9 4.0 %fusion = f32[16,128,256]{2,1,0:T(8,128)} fusion(f32[16,128,256,1]{2,1,3,0:T(8,128)S(1)} %fusion.16, f32[32,4,16,128]{3,1,2,0:T(4,128)} %all-to-all-done.3, f32[32,2,4,256]{3,0,2,1:T(8,128)S(1)} %sine_add_fusion.1), kind=kOutput, calls=%fused_computation.1 | convolution fusion | flops 403701760 | bytes 5373952 | tf_op jit(solution)/shard_map/sxn,sxyz->yzn/dot_general | solution.py:32
  (29 shorter events, 0.2 us)
Async XLA Ops:
  5.2 15.9 %collective-permute-start = (f32[6,128,256]{2,1,0:T(8,128)}, f32[6,128,256]{2,1,0:T(8,128)S(1)}, u32[]{:S(2)}, u32[]{:S(2)}) collective-permute-start(f32[6,128,256]{2,1,0:T(8,128)} %get-tuple-element.16), channel_id=1, source_target_pairs={{0,2},{2,4},{4,6},{6,8},{8,10},{10,12},{12,14},{14,16},{16,18},{18... | collective-permute-start | bytes 2359304 | tf_op jit(solution)/shard_map/ppermute | solution.py:236
  5.2 15.9 %collective-permute-start.1 = (f32[6,128,256]{2,1,0:T(8,128)}, f32[6,128,256]{2,1,0:T(8,128)S(1)}, u32[]{:S(2)}, u32[]{:S(2)}) collective-permute-start(f32[6,128,256]{2,1,0:T(8,128)} %get-tuple-element.17), channel_id=1, source_target_pairs={{2,0},{4,2},{6,4},{8,6},{10,8},{12,10},{14,12},{16,14},{18,16},{20... | collective-permute-start | bytes 2359304 | tf_op jit(solution)/shard_map/ppermute | solution.py:236
  9.0 11.2 %collective-permute-start.2 = (f32[2,6,16,1,256]{4,3,2,1,0:T(1,128)S(1)}, f32[2,6,16,1,256]{4,3,2,1,0:T(1,128)S(1)}, u32[]{:S(2)}, u32[]{:S(2)}) collective-permute-start(f32[2,6,16,1,256]{4,3,2,1,0:T(1,128)S(1)} %pad_maximum_fusion), channel_id=1, source_target_pairs={{0,1},{1,0},{2,3},{3,2},{4,5},{5,4},{6,7},{7,6},{8,9},{9,8},{10,11... | collective-permute-start | bytes 589832 | tf_op jit(solution)/shard_map/ppermute | solution.py:233
  21.1 1.0 copy-start.1
  21.1 1.2 copy-start.2
  42.2 11.7 %copy-start = (f32[16,128,256]{2,1,0:T(8,128)S(1)}, f32[16,128,256]{2,1,0:T(8,128)}, u32[]{:S(2)}) copy-start(f32[16,128,256]{2,1,0:T(8,128)} %get-tuple-element.25) | copy-start | bytes 6291460
  43.8 35.4 %all-to-all-start = ((f32[32,4,16,128]{3,2,1,0:T(8,128)}), f32[32,4,16,128]{3,2,1,0:T(8,128)S(1)}, u32[]{:S(2)}, u32[]{:S(2)}) async-start(f32[32,4,16,128]{3,2,1,0:T(8,128)} %copy.13), calls=%async_computation | async-start | bytes 2097152 | tf_op jit(solution)/shard_map/all_to_all | solution.py:310
  79.2 29.9 %all-to-all-start.2 = ((f32[32,4,16,128]{3,2,1,0:T(8,128)}), f32[32,4,16,128]{3,2,1,0:T(8,128)S(1)}, u32[]{:S(2)}, u32[]{:S(2)}) async-start(f32[32,4,16,128]{3,2,1,0:T(8,128)} %copy.19), calls=%async_computation.2 | async-start | bytes 2097152 | tf_op jit(solution)/shard_map/all_to_all | solution.py:310
  86.3 1.7 copy-start.5
  109.0 29.9 %all-to-all-start.1 = ((f32[32,4,16,128]{3,1,2,0:T(4,128)}), f32[32,4,16,128]{3,1,2,0:T(4,128)S(1)}, u32[]{:S(2)}, u32[]{:S(2)}) async-start(f32[32,4,16,128]{3,1,2,0:T(4,128)} %bitcast.18), calls=%async_computation.1 | async-start | bytes 2097152 | tf_op jit(solution)/shard_map/all_to_all | solution.py:325
  115.3 1.7 copy-start.6
  122.9 20.7 %copy-start.7 = (f32[2,16,1,256]{3,2,1,0:T(1,128)S(1)}, f32[2,16,1,256]{3,2,1,0:T(1,128)}, u32[]{:S(2)}) copy-start(f32[2,16,1,256]{3,2,1,0:T(1,128)} %get-tuple-element.24) | copy-start | bytes 98308
  122.9 20.7 %copy-start.8 = (f32[2,16,1,256]{3,2,1,0:T(1,128)S(1)}, f32[2,16,1,256]{3,2,1,0:T(1,128)}, u32[]{:S(2)}) copy-start(f32[2,16,1,256]{3,2,1,0:T(1,128)} %get-tuple-element.23) | copy-start | bytes 98308
  122.9 22.3 %copy-start.9 = (f32[2,128,256]{2,1,0:T(8,128)S(1)}, f32[2,128,256]{2,1,0:T(8,128)}, u32[]{:S(2)}) copy-start(f32[2,128,256]{2,1,0:T(8,128)} %get-tuple-element.22) | copy-start | bytes 786436
  138.9 42.0 %all-to-all-start.3 = ((f32[32,4,16,128]{3,1,2,0:T(4,128)}), f32[32,4,16,128]{3,1,2,0:T(4,128)}, u32[]{:S(2)}, u32[]{:S(2)}) async-start(f32[32,4,16,128]{3,1,2,0:T(4,128)} %bitcast.29), calls=%async_computation.3 | async-start | bytes 2097152 | tf_op jit(solution)/shard_map/all_to_all | solution.py:325
  143.6 9.9 %collective-permute-start.5 = (f32[2,2,16,1,256]{4,3,2,1,0:T(1,128)S(1)}, f32[2,2,16,1,256]{4,3,2,1,0:T(1,128)S(1)}, u32[]{:S(2)}, u32[]{:S(2)}) collective-permute-start(f32[2,2,16,1,256]{4,3,2,1,0:T(1,128)S(1)} %pad_maximum_fusion.1), channel_id=1, source_target_pairs={{0,1},{1,0},{2,3},{3,2},{4,5},{5,4},{6,7},{7,6},{8,9},{9,8},{10,11... | collective-permute-start | bytes 196616 | tf_op jit(solution)/shard_map/ppermute | solution.py:233
  145.2 26.4 %collective-permute-start.3 = (f32[2,128,256]{2,1,0:T(8,128)}, f32[2,128,256]{2,1,0:T(8,128)S(1)}, u32[]{:S(2)}, u32[]{:S(2)}) collective-permute-start(f32[2,128,256]{2,1,0:T(8,128)} %get-tuple-element.21), channel_id=1, source_target_pairs={{0,2},{2,4},{4,6},{6,8},{8,10},{10,12},{12,14},{14,16},{16,18},{18... | collective-permute-start | bytes 786440 | tf_op jit(solution)/shard_map/ppermute | solution.py:236
  145.2 26.4 %collective-permute-start.4 = (f32[2,128,256]{2,1,0:T(8,128)S(1)}, f32[2,128,256]{2,1,0:T(8,128)S(1)}, u32[]{:S(2)}, u32[]{:S(2)}) collective-permute-start(f32[2,128,256]{2,1,0:T(8,128)S(1)} %copy-done.9), channel_id=1, source_target_pairs={{2,0},{4,2},{6,4},{8,6},{10,8},{12,10},{14,12},{16,14},{18,16},{20... | collective-permute-start | bytes 786440 | tf_op jit(solution)/shard_map/ppermute | solution.py:236
  171.6 0.7 copy-start.3
  171.6 0.8 copy-start.4

commit v2 on v1

--- a/solution.py
+++ b/solution.py
@@ -287,7 +287,7 @@
     return (lam, phase_grad)
 
 
-def dipole_adjoint(phase_grad):
+def dipole_adjoint(phase_grad, lam):
     count_y = lax.axis_size("gy")
     count_z = lax.axis_size("gz")
     parts = count_y * count_z
@@ -307,6 +307,8 @@
     sent = []
     for p in range(pieces):
         spec = along("sxn,yzn->sxyz", table_x[:, p], phase_grad)
+        if p == pieces - 1 and pieces > 1:
+            lam, spec = lax.optimization_barrier((lam, spec))
         sent.append(lax.all_to_all(spec, ("gy", "gz"), 0, 0, tiled=True))
     result = None
     for p in range(pieces):
@@ -325,12 +327,12 @@
         spec = lax.all_to_all(spec, ("gy", "gz"), 0, 0, tiled=True)
         part = along("sxn,sxyz->yzn", table_x[:, p], spec)
         result = part if result is None else result + part
-    return result * scale
+    return result * scale, lam
 
 
 def per_device(mag_start, mag_middle, adjoint_end, phase, labels):
     lam, phase_grad = backward_sections(mag_start, mag_middle, adjoint_end, phase, labels)
-    chi_grad = dipole_adjoint(phase_grad)
+    chi_grad, lam = dipole_adjoint(phase_grad, lam)
     return (lam, chi_grad)
 
 

time: 186 us -> 187 us (level); the launches traced: 185 us -> 184 us
    all_to_all x2, waiting for transfers between devices: 14.3 us -> 38.2 us  [dipole_adjoint(): spec = lax.all_to_all(spec, ('gy', 'gz'), 0, 0, tiled=True)]
    all_to_all x2, waiting for transfers between devices: 36 us -> 12.3 us  [dipole_adjoint(): sent.append(lax.all_to_all(spec, ('gy', 'gz'), 0, 0, tiled=True))]
  transfers between devices with their start and end apart: 10 -> 10, of which waited for: 5 -> 5; matrix products, arithmetic and copies ran while one was open for 16% -> 17% of each run, Pallas kernels for 8% -> 9%
where the time goes in v2:
time: 187 us; the launch traced here: 184 us
  waiting for transfers between devices  72.6 us (39%)
  Pallas kernels  37.3 us (20%)
  starting transfers between devices  31.7 us (17%)
  matrix products  23.2 us (12%)
  local copies, waits for them, and re-layouts  14.8 us (8%)
  other arithmetic  3.14 us (2%)
    all_to_all x2, waiting for transfers between devices, dipole_adjoint(): spec = lax.all_to_all(spec, ('gy', 'gz'), 0, 0, tiled=True)  38.2 us
    dot_general x12, matrix products, along(): return jnp.einsum(spec, table, values, precision=lax.Precision.HIGH)  23.2 us
    ppermute x2, waiting for transfers between devices, send_edges(): lax.ppermute(last, axis, up)  17.6 us
    pallas_call x1, Pallas kernels, backward_sections(): pl.pallas_call(functools.partial(first_kernel, rows=rows), grid=grid, in_...  17.1 us
    all_to_all x2, starting transfers between devices, dipole_adjoint(): sent.append(lax.all_to_all(spec, ('gy', 'gz'), 0, 0, tiled=True))  14 us
    all_to_all x2, waiting for transfers between devices, dipole_adjoint(): sent.append(lax.all_to_all(spec, ('gy', 'gz'), 0, 0, tiled=True))  12.3 us
    all_to_all x2, starting transfers between devices, dipole_adjoint(): spec = lax.all_to_all(spec, ('gy', 'gz'), 0, 0, tiled=True)  9.27 us
    pallas_call x1, Pallas kernels, backward_sections(): pl.pallas_call(functools.partial(factor_kernel, rows=rows), grid=grid, in...  8.52 us
  transfers between devices with their start and end apart: 10, of which 5 were waited for; matrix products, arithmetic and copies ran while one was open for 17% of the time, Pallas kernels for 9%

profile of v2, /device:TPU:16, one launch (start us, length us, event | category | flops | bytes accessed | tf_op | source)
XLA Modules:
  0.0 183.7 jit_solution(12936719456472597142)
XLA Ops:
  0.6 4.5 %shard_map.69 = (f32[6,128,256]{2,1,0:T(8,128)}, f32[6,128,256]{2,1,0:T(8,128)}, f32[6,16,1,256]{3,2,1,0:T(1,128)}, f32[6,16,1,256]{3,2,1,0:T(1,128)}) custom-call(f32[2,16,128,256]{3,2,1,0:T(8,128)} %refs_2_.3, f32[2,16,128,256]{3,2,1,0:T(8,128)} %refs_2_.3, f32[2,16,128,256]{3,2,1,0:T(8,128)} %refs_2_.3, f32[2,16,128,256]{3,2,1,0:T(8,128)} %refs_2_.3, ...), custom_call_target="tpu_custom_call" | custom-call | tf_op jit(solution)/shard_map/pallas_call | solution.py:253
  5.2 0.1 collective-permute-start
  5.2 2.6 %collective-permute-start.1 = (f32[6,128,256]{2,1,0:T(8,128)}, f32[6,128,256]{2,1,0:T(8,128)S(1)}, u32[]{:S(2)}, u32[]{:S(2)}) collective-permute-start(f32[6,128,256]{2,1,0:T(8,128)} %get-tuple-element.19), channel_id=1, source_target_pairs={{2,0},{4,2},{6,4},{8,6},{10,8},{12,10},{14,12},{16,14},{18,16},{20... | collective-permute-start | bytes 2359304 | tf_op jit(solution)/shard_map/ppermute | solution.py:236
  7.9 1.1 pad_maximum_fusion
  9.0 1.6 collective-permute-start.2
  10.6 8.5 %shard_map.68 = (f32[2,16,128,256]{3,2,1,0:T(8,128)}, f32[2,16,128,256]{3,2,1,0:T(8,128)}) custom-call(f32[2,16,128,256]{3,2,1,0:T(8,128)} %refs_11_.1, f32[16,128,256]{2,1,0:T(8,128)} %refs_15_.1, s32[16,128,256]{2,1,0:T(8,128)} %refs_19_.1), custom_call_target="tpu_custom_call" | custom-call | tf_op jit(solution)/shard_map/pallas_call | solution.py:261
  19.1 1.1 sine_add_fusion.1
  20.2 0.8 slice_bitcast_fusion
  21.1 1.0 copy-done.1
  22.0 0.2 copy-done.2
  22.2 17.1 %shard_map.70 = (f32[16,128,256]{2,1,0:T(8,128)}, f32[2,16,128,256]{3,2,1,0:T(8,128)}, f32[2,128,256]{2,1,0:T(8,128)}, f32[2,128,256]{2,1,0:T(8,128)}, f32[2,16,...) custom-call(f32[2,16,128,256]{3,2,1,0:T(8,128)} %refs_2_.3, f32[2,16,128,256]{3,2,1,0:T(8,128)} %refs_2_.3, ...), custom_call_target="tpu_custom_call" | custom-call | tf_op jit(solution)/shard_map/pallas_call | solution.py:268
  39.3 2.8 %fusion.1 = f32[32,4,16,128]{3,0,2,1:T(8,128)S(1)} fusion(f32[16,128,256]{2,1,0:T(8,128)} %get-tuple-element.27, f32[32,2,4,256]{3,0,2,1:T(8,128)S(1)} %sine_add_fusion.1), kind=kOutput, calls=%fused_computation.2 | convolution fusion | flops 402653184 | bytes 3276800 | tf_op jit(solution)/shard_map/sxn,yzn->sxyz/dot_general | solution.py:32
  42.1 1.6 copy.13
  43.7 10.2 %all-to-all-start = ((f32[32,4,16,128]{3,2,1,0:T(8,128)}), f32[32,4,16,128]{3,2,1,0:T(8,128)}, u32[]{:S(2)}, u32[]{:S(2)}) async-start(f32[32,4,16,128]{3,2,1,0:T(8,128)} %copy.13), calls=%async_computation | async-start | bytes 2097152 | tf_op jit(solution)/shard_map/all_to_all | solution.py:312
  54.0 0.1 pad_maximum_fusion.1
  54.1 1.5 collective-permute-start.5
  55.6 2.6 %collective-permute-start.4 = (f32[2,128,256]{2,1,0:T(8,128)}, f32[2,128,256]{2,1,0:T(8,128)}, u32[]{:S(2)}, u32[]{:S(2)}) collective-permute-start(f32[2,128,256]{2,1,0:T(8,128)} %get-tuple-element.24), channel_id=1, source_target_pairs={{2,0},{4,2},{6,4},{8,6},{10,8},{12,10},{14,12},{16,14},{18,16},{20... | collective-permute-start | bytes 786440 | tf_op jit(solution)/shard_map/ppermute | solution.py:236
  58.2 1.2 fusion.3
  59.4 4.5 %collective-permute-done.5 = f32[2,2,16,1,256]{4,3,2,1,0:T(1,128)S(1)} collective-permute-done((f32[2,2,16,1,256]{4,3,2,1,0:T(1,128)S(1)}, f32[2,2,16,1,256]{4,3,2,1,0:T(1,128)S(1)}, u32[]{:S(2)}, u32[]{:S(2)}) %collective-permute-start.5) | collective-permute-done | bytes 65568 | tf_op jit(solution)/shard_map/ppermute | solution.py:233
  63.9 0.6 slice_bitcast_fusion.2
  64.5 17.6 %collective-permute-done.3.y_low_ref = f32[2,128,256]{2,1,0:T(8,128)} collective-permute-done((f32[2,128,256]{2,1,0:T(8,128)}, f32[2,128,256]{2,1,0:T(8,128)}, u32[]{:S(2)}, u32[]{:S(2)}) %collective-permute-start.3) | collective-permute-done | bytes 262176 | tf_op jit(solution)/shard_map/ppermute | solution.py:236
  82.1 7.1 %shard_map.71 = f32[2,16,128,256]{3,2,1,0:T(8,128)} custom-call(f32[2,16,128,256]{3,2,1,0:T(8,128)} %get-tuple-element.22.w_ref.w_prev.w_next, f32[2,16,128,256]{3,2,1,0:T(8,128)} %get-tuple-element.22.w_ref.w_prev.w_next, f32[2,16,128,256]{3,2,1,0:T(8,128)} %get-tuple-element.22.w_ref.w_prev.w_next, f32[2,128,256]{2,1,0:T(8,128)} %collective-permute-done.3.y_low_ref, ...), custom_call_target="tpu_custom_call" | custom-call | tf_op jit(solution)/shard_map/pallas_call | solution.py:279
  89.2 1.6 copy.19
  90.8 3.7 %all-to-all-start.2 = ((f32[32,4,16,128]{3,2,1,0:T(8,128)}), f32[32,4,16,128]{3,2,1,0:T(8,128)S(1)}, u32[]{:S(2)}, u32[]{:S(2)}) async-start(f32[32,4,16,128]{3,2,1,0:T(8,128)} %copy.19), calls=%async_computation.2 | async-start | bytes 2097152 | tf_op jit(solution)/shard_map/all_to_all | solution.py:312
  94.6 0.8 broadcast_add_fusion
  95.4 2.0 %copy.40 = f32[16,2,4,16,128]{4,1,3,0,2:T(2,128)S(1)} copy(f32[16,2,4,16,128]{4,3,2,1,0:T(8,128)} %bitcast.15) | data formatting | bytes 2097152 | tf_op jit(solution)/shard_map/reshape | solution.py:315
  97.5 0.8 reshape.120
  98.3 1.6 fusion.34
  100.0 1.8 fusion.5
  101.8 1.6 convolution_bitcast_fusion.2
  103.4 1.9 %fusion.30 = f32[4,256,256]{2,1,0:T(8,128)S(1)} fusion(f32[4,256,256]{1,2,0:T(8,128)S(1)} %convolution_bitcast_fusion.2), kind=kOutput, calls=%fused_computation.47 | convolution fusion | flops 403636224 | bytes 2097152 | tf_op jit(solution)/shard_map/kz,xyz->xyk/dot_general | solution.py:32
  105.3 0.5 reshape.121
  105.8 1.7 copy.17
  107.5 12.3 %all-to-all-done.2 = f32[32,4,16,128]{3,2,1,0:T(8,128)S(1)} async-done(((f32[32,4,16,128]{3,2,1,0:T(8,128)}), f32[32,4,16,128]{3,2,1,0:T(8,128)S(1)}, u32[]{:S(2)}, u32[]{:S(2)}) %all-to-all-start.2) | async-done | bytes 1048608 | tf_op jit(solution)/shard_map/all_to_all | solution.py:312
  119.8 4.6 %all-to-all-start.1 = ((f32[32,4,16,128]{3,1,2,0:T(4,128)}), f32[32,4,16,128]{3,1,2,0:T(4,128)S(1)}, u32[]{:S(2)}, u32[]{:S(2)}) async-start(f32[32,4,16,128]{3,1,2,0:T(4,128)} %bitcast.21), calls=%async_computation.1 | async-start | bytes 2097152 | tf_op jit(solution)/shard_map/all_to_all | solution.py:327
  124.5 0.8 copy.39
  125.3 0.8 reshape.124
  126.1 1.6 fusion.28
  127.8 1.8 fusion.6
  129.6 1.6 convolution_bitcast_fusion
  131.2 1.9 %fusion.24 = f32[4,256,256]{2,1,0:T(8,128)S(1)} fusion(f32[4,256,256]{1,2,0:T(8,128)S(1)} %convolution_bitcast_fusion), kind=kOutput, calls=%fused_computation.41 | convolution fusion | flops 403636224 | bytes 2097152 | tf_op jit(solution)/shard_map/kz,xyz->xyk/dot_general | solution.py:32
  133.1 0.5 reshape.125
  133.7 1.7 copy.23
  135.3 14.4 %all-to-all-done.1 = f32[32,4,16,128]{3,1,2,0:T(4,128)S(1)} async-done(((f32[32,4,16,128]{3,1,2,0:T(4,128)}), f32[32,4,16,128]{3,1,2,0:T(4,128)S(1)}, u32[]{:S(2)}, u32[]{:S(2)}) %all-to-all-start.1) | async-done | bytes 1048608 | tf_op jit(solution)/shard_map/all_to_all | solution.py:327
  149.7 4.7 %all-to-all-start.3 = ((f32[32,4,16,128]{3,1,2,0:T(4,128)}), f32[32,4,16,128]{3,1,2,0:T(4,128)}, u32[]{:S(2)}, u32[]{:S(2)}) async-start(f32[32,4,16,128]{3,1,2,0:T(4,128)} %bitcast.29), calls=%async_computation.3 | async-start | bytes 2097152 | tf_op jit(solution)/shard_map/all_to_all | solution.py:327
  154.4 1.5 fusion.16
  155.9 23.8 %all-to-all-done.3 = f32[32,4,16,128]{3,1,2,0:T(4,128)} async-done(((f32[32,4,16,128]{3,1,2,0:T(4,128)}), f32[32,4,16,128]{3,1,2,0:T(4,128)}, u32[]{:S(2)}, u32[]{:S(2)}) %all-to-all-start.3) | async-done | bytes 1048608 | tf_op jit(solution)/shard_map/all_to_all | solution.py:327
  179.7 4.0 %fusion = f32[16,128,256]{2,1,0:T(8,128)} fusion(f32[16,128,256,1]{2,1,3,0:T(8,128)S(1)} %fusion.16, f32[32,4,16,128]{3,1,2,0:T(4,128)} %all-to-all-done.3, f32[32,2,4,256]{3,0,2,1:T(8,128)S(1)} %sine_add_fusion.1), kind=kOutput, calls=%fused_computation.1 | convolution fusion | flops 403701760 | bytes 5373952 | tf_op jit(solution)/shard_map/sxn,sxyz->yzn/dot_general | solution.py:32
  (23 shorter events, 0.1 us)
Async XLA Ops:
  5.2 15.9 %collective-permute-start = (f32[6,128,256]{2,1,0:T(8,128)}, f32[6,128,256]{2,1,0:T(8,128)S(1)}, u32[]{:S(2)}, u32[]{:S(2)}) collective-permute-start(f32[6,128,256]{2,1,0:T(8,128)} %get-tuple-element.18), channel_id=1, source_target_pairs={{0,2},{2,4},{4,6},{6,8},{8,10},{10,12},{12,14},{14,16},{16,18},{18... | collective-permute-start | bytes 2359304 | tf_op jit(solution)/shard_map/ppermute | solution.py:236
  5.2 15.8 %collective-permute-start.1 = (f32[6,128,256]{2,1,0:T(8,128)}, f32[6,128,256]{2,1,0:T(8,128)S(1)}, u32[]{:S(2)}, u32[]{:S(2)}) collective-permute-start(f32[6,128,256]{2,1,0:T(8,128)} %get-tuple-element.19), channel_id=1, source_target_pairs={{2,0},{4,2},{6,4},{8,6},{10,8},{12,10},{14,12},{16,14},{18,16},{20... | collective-permute-start | bytes 2359304 | tf_op jit(solution)/shard_map/ppermute | solution.py:236
  9.0 11.2 %collective-permute-start.2 = (f32[2,6,16,1,256]{4,3,2,1,0:T(1,128)S(1)}, f32[2,6,16,1,256]{4,3,2,1,0:T(1,128)S(1)}, u32[]{:S(2)}, u32[]{:S(2)}) collective-permute-start(f32[2,6,16,1,256]{4,3,2,1,0:T(1,128)S(1)} %pad_maximum_fusion), channel_id=1, source_target_pairs={{0,1},{1,0},{2,3},{3,2},{4,5},{5,4},{6,7},{7,6},{8,9},{9,8},{10,11... | collective-permute-start | bytes 589832 | tf_op jit(solution)/shard_map/ppermute | solution.py:233
  21.0 1.0 copy-start.1
  21.1 1.2 copy-start.2
  42.1 11.9 %copy-start.5 = (f32[2,16,1,256]{3,2,1,0:T(1,128)S(1)}, f32[2,16,1,256]{3,2,1,0:T(1,128)}, u32[]{:S(2)}) copy-start(f32[2,16,1,256]{3,2,1,0:T(1,128)} %get-tuple-element.26) | copy-start | bytes 98308
  42.1 11.9 %copy-start.6 = (f32[2,16,1,256]{3,2,1,0:T(1,128)S(1)}, f32[2,16,1,256]{3,2,1,0:T(1,128)}, u32[]{:S(2)}) copy-start(f32[2,16,1,256]{3,2,1,0:T(1,128)} %get-tuple-element.25) | copy-start | bytes 98308
  42.1 16.1 %copy-start = (f32[16,128,256]{2,1,0:T(8,128)S(1)}, f32[16,128,256]{2,1,0:T(8,128)}, u32[]{:S(2)}) copy-start(f32[16,128,256]{2,1,0:T(8,128)} %get-tuple-element.27) | copy-start | bytes 6291460
  43.7 47.1 %all-to-all-start = ((f32[32,4,16,128]{3,2,1,0:T(8,128)}), f32[32,4,16,128]{3,2,1,0:T(8,128)}, u32[]{:S(2)}, u32[]{:S(2)}) async-start(f32[32,4,16,128]{3,2,1,0:T(8,128)} %copy.13), calls=%async_computation | async-start | bytes 2097152 | tf_op jit(solution)/shard_map/all_to_all | solution.py:312
  54.1 9.9 %collective-permute-start.5 = (f32[2,2,16,1,256]{4,3,2,1,0:T(1,128)S(1)}, f32[2,2,16,1,256]{4,3,2,1,0:T(1,128)S(1)}, u32[]{:S(2)}, u32[]{:S(2)}) collective-permute-start(f32[2,2,16,1,256]{4,3,2,1,0:T(1,128)S(1)} %pad_maximum_fusion.1), channel_id=1, source_target_pairs={{0,1},{1,0},{2,3},{3,2},{4,5},{5,4},{6,7},{7,6},{8,9},{9,8},{10,11... | collective-permute-start | bytes 196616 | tf_op jit(solution)/shard_map/ppermute | solution.py:233
  55.6 26.5 %collective-permute-start.3 = (f32[2,128,256]{2,1,0:T(8,128)}, f32[2,128,256]{2,1,0:T(8,128)}, u32[]{:S(2)}, u32[]{:S(2)}) collective-permute-start(f32[2,128,256]{2,1,0:T(8,128)} %get-tuple-element.23), channel_id=1, source_target_pairs={{0,2},{2,4},{4,6},{6,8},{8,10},{10,12},{12,14},{14,16},{16,18},{18... | collective-permute-start | bytes 786440 | tf_op jit(solution)/shard_map/ppermute | solution.py:236
  55.6 26.5 %collective-permute-start.4 = (f32[2,128,256]{2,1,0:T(8,128)}, f32[2,128,256]{2,1,0:T(8,128)}, u32[]{:S(2)}, u32[]{:S(2)}) collective-permute-start(f32[2,128,256]{2,1,0:T(8,128)} %get-tuple-element.24), channel_id=1, source_target_pairs={{2,0},{4,2},{6,4},{8,6},{10,8},{12,10},{14,12},{16,14},{18,16},{20... | collective-permute-start | bytes 786440 | tf_op jit(solution)/shard_map/ppermute | solution.py:236
  90.8 29.0 %all-to-all-start.2 = ((f32[32,4,16,128]{3,2,1,0:T(8,128)}), f32[32,4,16,128]{3,2,1,0:T(8,128)S(1)}, u32[]{:S(2)}, u32[]{:S(2)}) async-start(f32[32,4,16,128]{3,2,1,0:T(8,128)} %copy.19), calls=%async_computation.2 | async-start | bytes 2097152 | tf_op jit(solution)/shard_map/all_to_all | solution.py:312
  98.3 1.7 copy-start.3
  119.8 29.9 %all-to-all-start.1 = ((f32[32,4,16,128]{3,1,2,0:T(4,128)}), f32[32,4,16,128]{3,1,2,0:T(4,128)S(1)}, u32[]{:S(2)}, u32[]{:S(2)}) async-start(f32[32,4,16,128]{3,1,2,0:T(4,128)} %bitcast.21), calls=%async_computation.1 | async-start | bytes 2097152 | tf_op jit(solution)/shard_map/all_to_all | solution.py:327
  126.1 1.7 copy-start.4
  149.7 30.0 %all-to-all-start.3 = ((f32[32,4,16,128]{3,1,2,0:T(4,128)}), f32[32,4,16,128]{3,1,2,0:T(4,128)}, u32[]{:S(2)}, u32[]{:S(2)}) async-start(f32[32,4,16,128]{3,1,2,0:T(4,128)} %bitcast.29), calls=%async_computation.3 | async-start | bytes 2097152 | tf_op jit(solution)/shard_map/all_to_all | solution.py:327

commit v3 on v2

--- a/solution.py
+++ b/solution.py
@@ -276,6 +276,11 @@
     )(mag_middle, mag_middle, mag_middle, mag_start, mag_start, mag_start,
       w_first, w_first, w_first, factor, *halos)
     halos = send_edges(*w2_edges)
+    return phase_grad, functools.partial(finish_lambda, w_second, rows, grid, cur, whole, zspec, length_z, length_x), halos
+
+
+def finish_lambda(w_second, rows, grid, cur, whole, zspec, length_z, length_x, halos):
+    pair = jax.ShapeDtypeStruct(w_second.shape, jnp.float32)
     lam = pl.pallas_call(
         functools.partial(second_kernel, rows=rows),
         grid=grid,
@@ -284,10 +289,10 @@
         out_specs=cur,
         out_shape=pair,
     )(w_second, w_second, w_second, *halos)
-    return (lam, phase_grad)
-
-
-def dipole_adjoint(phase_grad, lam):
+    return lam
+
+
+def dipole_adjoint(phase_grad, finish, halos):
     count_y = lax.axis_size("gy")
     count_z = lax.axis_size("gz")
     parts = count_y * count_z
@@ -307,9 +312,11 @@
     sent = []
     for p in range(pieces):
         spec = along("sxn,yzn->sxyz", table_x[:, p], phase_grad)
-        if p == pieces - 1 and pieces > 1:
-            lam, spec = lax.optimization_barrier((lam, spec))
+        if p == 0:
+            halos, spec = lax.optimization_barrier((halos, spec))
         sent.append(lax.all_to_all(spec, ("gy", "gz"), 0, 0, tiled=True))
+        if p == 0:
+            lam = finish(halos)
     result = None
     for p in range(pieces):
         spec = sent[p].reshape(count_y, count_z, piece_x, block_y, block_z)
@@ -331,8 +338,8 @@
 
 
 def per_device(mag_start, mag_middle, adjoint_end, phase, labels):
-    lam, phase_grad = backward_sections(mag_start, mag_middle, adjoint_end, phase, labels)
-    chi_grad, lam = dipole_adjoint(phase_grad, lam)
+    phase_grad, finish, halos = backward_sections(mag_start, mag_middle, adjoint_end, phase, labels)
+    chi_grad, lam = dipole_adjoint(phase_grad, finish, halos)
     return (lam, chi_grad)
 
 

time: 187 us -> 184 us (0.984)
  waiting for transfers between devices: 72.6 us -> 67.9 us
    all_to_all x2, waiting for transfers between devices: 12.3 us -> 36 us  [dipole_adjoint(): sent.append(lax.all_to_all(spec, ('gy', 'gz'), 0, 0, tiled=True))]
    ppermute x2, waiting for transfers between devices: 17.6 us -> 0.01 us  [send_edges(): lax.ppermute(last, axis, up)]
    all_to_all x2, waiting for transfers between devices: 38.2 us -> 31.1 us  [dipole_adjoint(): spec = lax.all_to_all(spec, ('gy', 'gz'), 0, 0, tiled=True)]
    ppermute x2, starting transfers between devices: 0.06 us -> 5.38 us  [send_edges(): lax.ppermute(last, axis, up)]
    ppermute x2, waiting for transfers between devices: 4.51 us -> 0.01 us  [send_edges(): both = lax.ppermute(jnp.stack([last, first]), axis, up)]
    ppermute x2, starting transfers between devices: 5.27 us -> 2.63 us  [send_edges(): lax.ppermute(first, axis, down)]
  transfers between devices with their start and end apart: 10 -> 10, of which waited for: 5 -> 5; matrix products, arithmetic and copies ran while one was open for 17% -> 18% of each run, Pallas kernels for 9% -> 9%
where the time goes in v3:
time: 184 us; the launch traced here: 181 us
  waiting for transfers between devices  67.9 us (37%)
  Pallas kernels  37.3 us (20%)
  starting transfers between devices  33.5 us (18%)
  matrix products  23.2 us (13%)
  local copies, waits for them, and re-layouts  14.3 us (8%)
  other arithmetic  3.93 us (2%)
    all_to_all x2, waiting for transfers between devices, dipole_adjoint(): sent.append(lax.all_to_all(spec, ('gy', 'gz'), 0, 0, tiled=True))  36 us
    all_to_all x2, waiting for transfers between devices, dipole_adjoint(): spec = lax.all_to_all(spec, ('gy', 'gz'), 0, 0, tiled=True)  31.1 us
    dot_general x12, matrix products, along(): return jnp.einsum(spec, table, values, precision=lax.Precision.HIGH)  23.2 us
    pallas_call x1, Pallas kernels, backward_sections(): pl.pallas_call(functools.partial(first_kernel, rows=rows), grid=grid, in_...  17.1 us
    all_to_all x2, starting transfers between devices, dipole_adjoint(): sent.append(lax.all_to_all(spec, ('gy', 'gz'), 0, 0, tiled=True))  14.1 us
    all_to_all x2, starting transfers between devices, dipole_adjoint(): spec = lax.all_to_all(spec, ('gy', 'gz'), 0, 0, tiled=True)  9.27 us
    pallas_call x1, Pallas kernels, backward_sections(): pl.pallas_call(functools.partial(factor_kernel, rows=rows), grid=grid, in...  8.52 us
    pallas_call x1, Pallas kernels, finish_lambda(): pl.pallas_call(functools.partial(second_kernel, rows=rows), grid=grid, in...  7.13 us
  transfers between devices with their start and end apart: 10, of which 5 were waited for; matrix products, arithmetic and copies ran while one was open for 18% of the time, Pallas kernels for 9%

profile of v3, /device:TPU:16, one launch (start us, length us, event | category | flops | bytes accessed | tf_op | source)
XLA Modules:
  0.0 181.1 jit_solution(6249372684284062351)
XLA Ops:
  0.6 4.5 %shard_map.69 = (f32[6,128,256]{2,1,0:T(8,128)}, f32[6,128,256]{2,1,0:T(8,128)}, f32[6,16,1,256]{3,2,1,0:T(1,128)}, f32[6,16,1,256]{3,2,1,0:T(1,128)}) custom-call(f32[2,16,128,256]{3,2,1,0:T(8,128)} %refs_2_.3, f32[2,16,128,256]{3,2,1,0:T(8,128)} %refs_2_.3, f32[2,16,128,256]{3,2,1,0:T(8,128)} %refs_2_.3, f32[2,16,128,256]{3,2,1,0:T(8,128)} %refs_2_.3, ...), custom_call_target="tpu_custom_call" | custom-call | tf_op jit(solution)/shard_map/pallas_call | solution.py:253
  5.2 2.6 %collective-permute-start.1 = (f32[6,128,256]{2,1,0:T(8,128)}, f32[6,128,256]{2,1,0:T(8,128)S(1)}, u32[]{:S(2)}, u32[]{:S(2)}) collective-permute-start(f32[6,128,256]{2,1,0:T(8,128)} %get-tuple-element.22), channel_id=1, source_target_pairs={{2,0},{4,2},{6,4},{8,6},{10,8},{12,10},{14,12},{16,14},{18,16},{20... | collective-permute-start | bytes 2359304 | tf_op jit(solution)/shard_map/ppermute | solution.py:236
  7.9 1.1 pad_maximum_fusion
  9.0 1.6 collective-permute-start.2
  10.6 8.5 %shard_map.68 = (f32[2,16,128,256]{3,2,1,0:T(8,128)}, f32[2,16,128,256]{3,2,1,0:T(8,128)}) custom-call(f32[2,16,128,256]{3,2,1,0:T(8,128)} %refs_11_.1, f32[16,128,256]{2,1,0:T(8,128)} %refs_15_.1, s32[16,128,256]{2,1,0:T(8,128)} %refs_19_.1), custom_call_target="tpu_custom_call" | custom-call | tf_op jit(solution)/shard_map/pallas_call | solution.py:261
  19.1 1.1 sine_add_fusion.1
  20.2 0.8 slice_bitcast_fusion
  21.1 1.0 copy-done.1
  22.0 0.2 copy-done.2
  22.2 17.1 %shard_map.70 = (f32[16,128,256]{2,1,0:T(8,128)}, f32[2,16,128,256]{3,2,1,0:T(8,128)}, f32[2,128,256]{2,1,0:T(8,128)}, f32[2,128,256]{2,1,0:T(8,128)}, f32[2,16,...) custom-call(f32[2,16,128,256]{3,2,1,0:T(8,128)} %refs_2_.3, f32[2,16,128,256]{3,2,1,0:T(8,128)} %refs_2_.3, ...), custom_call_target="tpu_custom_call" | custom-call | tf_op jit(solution)/shard_map/pallas_call | solution.py:268
  39.3 0.8 pad_maximum_fusion.1
  40.2 0.6 collective-permute-start.5
  40.8 5.3 %collective-permute-start.3 = (f32[2,128,256]{2,1,0:T(8,128)}, f32[2,128,256]{2,1,0:T(8,128)S(1)}, u32[]{:S(2)}, u32[]{:S(2)}) collective-permute-start(f32[2,128,256]{2,1,0:T(8,128)} %get-tuple-element.26), channel_id=1, source_target_pairs={{0,2},{2,4},{4,6},{6,8},{8,10},{10,12},{12,14},{14,16},{16,18},{18... | collective-permute-start | bytes 786440 | tf_op jit(solution)/shard_map/ppermute | solution.py:236
  46.1 2.8 %fusion.3 = f32[32,4,16,128]{3,0,2,1:T(8,128)S(1)} fusion(f32[16,128,256]{2,1,0:T(8,128)} %get-tuple-element.30, f32[32,2,4,256]{3,0,2,1:T(8,128)S(1)} %sine_add_fusion.1), kind=kOutput, calls=%fused_computation.4 | convolution fusion | flops 402653184 | bytes 3276800 | tf_op jit(solution)/shard_map/sxn,yzn->sxyz/dot_general | solution.py:32
  48.9 0.6 slice_bitcast_fusion.2
  49.5 0.8 collective-permute-done.4.y_high_ref
  50.4 0.7 copy-done.4
  51.1 1.6 copy.13
  52.6 9.5 %all-to-all-start = ((f32[32,4,16,128]{3,2,1,0:T(8,128)}), f32[32,4,16,128]{3,2,1,0:T(8,128)S(1)}, u32[]{:S(2)}, u32[]{:S(2)}) async-start(f32[32,4,16,128]{3,2,1,0:T(8,128)} %copy.13), calls=%async_computation | async-start | bytes 2097152 | tf_op jit(solution)/shard_map/all_to_all | solution.py:317
  62.2 1.2 fusion.1
  63.3 1.6 copy.19
  65.0 22.5 %all-to-all-done = f32[32,4,16,128]{3,2,1,0:T(8,128)S(1)} async-done(((f32[32,4,16,128]{3,2,1,0:T(8,128)}), f32[32,4,16,128]{3,2,1,0:T(8,128)S(1)}, u32[]{:S(2)}, u32[]{:S(2)}) %all-to-all-start) | async-done | bytes 1048608 | tf_op jit(solution)/shard_map/all_to_all | solution.py:317
  87.4 4.6 %all-to-all-start.2 = ((f32[32,4,16,128]{3,2,1,0:T(8,128)}), f32[32,4,16,128]{3,2,1,0:T(8,128)S(1)}, u32[]{:S(2)}, u32[]{:S(2)}) async-start(f32[32,4,16,128]{3,2,1,0:T(8,128)} %copy.19), calls=%async_computation.2 | async-start | bytes 2097152 | tf_op jit(solution)/shard_map/all_to_all | solution.py:317
  92.1 0.8 broadcast_add_fusion
  92.9 0.8 copy.40
  93.7 0.8 reshape.120
  94.5 1.6 fusion.34
  96.2 1.8 fusion.5
  98.0 1.6 convolution_bitcast_fusion.2
  99.6 1.9 %fusion.30 = f32[4,256,256]{2,1,0:T(8,128)S(1)} fusion(f32[4,256,256]{1,2,0:T(8,128)S(1)} %convolution_bitcast_fusion.2), kind=kOutput, calls=%fused_computation.47 | convolution fusion | flops 403636224 | bytes 2097152 | tf_op jit(solution)/shard_map/kz,xyz->xyk/dot_general | solution.py:32
  101.5 0.5 reshape.121
  102.1 1.7 copy.17
  103.7 13.5 %all-to-all-done.2 = f32[32,4,16,128]{3,2,1,0:T(8,128)S(1)} async-done(((f32[32,4,16,128]{3,2,1,0:T(8,128)}), f32[32,4,16,128]{3,2,1,0:T(8,128)S(1)}, u32[]{:S(2)}, u32[]{:S(2)}) %all-to-all-start.2) | async-done | bytes 1048608 | tf_op jit(solution)/shard_map/all_to_all | solution.py:317
  117.3 4.6 %all-to-all-start.1 = ((f32[32,4,16,128]{3,1,2,0:T(4,128)}), f32[32,4,16,128]{3,1,2,0:T(4,128)S(1)}, u32[]{:S(2)}, u32[]{:S(2)}) async-start(f32[32,4,16,128]{3,1,2,0:T(4,128)} %bitcast.18), calls=%async_computation.1 | async-start | bytes 2097152 | tf_op jit(solution)/shard_map/all_to_all | solution.py:334
  121.9 0.8 copy.39
  122.7 0.8 reshape.124
  123.6 1.6 fusion.28
  125.2 1.8 fusion.6
  127.0 1.6 convolution_bitcast_fusion
  128.7 1.9 %fusion.24 = f32[4,256,256]{2,1,0:T(8,128)S(1)} fusion(f32[4,256,256]{1,2,0:T(8,128)S(1)} %convolution_bitcast_fusion), kind=kOutput, calls=%fused_computation.41 | convolution fusion | flops 403636224 | bytes 2097152 | tf_op jit(solution)/shard_map/kz,xyz->xyk/dot_general | solution.py:32
  130.5 0.5 reshape.125
  131.1 1.7 copy.23
  132.8 14.4 %all-to-all-done.1 = f32[32,4,16,128]{3,1,2,0:T(4,128)S(1)} async-done(((f32[32,4,16,128]{3,1,2,0:T(4,128)}), f32[32,4,16,128]{3,1,2,0:T(4,128)S(1)}, u32[]{:S(2)}, u32[]{:S(2)}) %all-to-all-start.1) | async-done | bytes 1048608 | tf_op jit(solution)/shard_map/all_to_all | solution.py:334
  147.1 4.7 %all-to-all-start.3 = ((f32[32,4,16,128]{3,1,2,0:T(4,128)}), f32[32,4,16,128]{3,1,2,0:T(4,128)}, u32[]{:S(2)}, u32[]{:S(2)}) async-start(f32[32,4,16,128]{3,1,2,0:T(4,128)} %bitcast.29), calls=%async_computation.3 | async-start | bytes 2097152 | tf_op jit(solution)/shard_map/all_to_all | solution.py:334
  151.8 7.1 %shard_map.71 = f32[2,16,128,256]{3,2,1,0:T(8,128)} custom-call(f32[2,16,128,256]{3,2,1,0:T(8,128)} %get-tuple-element.25.w_ref.w_prev.w_next, f32[2,16,128,256]{3,2,1,0:T(8,128)} %get-tuple-element.25.w_ref.w_prev.w_next, f32[2,16,128,256]{3,2,1,0:T(8,128)} %get-tuple-element.25.w_ref.w_prev.w_next, f32[2,128,256]{2,1,0:T(8,128)} %copy-done.3, ...), custom_call_target="tpu_custom_call" | custom-call | tf_op jit(solution)/shard_map/pallas_call | solution.py:284
  158.9 1.5 fusion.16
  160.4 16.7 %all-to-all-done.3 = f32[32,4,16,128]{3,1,2,0:T(4,128)} async-done(((f32[32,4,16,128]{3,1,2,0:T(4,128)}), f32[32,4,16,128]{3,1,2,0:T(4,128)}, u32[]{:S(2)}, u32[]{:S(2)}) %all-to-all-start.3) | async-done | bytes 1048608 | tf_op jit(solution)/shard_map/all_to_all | solution.py:334
  177.1 4.0 %fusion = f32[16,128,256]{2,1,0:T(8,128)} fusion(f32[16,128,256,1]{2,1,3,0:T(8,128)S(1)} %fusion.16, f32[32,4,16,128]{3,1,2,0:T(4,128)} %all-to-all-done.3, f32[32,2,4,256]{3,0,2,1:T(8,128)S(1)} %sine_add_fusion.1), kind=kOutput, calls=%fused_computation.1 | convolution fusion | flops 403701760 | bytes 5373952 | tf_op jit(solution)/shard_map/sxn,sxyz->yzn/dot_general | solution.py:32
  (23 shorter events, 0.1 us)
Async XLA Ops:
  5.2 15.9 %collective-permute-start = (f32[6,128,256]{2,1,0:T(8,128)}, f32[6,128,256]{2,1,0:T(8,128)S(1)}, u32[]{:S(2)}, u32[]{:S(2)}) collective-permute-start(f32[6,128,256]{2,1,0:T(8,128)} %get-tuple-element.21), channel_id=1, source_target_pairs={{0,2},{2,4},{4,6},{6,8},{8,10},{10,12},{12,14},{14,16},{16,18},{18... | collective-permute-start | bytes 2359304 | tf_op jit(solution)/shard_map/ppermute | solution.py:236
  5.2 15.8 %collective-permute-start.1 = (f32[6,128,256]{2,1,0:T(8,128)}, f32[6,128,256]{2,1,0:T(8,128)S(1)}, u32[]{:S(2)}, u32[]{:S(2)}) collective-permute-start(f32[6,128,256]{2,1,0:T(8,128)} %get-tuple-element.22), channel_id=1, source_target_pairs={{2,0},{4,2},{6,4},{8,6},{10,8},{12,10},{14,12},{16,14},{18,16},{20... | collective-permute-start | bytes 2359304 | tf_op jit(solution)/shard_map/ppermute | solution.py:236
  9.0 11.2 %collective-permute-start.2 = (f32[2,6,16,1,256]{4,3,2,1,0:T(1,128)S(1)}, f32[2,6,16,1,256]{4,3,2,1,0:T(1,128)S(1)}, u32[]{:S(2)}, u32[]{:S(2)}) collective-permute-start(f32[2,6,16,1,256]{4,3,2,1,0:T(1,128)S(1)} %pad_maximum_fusion), channel_id=1, source_target_pairs={{0,1},{1,0},{2,3},{3,2},{4,5},{5,4},{6,7},{7,6},{8,9},{9,8},{10,11... | collective-permute-start | bytes 589832 | tf_op jit(solution)/shard_map/ppermute | solution.py:233
  21.0 1.0 copy-start.1
  21.1 1.2 copy-start.2
  40.2 8.7 %collective-permute-start.5 = (f32[2,2,16,1,256]{4,3,2,1,0:T(1,128)S(1)}, f32[2,2,16,1,256]{4,3,2,1,0:T(1,128)S(1)}, u32[]{:S(2)}, u32[]{:S(2)}) collective-permute-start(f32[2,2,16,1,256]{4,3,2,1,0:T(1,128)S(1)} %pad_maximum_fusion.1), channel_id=1, source_target_pairs={{0,1},{1,0},{2,3},{3,2},{4,5},{5,4},{6,7},{7,6},{8,9},{9,8},{10,11... | collective-permute-start | bytes 196616 | tf_op jit(solution)/shard_map/ppermute | solution.py:233
  40.8 8.7 %collective-permute-start.3 = (f32[2,128,256]{2,1,0:T(8,128)}, f32[2,128,256]{2,1,0:T(8,128)S(1)}, u32[]{:S(2)}, u32[]{:S(2)}) collective-permute-start(f32[2,128,256]{2,1,0:T(8,128)} %get-tuple-element.26), channel_id=1, source_target_pairs={{0,2},{2,4},{4,6},{6,8},{8,10},{10,12},{12,14},{14,16},{16,18},{18... | collective-permute-start | bytes 786440 | tf_op jit(solution)/shard_map/ppermute | solution.py:236
  46.1 4.3 %collective-permute-start.4 = (f32[2,128,256]{2,1,0:T(8,128)}, f32[2,128,256]{2,1,0:T(8,128)S(1)}, u32[]{:S(2)}, u32[]{:S(2)}) collective-permute-start(f32[2,128,256]{2,1,0:T(8,128)} %get-tuple-element.27), channel_id=1, source_target_pairs={{2,0},{4,2},{6,4},{8,6},{10,8},{12,10},{14,12},{16,14},{18,16},{20... | collective-permute-start | bytes 786440 | tf_op jit(solution)/shard_map/ppermute | solution.py:236
  49.5 0.9 copy-start.3
  50.3 0.7 copy-start.4
  51.1 11.1 %copy-start = (f32[16,128,256]{2,1,0:T(8,128)S(1)}, f32[16,128,256]{2,1,0:T(8,128)}, u32[]{:S(2)}) copy-start(f32[16,128,256]{2,1,0:T(8,128)} %get-tuple-element.30) | copy-start | bytes 6291460
  52.6 34.8 %all-to-all-start = ((f32[32,4,16,128]{3,2,1,0:T(8,128)}), f32[32,4,16,128]{3,2,1,0:T(8,128)S(1)}, u32[]{:S(2)}, u32[]{:S(2)}) async-start(f32[32,4,16,128]{3,2,1,0:T(8,128)} %copy.13), calls=%async_computation | async-start | bytes 2097152 | tf_op jit(solution)/shard_map/all_to_all | solution.py:317
  87.4 29.9 %all-to-all-start.2 = ((f32[32,4,16,128]{3,2,1,0:T(8,128)}), f32[32,4,16,128]{3,2,1,0:T(8,128)S(1)}, u32[]{:S(2)}, u32[]{:S(2)}) async-start(f32[32,4,16,128]{3,2,1,0:T(8,128)} %copy.19), calls=%async_computation.2 | async-start | bytes 2097152 | tf_op jit(solution)/shard_map/all_to_all | solution.py:317
  94.5 1.7 copy-start.5
  117.3 29.9 %all-to-all-start.1 = ((f32[32,4,16,128]{3,1,2,0:T(4,128)}), f32[32,4,16,128]{3,1,2,0:T(4,128)S(1)}, u32[]{:S(2)}, u32[]{:S(2)}) async-start(f32[32,4,16,128]{3,1,2,0:T(4,128)} %bitcast.18), calls=%async_computation.1 | async-start | bytes 2097152 | tf_op jit(solution)/shard_map/all_to_all | solution.py:334
  123.6 1.7 copy-start.6
  147.1 30.0 %all-to-all-start.3 = ((f32[32,4,16,128]{3,1,2,0:T(4,128)}), f32[32,4,16,128]{3,1,2,0:T(4,128)}, u32[]{:S(2)}, u32[]{:S(2)}) async-start(f32[32,4,16,128]{3,1,2,0:T(4,128)} %bitcast.29), calls=%async_computation.3 | async-start | bytes 2097152 | tf_op jit(solution)/shard_map/all_to_all | solution.py:334

commit v4 on v3

--- a/solution.py
+++ b/solution.py
@@ -43,10 +43,14 @@
 
 
 def neighbour_planes(cur_ref, prev_ref, next_ref, y_low_ref, y_high_ref, rows, field, comp, r, step, last):
-    below = cur_ref[comp, jnp.maximum(r - 1, 0)]
-    below = jnp.where(r == 0, jnp.where(step == 0, y_low_ref[field], prev_ref[comp, 0]), below)
-    above = cur_ref[comp, jnp.minimum(r + 1, rows - 1)]
-    above = jnp.where(r == rows - 1, jnp.where(step == last, y_high_ref[field], next_ref[comp, 0]), above)
+    if isinstance(r, int) and r == 0:
+        below = jnp.where(step == 0, y_low_ref[field], prev_ref[comp, 0])
+    else:
+        below = cur_ref[comp, r - 1]
+    if isinstance(r, int) and r == rows - 1:
+        above = jnp.where(step == last, y_high_ref[field], next_ref[comp, 0])
+    else:
+        above = cur_ref[comp, r + 1]
     return below, above
 
 
@@ -54,23 +58,27 @@
     for c, value in enumerate(values):
         z_first_ref[c, r] = value[0:1]
         z_last_ref[c, r] = value[value.shape[0] - 1:]
-
-    @pl.when(jnp.logical_and(r == 0, step == 0))
-    def _():
-        for c, value in enumerate(values):
-            y_first_ref[c] = value
-
-    @pl.when(jnp.logical_and(r == rows - 1, step == last))
-    def _():
-        for c, value in enumerate(values):
-            y_last_ref[c] = value
+    if isinstance(r, int) and r == 0:
+        @pl.when(step == 0)
+        def _():
+            for c, value in enumerate(values):
+                y_first_ref[c] = value
+    if isinstance(r, int) and r == rows - 1:
+        @pl.when(step == last)
+        def _():
+            for c, value in enumerate(values):
+                y_last_ref[c] = value
 
 
 def for_rows(rows, body):
-    def loop_body(r, carry):
-        body(r)
-        return carry
-    lax.fori_loop(0, rows, loop_body, 0)
+    body(0)
+    if rows > 2:
+        def loop_body(r, carry):
+            body(r)
+            return carry
+        lax.fori_loop(1, rows - 1, loop_body, 0)
+    if rows > 1:
+        body(rows - 1)
 
 
 def sin_cos(x):

time: 184 us -> 183 us (level)
  no operation moved by 1% of the time
where the time goes in v4:
time: 183 us; the launch traced here: 180 us
  waiting for transfers between devices  68.2 us (37%)
  Pallas kernels  36.1 us (20%)
  starting transfers between devices  33.5 us (18%)
  matrix products  23.2 us (13%)
  local copies, waits for them, and re-layouts  14.3 us (8%)
  other arithmetic  3.93 us (2%)
    all_to_all x2, waiting for transfers between devices, dipole_adjoint(): sent.append(lax.all_to_all(spec, ('gy', 'gz'), 0, 0, tiled=True))  36 us
    all_to_all x2, waiting for transfers between devices, dipole_adjoint(): spec = lax.all_to_all(spec, ('gy', 'gz'), 0, 0, tiled=True)  31.3 us
    dot_general x12, matrix products, along(): return jnp.einsum(spec, table, values, precision=lax.Precision.HIGH)  23.2 us
    pallas_call x1, Pallas kernels, backward_sections(): pl.pallas_call(functools.partial(first_kernel, rows=rows), grid=grid, in_...  16.1 us
    all_to_all x2, starting transfers between devices, dipole_adjoint(): sent.append(lax.all_to_all(spec, ('gy', 'gz'), 0, 0, tiled=True))  14.1 us
    all_to_all x2, starting transfers between devices, dipole_adjoint(): spec = lax.all_to_all(spec, ('gy', 'gz'), 0, 0, tiled=True)  9.27 us
    pallas_call x1, Pallas kernels, backward_sections(): pl.pallas_call(functools.partial(factor_kernel, rows=rows), grid=grid, in...  8.52 us
    pallas_call x1, Pallas kernels, finish_lambda(): pl.pallas_call(functools.partial(second_kernel, rows=rows), grid=grid, in...  6.87 us
  transfers between devices with their start and end apart: 10, of which 5 were waited for; matrix products, arithmetic and copies ran while one was open for 18% of the time, Pallas kernels for 9%

profile of v4, /device:TPU:16, one launch (start us, length us, event | category | flops | bytes accessed | tf_op | source)
XLA Modules:
  0.0 180.2 jit_solution(14789141279675595696)
XLA Ops:
  0.6 4.5 %shard_map.69 = (f32[6,128,256]{2,1,0:T(8,128)}, f32[6,128,256]{2,1,0:T(8,128)}, f32[6,16,1,256]{3,2,1,0:T(1,128)}, f32[6,16,1,256]{3,2,1,0:T(1,128)}) custom-call(f32[2,16,128,256]{3,2,1,0:T(8,128)} %refs_2_.3, f32[2,16,128,256]{3,2,1,0:T(8,128)} %refs_2_.3, f32[2,16,128,256]{3,2,1,0:T(8,128)} %refs_2_.3, f32[2,16,128,256]{3,2,1,0:T(8,128)} %refs_2_.3, ...), custom_call_target="tpu_custom_call" | custom-call | tf_op jit(solution)/shard_map/pallas_call | solution.py:261
  5.2 2.6 %collective-permute-start.1 = (f32[6,128,256]{2,1,0:T(8,128)}, f32[6,128,256]{2,1,0:T(8,128)S(1)}, u32[]{:S(2)}, u32[]{:S(2)}) collective-permute-start(f32[6,128,256]{2,1,0:T(8,128)} %get-tuple-element.22), channel_id=1, source_target_pairs={{2,0},{4,2},{6,4},{8,6},{10,8},{12,10},{14,12},{16,14},{18,16},{20... | collective-permute-start | bytes 2359304 | tf_op jit(solution)/shard_map/ppermute | solution.py:244
  7.9 1.1 pad_maximum_fusion
  9.0 1.6 collective-permute-start.2
  10.6 8.5 %shard_map.68 = (f32[2,16,128,256]{3,2,1,0:T(8,128)}, f32[2,16,128,256]{3,2,1,0:T(8,128)}) custom-call(f32[2,16,128,256]{3,2,1,0:T(8,128)} %refs_11_.1, f32[16,128,256]{2,1,0:T(8,128)} %refs_15_.1, s32[16,128,256]{2,1,0:T(8,128)} %refs_19_.1), custom_call_target="tpu_custom_call" | custom-call | tf_op jit(solution)/shard_map/pallas_call | solution.py:269
  19.1 1.1 sine_add_fusion.1
  20.2 0.8 slice_bitcast_fusion
  21.1 1.0 copy-done.1
  22.0 0.2 copy-done.2
  22.2 16.1 %shard_map.70 = (f32[16,128,256]{2,1,0:T(8,128)}, f32[2,16,128,256]{3,2,1,0:T(8,128)}, f32[2,128,256]{2,1,0:T(8,128)}, f32[2,128,256]{2,1,0:T(8,128)}, f32[2,16,...) custom-call(f32[2,16,128,256]{3,2,1,0:T(8,128)} %refs_2_.3, f32[2,16,128,256]{3,2,1,0:T(8,128)} %refs_2_.3, ...), custom_call_target="tpu_custom_call" | custom-call | tf_op jit(solution)/shard_map/pallas_call | solution.py:276
  38.4 0.8 pad_maximum_fusion.1
  39.2 0.6 collective-permute-start.5
  39.8 5.3 %collective-permute-start.3 = (f32[2,128,256]{2,1,0:T(8,128)}, f32[2,128,256]{2,1,0:T(8,128)S(1)}, u32[]{:S(2)}, u32[]{:S(2)}) collective-permute-start(f32[2,128,256]{2,1,0:T(8,128)} %get-tuple-element.26), channel_id=1, source_target_pairs={{0,2},{2,4},{4,6},{6,8},{8,10},{10,12},{12,14},{14,16},{16,18},{18... | collective-permute-start | bytes 786440 | tf_op jit(solution)/shard_map/ppermute | solution.py:244
  45.1 2.8 %fusion.3 = f32[32,4,16,128]{3,0,2,1:T(8,128)S(1)} fusion(f32[16,128,256]{2,1,0:T(8,128)} %get-tuple-element.30, f32[32,2,4,256]{3,0,2,1:T(8,128)S(1)} %sine_add_fusion.1), kind=kOutput, calls=%fused_computation.4 | convolution fusion | flops 402653184 | bytes 3276800 | tf_op jit(solution)/shard_map/sxn,yzn->sxyz/dot_general | solution.py:32
  47.9 0.6 slice_bitcast_fusion.2
  48.5 0.9 collective-permute-done.4.y_high_ref
  49.4 0.7 copy-done.4
  50.1 1.6 copy.13
  51.7 9.5 %all-to-all-start = ((f32[32,4,16,128]{3,2,1,0:T(8,128)}), f32[32,4,16,128]{3,2,1,0:T(8,128)S(1)}, u32[]{:S(2)}, u32[]{:S(2)}) async-start(f32[32,4,16,128]{3,2,1,0:T(8,128)} %copy.13), calls=%async_computation | async-start | bytes 2097152 | tf_op jit(solution)/shard_map/all_to_all | solution.py:325
  61.2 1.2 fusion.1
  62.4 1.6 copy.19
  64.0 22.5 %all-to-all-done = f32[32,4,16,128]{3,2,1,0:T(8,128)S(1)} async-done(((f32[32,4,16,128]{3,2,1,0:T(8,128)}), f32[32,4,16,128]{3,2,1,0:T(8,128)S(1)}, u32[]{:S(2)}, u32[]{:S(2)}) %all-to-all-start) | async-done | bytes 1048608 | tf_op jit(solution)/shard_map/all_to_all | solution.py:325
  86.5 4.6 %all-to-all-start.2 = ((f32[32,4,16,128]{3,2,1,0:T(8,128)}), f32[32,4,16,128]{3,2,1,0:T(8,128)S(1)}, u32[]{:S(2)}, u32[]{:S(2)}) async-start(f32[32,4,16,128]{3,2,1,0:T(8,128)} %copy.19), calls=%async_computation.2 | async-start | bytes 2097152 | tf_op jit(solution)/shard_map/all_to_all | solution.py:325
  91.1 0.8 broadcast_add_fusion
  91.9 0.8 copy.40
  92.7 0.8 reshape.120
  93.6 1.6 fusion.34
  95.3 1.8 fusion.5
  97.0 1.6 convolution_bitcast_fusion.2
  98.7 1.9 %fusion.30 = f32[4,256,256]{2,1,0:T(8,128)S(1)} fusion(f32[4,256,256]{1,2,0:T(8,128)S(1)} %convolution_bitcast_fusion.2), kind=kOutput, calls=%fused_computation.47 | convolution fusion | flops 403636224 | bytes 2097152 | tf_op jit(solution)/shard_map/kz,xyz->xyk/dot_general | solution.py:32
  100.6 0.5 reshape.121
  101.1 1.7 copy.17
  102.8 13.5 %all-to-all-done.2 = f32[32,4,16,128]{3,2,1,0:T(8,128)S(1)} async-done(((f32[32,4,16,128]{3,2,1,0:T(8,128)}), f32[32,4,16,128]{3,2,1,0:T(8,128)S(1)}, u32[]{:S(2)}, u32[]{:S(2)}) %all-to-all-start.2) | async-done | bytes 1048608 | tf_op jit(solution)/shard_map/all_to_all | solution.py:325
  116.3 4.6 %all-to-all-start.1 = ((f32[32,4,16,128]{3,1,2,0:T(4,128)}), f32[32,4,16,128]{3,1,2,0:T(4,128)S(1)}, u32[]{:S(2)}, u32[]{:S(2)}) async-start(f32[32,4,16,128]{3,1,2,0:T(4,128)} %bitcast.18), calls=%async_computation.1 | async-start | bytes 2097152 | tf_op jit(solution)/shard_map/all_to_all | solution.py:342
  121.0 0.8 copy.39
  121.8 0.8 reshape.124
  122.6 1.6 fusion.28
  124.3 1.8 fusion.6
  126.1 1.6 convolution_bitcast_fusion
  127.7 1.9 %fusion.24 = f32[4,256,256]{2,1,0:T(8,128)S(1)} fusion(f32[4,256,256]{1,2,0:T(8,128)S(1)} %convolution_bitcast_fusion), kind=kOutput, calls=%fused_computation.41 | convolution fusion | flops 403636224 | bytes 2097152 | tf_op jit(solution)/shard_map/kz,xyz->xyk/dot_general | solution.py:32
  129.6 0.5 reshape.125
  130.1 1.7 copy.23
  131.8 14.4 %all-to-all-done.1 = f32[32,4,16,128]{3,1,2,0:T(4,128)S(1)} async-done(((f32[32,4,16,128]{3,1,2,0:T(4,128)}), f32[32,4,16,128]{3,1,2,0:T(4,128)S(1)}, u32[]{:S(2)}, u32[]{:S(2)}) %all-to-all-start.1) | async-done | bytes 1048608 | tf_op jit(solution)/shard_map/all_to_all | solution.py:342
  146.2 4.7 %all-to-all-start.3 = ((f32[32,4,16,128]{3,1,2,0:T(4,128)}), f32[32,4,16,128]{3,1,2,0:T(4,128)}, u32[]{:S(2)}, u32[]{:S(2)}) async-start(f32[32,4,16,128]{3,1,2,0:T(4,128)} %bitcast.29), calls=%async_computation.3 | async-start | bytes 2097152 | tf_op jit(solution)/shard_map/all_to_all | solution.py:342
  150.9 6.9 %shard_map.71 = f32[2,16,128,256]{3,2,1,0:T(8,128)} custom-call(f32[2,16,128,256]{3,2,1,0:T(8,128)} %get-tuple-element.25.w_ref.w_prev.w_next, f32[2,16,128,256]{3,2,1,0:T(8,128)} %get-tuple-element.25.w_ref.w_prev.w_next, f32[2,16,128,256]{3,2,1,0:T(8,128)} %get-tuple-element.25.w_ref.w_prev.w_next, f32[2,128,256]{2,1,0:T(8,128)} %copy-done.3, ...), custom_call_target="tpu_custom_call" | custom-call | tf_op jit(solution)/shard_map/pallas_call | solution.py:292
  157.7 1.5 fusion.16
  159.2 17.0 %all-to-all-done.3 = f32[32,4,16,128]{3,1,2,0:T(4,128)} async-done(((f32[32,4,16,128]{3,1,2,0:T(4,128)}), f32[32,4,16,128]{3,1,2,0:T(4,128)}, u32[]{:S(2)}, u32[]{:S(2)}) %all-to-all-start.3) | async-done | bytes 1048608 | tf_op jit(solution)/shard_map/all_to_all | solution.py:342
  176.2 4.0 %fusion = f32[16,128,256]{2,1,0:T(8,128)} fusion(f32[16,128,256,1]{2,1,3,0:T(8,128)S(1)} %fusion.16, f32[32,4,16,128]{3,1,2,0:T(4,128)} %all-to-all-done.3, f32[32,2,4,256]{3,0,2,1:T(8,128)S(1)} %sine_add_fusion.1), kind=kOutput, calls=%fused_computation.1 | convolution fusion | flops 403701760 | bytes 5373952 | tf_op jit(solution)/shard_map/sxn,sxyz->yzn/dot_general | solution.py:32
  (23 shorter events, 0.1 us)
Async XLA Ops:
  5.2 15.9 %collective-permute-start = (f32[6,128,256]{2,1,0:T(8,128)}, f32[6,128,256]{2,1,0:T(8,128)S(1)}, u32[]{:S(2)}, u32[]{:S(2)}) collective-permute-start(f32[6,128,256]{2,1,0:T(8,128)} %get-tuple-element.21), channel_id=1, source_target_pairs={{0,2},{2,4},{4,6},{6,8},{8,10},{10,12},{12,14},{14,16},{16,18},{18... | collective-permute-start | bytes 2359304 | tf_op jit(solution)/shard_map/ppermute | solution.py:244
  5.2 15.8 %collective-permute-start.1 = (f32[6,128,256]{2,1,0:T(8,128)}, f32[6,128,256]{2,1,0:T(8,128)S(1)}, u32[]{:S(2)}, u32[]{:S(2)}) collective-permute-start(f32[6,128,256]{2,1,0:T(8,128)} %get-tuple-element.22), channel_id=1, source_target_pairs={{2,0},{4,2},{6,4},{8,6},{10,8},{12,10},{14,12},{16,14},{18,16},{20... | collective-permute-start | bytes 2359304 | tf_op jit(solution)/shard_map/ppermute | solution.py:244
  9.0 11.2 %collective-permute-start.2 = (f32[2,6,16,1,256]{4,3,2,1,0:T(1,128)S(1)}, f32[2,6,16,1,256]{4,3,2,1,0:T(1,128)S(1)}, u32[]{:S(2)}, u32[]{:S(2)}) collective-permute-start(f32[2,6,16,1,256]{4,3,2,1,0:T(1,128)S(1)} %pad_maximum_fusion), channel_id=1, source_target_pairs={{0,1},{1,0},{2,3},{3,2},{4,5},{5,4},{6,7},{7,6},{8,9},{9,8},{10,11... | collective-permute-start | bytes 589832 | tf_op jit(solution)/shard_map/ppermute | solution.py:241
  21.0 1.0 copy-start.1
  21.1 1.2 copy-start.2
  39.2 8.7 %collective-permute-start.5 = (f32[2,2,16,1,256]{4,3,2,1,0:T(1,128)S(1)}, f32[2,2,16,1,256]{4,3,2,1,0:T(1,128)S(1)}, u32[]{:S(2)}, u32[]{:S(2)}) collective-permute-start(f32[2,2,16,1,256]{4,3,2,1,0:T(1,128)S(1)} %pad_maximum_fusion.1), channel_id=1, source_target_pairs={{0,1},{1,0},{2,3},{3,2},{4,5},{5,4},{6,7},{7,6},{8,9},{9,8},{10,11... | collective-permute-start | bytes 196616 | tf_op jit(solution)/shard_map/ppermute | solution.py:241
  39.8 8.7 %collective-permute-start.3 = (f32[2,128,256]{2,1,0:T(8,128)}, f32[2,128,256]{2,1,0:T(8,128)S(1)}, u32[]{:S(2)}, u32[]{:S(2)}) collective-permute-start(f32[2,128,256]{2,1,0:T(8,128)} %get-tuple-element.26), channel_id=1, source_target_pairs={{0,2},{2,4},{4,6},{6,8},{8,10},{10,12},{12,14},{14,16},{16,18},{18... | collective-permute-start | bytes 786440 | tf_op jit(solution)/shard_map/ppermute | solution.py:244
  45.1 4.3 %collective-permute-start.4 = (f32[2,128,256]{2,1,0:T(8,128)}, f32[2,128,256]{2,1,0:T(8,128)S(1)}, u32[]{:S(2)}, u32[]{:S(2)}) collective-permute-start(f32[2,128,256]{2,1,0:T(8,128)} %get-tuple-element.27), channel_id=1, source_target_pairs={{2,0},{4,2},{6,4},{8,6},{10,8},{12,10},{14,12},{16,14},{18,16},{20... | collective-permute-start | bytes 786440 | tf_op jit(solution)/shard_map/ppermute | solution.py:244
  48.5 0.9 copy-start.3
  49.4 0.7 copy-start.4
  50.1 11.1 %copy-start = (f32[16,128,256]{2,1,0:T(8,128)S(1)}, f32[16,128,256]{2,1,0:T(8,128)}, u32[]{:S(2)}) copy-start(f32[16,128,256]{2,1,0:T(8,128)} %get-tuple-element.30) | copy-start | bytes 6291460
  51.7 34.8 %all-to-all-start = ((f32[32,4,16,128]{3,2,1,0:T(8,128)}), f32[32,4,16,128]{3,2,1,0:T(8,128)S(1)}, u32[]{:S(2)}, u32[]{:S(2)}) async-start(f32[32,4,16,128]{3,2,1,0:T(8,128)} %copy.13), calls=%async_computation | async-start | bytes 2097152 | tf_op jit(solution)/shard_map/all_to_all | solution.py:325
  86.5 29.9 %all-to-all-start.2 = ((f32[32,4,16,128]{3,2,1,0:T(8,128)}), f32[32,4,16,128]{3,2,1,0:T(8,128)S(1)}, u32[]{:S(2)}, u32[]{:S(2)}) async-start(f32[32,4,16,128]{3,2,1,0:T(8,128)} %copy.19), calls=%async_computation.2 | async-start | bytes 2097152 | tf_op jit(solution)/shard_map/all_to_all | solution.py:325
  93.6 1.7 copy-start.5
  116.3 29.9 %all-to-all-start.1 = ((f32[32,4,16,128]{3,1,2,0:T(4,128)}), f32[32,4,16,128]{3,1,2,0:T(4,128)S(1)}, u32[]{:S(2)}, u32[]{:S(2)}) async-start(f32[32,4,16,128]{3,1,2,0:T(4,128)} %bitcast.18), calls=%async_computation.1 | async-start | bytes 2097152 | tf_op jit(solution)/shard_map/all_to_all | solution.py:342
  122.6 1.7 copy-start.6
  146.2 30.0 %all-to-all-start.3 = ((f32[32,4,16,128]{3,1,2,0:T(4,128)}), f32[32,4,16,128]{3,1,2,0:T(4,128)}, u32[]{:S(2)}, u32[]{:S(2)}) async-start(f32[32,4,16,128]{3,1,2,0:T(4,128)} %bitcast.29), calls=%async_computation.3 | async-start | bytes 2097152 | tf_op jit(solution)/shard_map/all_to_all | solution.py:342

commit v5 on v4

--- a/solution.py
+++ b/solution.py
@@ -167,11 +167,10 @@
     return [plane, plane, row, row], [plane_spec, plane_spec, row_spec, row_spec]
 
 
-def first_kernel(*refs, rows):
+def first_kernel(*refs, rows, base, last):
     (mm_ref, mm_prev, mm_next, ms_ref, ms_prev, ms_next, w_ref, w_prev, w_next,
      factor_ref, y_low_ref, y_high_ref, z_low_ref, z_high_ref, pg_ref, w2_ref) = refs[:16]
-    step = pl.program_id(0)
-    last = pl.num_programs(0) - 1
+    step = pl.program_id(0) + base
     fields = ((mm_ref, mm_prev, mm_next), (ms_ref, ms_prev, ms_next), (w_ref, w_prev, w_next))
 
     def body(r):
@@ -221,13 +220,13 @@
     return rows
 
 
-def field_specs(shape, rows):
+def field_specs(shape, rows, base=0):
     comps, length_y, length_z, length_x = shape
-    cur = pl.BlockSpec((comps, rows, length_z, length_x), lambda i: (0, i, 0, 0))
+    cur = pl.BlockSpec((comps, rows, length_z, length_x), lambda i: (0, i + base, 0, 0))
     prev = pl.BlockSpec((comps, 1, length_z, length_x),
-                        lambda i: (0, jnp.maximum(i * rows - 1, 0), 0, 0))
+                        lambda i: (0, jnp.maximum((i + base) * rows - 1, 0), 0, 0))
     nxt = pl.BlockSpec((comps, 1, length_z, length_x),
-                       lambda i: (0, jnp.minimum(i * rows + rows, length_y - 1), 0, 0))
+                       lambda i: (0, jnp.minimum((i + base) * rows + rows, length_y - 1), 0, 0))
     return [cur, prev, nxt]
 
 
@@ -273,18 +272,38 @@
         out_specs=[cur, cur],
         out_shape=[pair, pair],
     )(adjoint_end, phase, labels)
-    phase_grad, w_second, *w2_edges = pl.pallas_call(
-        functools.partial(first_kernel, rows=rows),
-        grid=grid,
-        in_specs=field_specs(mag_middle.shape, rows) + field_specs(mag_start.shape, rows)
-        + field_specs(w_first.shape, rows)
-        + [cur, whole((6, length_z, length_x)), whole((6, length_z, length_x)), zspec(6), zspec(6)],
-        out_specs=[cur_plane, cur] + edge_specs,
-        out_shape=[plane, pair] + edge_shapes,
-    )(mag_middle, mag_middle, mag_middle, mag_start, mag_start, mag_start,
-      w_first, w_first, w_first, factor, *halos)
+    blocks = length_y // rows
+    halves = 2 if blocks % 2 == 0 else 1
+    half_blocks = blocks // halves
+    half_y = half_blocks * rows
+    half_edge_shapes, half_edge_specs = edge_outputs(2, half_y, length_z, length_x, rows)
+    grads, seconds, y_firsts, y_lasts, z_firsts, z_lasts = [], [], [], [], [], []
+    for h in range(halves):
+        base = h * half_blocks
+        grad, second, y_first, y_last, z_first, z_last = pl.pallas_call(
+            functools.partial(first_kernel, rows=rows, base=base, last=blocks - 1),
+            grid=(half_blocks,),
+            in_specs=field_specs(mag_middle.shape, rows, base) + field_specs(mag_start.shape, rows, base)
+            + field_specs(w_first.shape, rows, base)
+            + [pl.BlockSpec((2, rows, length_z, length_x), lambda i, b=base: (0, i + b, 0, 0)),
+               whole((6, length_z, length_x)), whole((6, length_z, length_x)),
+               pl.BlockSpec((6, rows, 1, length_x), lambda i, b=base: (0, i + b, 0, 0)),
+               pl.BlockSpec((6, rows, 1, length_x), lambda i, b=base: (0, i + b, 0, 0))],
+            out_specs=[cur_plane, cur] + half_edge_specs,
+            out_shape=[jax.ShapeDtypeStruct((half_y, length_z, length_x), jnp.float32),
+                       jax.ShapeDtypeStruct((2, half_y, length_z, length_x), jnp.float32)] + half_edge_shapes,
+        )(mag_middle, mag_middle, mag_middle, mag_start, mag_start, mag_start,
+          w_first, w_first, w_first, factor, *halos)
+        grads.append(grad)
+        seconds.append(second)
+        y_firsts.append(y_first)
+        y_lasts.append(y_last)
+        z_firsts.append(z_first)
+        z_lasts.append(z_last)
+    w_second = jnp.concatenate(seconds, axis=1) if halves > 1 else seconds[0]
+    w2_edges = [y_firsts[0], y_lasts[-1], jnp.concatenate(z_firsts, axis=1), jnp.concatenate(z_lasts, axis=1)]
     halos = send_edges(*w2_edges)
-    return phase_grad, functools.partial(finish_lambda, w_second, rows, grid, cur, whole, zspec, length_z, length_x), halos
+    return grads, functools.partial(finish_lambda, w_second, rows, grid, cur, whole, zspec, length_z, length_x), halos
 
 
 def finish_lambda(w_second, rows, grid, cur, whole, zspec, length_z, length_x, halos):
@@ -300,17 +319,20 @@
     return lam
 
 
-def dipole_adjoint(phase_grad, finish, halos):
+def dipole_adjoint(grads, finish, halos):
     count_y = lax.axis_size("gy")
     count_z = lax.axis_size("gz")
     parts = count_y * count_z
-    block_y, block_z, length_x = phase_grad.shape
+    halves = len(grads)
+    half_y, block_z, length_x = grads[0].shape
+    block_y = half_y * halves
     length_y = block_y * count_y
     length_z = block_z * count_z
     block_x = length_x // parts
     pieces = 2 if block_x % 2 == 0 else 1
     piece_x = block_x // pieces
-    table_x = cas_table(length_x).reshape(parts, pieces, piece_x, length_x)
+    table = cas_table(length_x)
+    table_x = table.reshape(parts, pieces, piece_x, length_x)
     table_y = cas_table(length_y)
     table_z = cas_table(length_z)
     scale = 1.0 / (float(length_y) * float(length_z) * float(length_x))
@@ -318,17 +340,17 @@
     freq_z = signed_freq(jnp.arange(length_z, dtype=jnp.int32), length_z)
     index = lax.axis_index("gy") * count_z + lax.axis_index("gz")
     sent = []
-    for p in range(pieces):
-        spec = along("sxn,yzn->sxyz", table_x[:, p], phase_grad)
-        if p == 0:
+    for h in range(halves):
+        spec = along("kn,yzn->kyz", table, grads[h]).reshape(parts, block_x, half_y, block_z)
+        if h == halves - 1:
             halos, spec = lax.optimization_barrier((halos, spec))
         sent.append(lax.all_to_all(spec, ("gy", "gz"), 0, 0, tiled=True))
-        if p == 0:
-            lam = finish(halos)
+    lam = finish(halos)
+    spec = jnp.stack(sent).reshape(halves, count_y, count_z, block_x, half_y, block_z)
+    whole_spec = spec.transpose(3, 1, 0, 4, 2, 5).reshape(block_x, length_y, length_z)
     result = None
     for p in range(pieces):
-        spec = sent[p].reshape(count_y, count_z, piece_x, block_y, block_z)
-        spec = spec.transpose(2, 0, 3, 1, 4).reshape(piece_x, length_y, length_z)
+        spec = whole_spec[p * piece_x:(p + 1) * piece_x]
         spec = along("kz,xyz->xyk", table_z, spec)
         spec = along("ky,xyz->xkz", table_y, spec)
         first_x = index * block_x + p * piece_x
@@ -346,8 +368,8 @@
 
 
 def per_device(mag_start, mag_middle, adjoint_end, phase, labels):
-    phase_grad, finish, halos = backward_sections(mag_start, mag_middle, adjoint_end, phase, labels)
-    chi_grad, lam = dipole_adjoint(phase_grad, finish, halos)
+    grads, finish, halos = backward_sections(mag_start, mag_middle, adjoint_end, phase, labels)
+    chi_grad, lam = dipole_adjoint(grads, finish, halos)
     return (lam, chi_grad)
 
 

time: 183 us -> 184 us (level)
  Pallas kernels: 36.1 us -> 42 us
  waiting for transfers between devices: 68.2 us -> 62.7 us
  other arithmetic: 3.93 us -> 7.42 us
  local copies, waits for them, and re-layouts: 14.3 us -> 11.6 us
  starting transfers between devices: 33.5 us -> 31.1 us
    all_to_all x2, waiting for transfers between devices: 36 us -> 24.9 us  [dipole_adjoint(): sent.append(lax.all_to_all(spec, ('gy', 'gz'), 0, 0, tiled=True))]
    ppermute x2, waiting for transfers between devices: 0.86 us -> 7.77 us  [send_edges(): lax.ppermute(first, axis, down)]
    pallas_call x1 -> x2, Pallas kernels: 16.1 us -> 22.2 us  [backward_sections(): pl.pallas_call(functools.partial(first_kernel, rows=rows, base=base, last...]
    ppermute x2, starting transfers between devices: 5.38 us -> 0.06 us  [send_edges(): lax.ppermute(last, axis, up)]
    concatenate x0 -> x1, other arithmetic: none -> 4.04 us  [backward_sections(): w_second = jnp.concatenate(seconds, axis=1) if halves > 1 else seconds[0]]
    all_to_all x2, waiting for transfers between devices: 31.3 us -> 27.9 us  [dipole_adjoint(): spec = lax.all_to_all(spec, ('gy', 'gz'), 0, 0, tiled=True)]
    reshape x4 -> x1, local copies, waits for them, and re-layouts: 3.3 us -> 1.09 us  [dipole_adjoint(): along('kn,yzn->kyz', table, grads[h])]
    ppermute x2, waiting for transfers between devices: 0.01 us -> 2.11 us  [send_edges(): lax.ppermute(last, axis, up)]
  transfers between devices with their start and end apart: 10 -> 10, of which waited for: 5 -> 5; matrix products, arithmetic and copies ran while one was open for 18% -> 13% of each run, Pallas kernels for 9% -> 15%
where the time goes in v5:
time: 184 us; the launch traced here: 181 us
  waiting for transfers between devices  62.7 us (34%)
  Pallas kernels  42 us (23%)
  starting transfers between devices  31.1 us (17%)
  matrix products  25 us (14%)
  local copies, waits for them, and re-layouts  11.6 us (6%)
  other arithmetic  7.42 us (4%)
    all_to_all x2, waiting for transfers between devices, dipole_adjoint(): spec = lax.all_to_all(spec, ('gy', 'gz'), 0, 0, tiled=True)  27.9 us
    dot_general x12, matrix products, along(): return jnp.einsum(spec, table, values, precision=lax.Precision.HIGH)  25 us
    all_to_all x2, waiting for transfers between devices, dipole_adjoint(): sent.append(lax.all_to_all(spec, ('gy', 'gz'), 0, 0, tiled=True))  24.9 us
    pallas_call x2, Pallas kernels, backward_sections(): pl.pallas_call(functools.partial(first_kernel, rows=rows, base=base, last...  22.2 us
    all_to_all x2, starting transfers between devices, dipole_adjoint(): sent.append(lax.all_to_all(spec, ('gy', 'gz'), 0, 0, tiled=True))  15.1 us
    all_to_all x2, starting transfers between devices, dipole_adjoint(): spec = lax.all_to_all(spec, ('gy', 'gz'), 0, 0, tiled=True)  9.25 us
    pallas_call x1, Pallas kernels, backward_sections(): pl.pallas_call(functools.partial(factor_kernel, rows=rows), grid=grid, in...  8.44 us
    ppermute x2, waiting for transfers between devices, send_edges(): lax.ppermute(first, axis, down)  7.77 us
  transfers between devices with their start and end apart: 10, of which 5 were waited for; matrix products, arithmetic and copies ran while one was open for 13% of the time, Pallas kernels for 15%

profile of v5, /device:TPU:16, one launch (start us, length us, event | category | flops | bytes accessed | tf_op | source)
XLA Modules:
  0.0 180.8 jit_solution(1601975964086940970)
XLA Ops:
  0.6 4.5 %shard_map.69 = (f32[6,128,256]{2,1,0:T(8,128)}, f32[6,128,256]{2,1,0:T(8,128)}, f32[6,16,1,256]{3,2,1,0:T(1,128)}, f32[6,16,1,256]{3,2,1,0:T(1,128)}) custom-call(f32[2,16,128,256]{3,2,1,0:T(8,128)} %refs_2_.5, f32[2,16,128,256]{3,2,1,0:T(8,128)} %refs_2_.5, f32[2,16,128,256]{3,2,1,0:T(8,128)} %refs_2_.5, f32[2,16,128,256]{3,2,1,0:T(8,128)} %refs_2_.5, ...), custom_call_target="tpu_custom_call" | custom-call | tf_op jit(solution)/shard_map/pallas_call | solution.py:260
  5.2 2.6 %collective-permute-start.1 = (f32[6,128,256]{2,1,0:T(8,128)}, f32[6,128,256]{2,1,0:T(8,128)S(1)}, u32[]{:S(2)}, u32[]{:S(2)}) collective-permute-start(f32[6,128,256]{2,1,0:T(8,128)} %get-tuple-element.26), channel_id=1, source_target_pairs={{2,0},{4,2},{6,4},{8,6},{10,8},{12,10},{14,12},{16,14},{18,16},{20... | collective-permute-start | bytes 2359304 | tf_op jit(solution)/shard_map/ppermute | solution.py:243
  7.9 1.1 pad_maximum_fusion.1
  9.0 1.6 collective-permute-start.2
  10.6 8.4 %shard_map.68 = (f32[2,16,128,256]{3,2,1,0:T(8,128)}, f32[2,16,128,256]{3,2,1,0:T(8,128)}) custom-call(f32[2,16,128,256]{3,2,1,0:T(8,128)} %refs_11_.1, f32[16,128,256]{2,1,0:T(8,128)} %refs_15_.1, s32[16,128,256]{2,1,0:T(8,128)} %refs_19_.1), custom_call_target="tpu_custom_call" | custom-call | tf_op jit(solution)/shard_map/pallas_call | solution.py:268
  19.0 0.8 slice_bitcast_fusion.4
  19.9 1.0 copy-done.1
  20.8 0.2 copy-done.2
  21.1 11.0 %shard_map.70 = (f32[8,128,256]{2,1,0:T(8,128)}, f32[2,8,128,256]{3,2,1,0:T(8,128)}, f32[2,128,256]{2,1,0:T(8,128)}, f32[2,128,256]{2,1,0:T(8,128)}, f32[2,8,1,256]{3,2,1,0:T(1,128)}, /*index=5*/f32[2,8,1,256]{3,2,1,0:T(1,128)}) custom-call(f32[2,16,128,256]{3,2,1,0:T(8,128)} %refs_2_.5, f32[2,16,128,256]{3,2,1,0:T(8,128)} %refs_2_.5, ...), custom_call_target="tpu_custom_call" | custom-call | tf_op jit(solution)/shard_map/pallas_call | solution.py:283
  32.0 2.9 %convolution_bitcast_fusion.4 = f32[32,8,8,128]{3,1,0,2:T(8,128)S(1)} fusion(f32[8,128,256]{2,1,0:T(8,128)} %get-tuple-element.42), kind=kOutput, calls=%fused_computation.12 | convolution fusion | flops 403636224 | bytes 2097152 | tf_op jit(solution)/shard_map/kn,yzn->kyz/dot_general | solution.py:32
  34.9 1.1 copy.13
  36.0 11.4 %all-to-all-start = ((f32[32,8,8,128]{3,1,2,0:T(8,128)}), f32[32,8,8,128]{3,1,2,0:T(8,128)S(1)}, u32[]{:S(2)}, u32[]{:S(2)}) async-start(f32[32,8,8,128]{3,1,2,0:T(8,128)} %copy.13), calls=%async_computation | async-start | bytes 2097152 | tf_op jit(solution)/shard_map/all_to_all | solution.py:347
  47.4 11.2 %shard_map.71 = (f32[8,128,256]{2,1,0:T(8,128)}, f32[2,8,128,256]{3,2,1,0:T(8,128)}, f32[2,128,256]{2,1,0:T(8,128)}, f32[2,128,256]{2,1,0:T(8,128)}, f32[2,8,1,256]{3,2,1,0:T(1,128)}, /*index=5*/f32[2,8,1,256]{3,2,1,0:T(1,128)}) custom-call(f32[2,16,128,256]{3,2,1,0:T(8,128)} %refs_2_.5, f32[2,16,128,256]{3,2,1,0:T(8,128)} %refs_2_.5, ...), custom_call_target="tpu_custom_call" | custom-call | tf_op jit(solution)/shard_map/pallas_call | solution.py:283
  58.7 0.8 maximum_bitcast_fusion.1
  59.5 1.5 collective-permute-start.5
  61.1 0.9 collective-permute-start.4
  62.0 2.9 %convolution_bitcast_fusion.5 = f32[32,8,8,128]{3,1,0,2:T(8,128)S(1)} fusion(f32[8,128,256]{2,1,0:T(8,128)} %get-tuple-element.37), kind=kOutput, calls=%fused_computation.13 | convolution fusion | flops 403636224 | bytes 2097152 | tf_op jit(solution)/shard_map/kn,yzn->kyz/dot_general | solution.py:32
  64.9 0.6 slice_bitcast_fusion.6
  65.5 7.8 %collective-permute-done.4.y_high_ref = f32[2,128,256]{2,1,0:T(8,128)S(1)} collective-permute-done((f32[2,128,256]{2,1,0:T(8,128)S(1)}, f32[2,128,256]{2,1,0:T(8,128)S(1)}, u32[]{:S(2)}, u32[]{:S(2)}) %collective-permute-start.4) | collective-permute-done | bytes 262176 | tf_op jit(solution)/shard_map/ppermute | solution.py:243
  73.3 2.1 %collective-permute-done.3.y_low_ref = f32[2,128,256]{2,1,0:T(8,128)S(1)} collective-permute-done((f32[2,128,256]{2,1,0:T(8,128)}, f32[2,128,256]{2,1,0:T(8,128)S(1)}, u32[]{:S(2)}, u32[]{:S(2)}) %collective-permute-start.3) | collective-permute-done | bytes 262176 | tf_op jit(solution)/shard_map/ppermute | solution.py:243
  75.4 0.7 copy-done.5
  76.1 1.1 copy.15
  77.2 3.7 %all-to-all-start.1 = ((f32[32,8,8,128]{3,1,2,0:T(8,128)}), f32[32,8,8,128]{3,1,2,0:T(8,128)S(1)}, u32[]{:S(2)}, u32[]{:S(2)}) async-start(f32[32,8,8,128]{3,1,2,0:T(8,128)} %copy.15), calls=%async_computation.1 | async-start | bytes 2097152 | tf_op jit(solution)/shard_map/all_to_all | solution.py:347
  81.1 0.2 copy.14
  81.4 24.9 %all-to-all-done.1 = f32[32,8,8,128]{3,1,2,0:T(8,128)S(1)} async-done(((f32[32,8,8,128]{3,1,2,0:T(8,128)}), f32[32,8,8,128]{3,1,2,0:T(8,128)S(1)}, u32[]{:S(2)}, u32[]{:S(2)}) %all-to-all-start.1) | async-done | bytes 1048608 | tf_op jit(solution)/shard_map/all_to_all | solution.py:347
  106.2 0.2 copy.16
  106.6 1.2 fusion.84
  107.8 1.6 fusion.30
  109.4 1.8 fusion.1
  111.2 1.6 convolution_bitcast_fusion.2
  112.8 1.9 %fusion.26 = f32[4,256,256]{2,1,0:T(8,128)S(1)} fusion(f32[4,256,256]{1,2,0:T(8,128)S(1)} %convolution_bitcast_fusion.2), kind=kOutput, calls=%fused_computation.45 | convolution fusion | flops 403636224 | bytes 2097152 | tf_op jit(solution)/shard_map/kz,xyz->xyk/dot_general | solution.py:32
  114.7 0.5 reshape.123
  115.3 1.7 copy.19
  117.0 4.6 %all-to-all-start.2 = ((f32[32,4,16,128]{3,1,2,0:T(4,128)}), f32[32,4,16,128]{3,1,2,0:T(4,128)S(1)}, u32[]{:S(2)}, u32[]{:S(2)}) async-start(f32[32,4,16,128]{3,1,2,0:T(4,128)} %bitcast.18), calls=%async_computation.2 | async-start | bytes 2097152 | tf_op jit(solution)/shard_map/all_to_all | solution.py:364
  121.6 1.6 fusion.24
  123.2 1.8 fusion.2
  125.0 1.6 convolution_bitcast_fusion
  126.7 1.9 %fusion.20 = f32[4,256,256]{2,1,0:T(8,128)S(1)} fusion(f32[4,256,256]{1,2,0:T(8,128)S(1)} %convolution_bitcast_fusion), kind=kOutput, calls=%fused_computation.39 | convolution fusion | flops 403636224 | bytes 2097152 | tf_op jit(solution)/shard_map/kz,xyz->xyk/dot_general | solution.py:32
  128.6 0.5 reshape.125
  129.1 1.7 copy.23
  130.8 16.1 %all-to-all-done.2 = f32[32,4,16,128]{3,1,2,0:T(4,128)S(1)} async-done(((f32[32,4,16,128]{3,1,2,0:T(4,128)}), f32[32,4,16,128]{3,1,2,0:T(4,128)S(1)}, u32[]{:S(2)}, u32[]{:S(2)}) %all-to-all-start.2) | async-done | bytes 1048608 | tf_op jit(solution)/shard_map/all_to_all | solution.py:364
  146.8 4.7 %all-to-all-start.3 = ((f32[32,4,16,128]{3,1,2,0:T(4,128)}), f32[32,4,16,128]{3,1,2,0:T(4,128)}, u32[]{:S(2)}, u32[]{:S(2)}) async-start(f32[32,4,16,128]{3,1,2,0:T(4,128)} %bitcast.27), calls=%async_computation.3 | async-start | bytes 2097152 | tf_op jit(solution)/shard_map/all_to_all | solution.py:364
  151.5 1.1 sine_add_fusion
  152.6 4.0 %pad_maximum_fusion.w_ref.w_prev.w_next = f32[2,16,128,256]{3,2,1,0:T(8,128)} fusion(f32[2,8,128,256]{3,2,1,0:T(8,128)} %get-tuple-element.30, f32[2,8,128,256]{3,2,1,0:T(8,128)S(1)} %copy-done.3), kind=kLoop, calls=%fused_computation | loop fusion | flops 1048576 | bytes 8388608 | tf_op jit(solution)/shard_map/concatenate | solution.py:303
  156.7 6.8 %shard_map.72 = f32[2,16,128,256]{3,2,1,0:T(8,128)} custom-call(f32[2,16,128,256]{3,2,1,0:T(8,128)} %pad_maximum_fusion.w_ref.w_prev.w_next, f32[2,16,128,256]{3,2,1,0:T(8,128)} %pad_maximum_fusion.w_ref.w_prev.w_next, f32[2,16,128,256]{3,2,1,0:T(8,128)} %pad_maximum_fusion.w_ref.w_prev.w_next, f32[2,128,256]{2,1,0:T(8,128)} %copy-done.5, ...), custom_call_target="tpu_custom_call" | custom-call | tf_op jit(solution)/shard_map/pallas_call | solution.py:311
  163.5 1.5 fusion.12
  165.0 11.8 %all-to-all-done.3 = f32[32,4,16,128]{3,1,2,0:T(4,128)} async-done(((f32[32,4,16,128]{3,1,2,0:T(4,128)}), f32[32,4,16,128]{3,1,2,0:T(4,128)}, u32[]{:S(2)}, u32[]{:S(2)}) %all-to-all-start.3) | async-done | bytes 1048608 | tf_op jit(solution)/shard_map/all_to_all | solution.py:364
  176.8 4.0 %fusion = f32[16,128,256]{2,1,0:T(8,128)} fusion(f32[16,128,256,1]{2,1,3,0:T(8,128)S(1)} %fusion.12, f32[32,4,16,128]{3,1,2,0:T(4,128)} %all-to-all-done.3, f32[32,2,4,256]{3,0,2,1:T(8,128)S(1)} %sine_add_fusion), kind=kOutput, calls=%fused_computation.3 | convolution fusion | flops 403701760 | bytes 5373952 | tf_op jit(solution)/shard_map/sxn,sxyz->yzn/dot_general | solution.py:32
  (30 shorter events, 0.4 us)
Async XLA Ops:
  5.2 14.7 %collective-permute-start = (f32[6,128,256]{2,1,0:T(8,128)}, f32[6,128,256]{2,1,0:T(8,128)S(1)}, u32[]{:S(2)}, u32[]{:S(2)}) collective-permute-start(f32[6,128,256]{2,1,0:T(8,128)} %get-tuple-element.25), channel_id=1, source_target_pairs={{0,2},{2,4},{4,6},{6,8},{8,10},{10,12},{12,14},{14,16},{16,18},{18... | collective-permute-start | bytes 2359304 | tf_op jit(solution)/shard_map/ppermute | solution.py:243
  5.2 14.6 %collective-permute-start.1 = (f32[6,128,256]{2,1,0:T(8,128)}, f32[6,128,256]{2,1,0:T(8,128)S(1)}, u32[]{:S(2)}, u32[]{:S(2)}) collective-permute-start(f32[6,128,256]{2,1,0:T(8,128)} %get-tuple-element.26), channel_id=1, source_target_pairs={{2,0},{4,2},{6,4},{8,6},{10,8},{12,10},{14,12},{16,14},{18,16},{20... | collective-permute-start | bytes 2359304 | tf_op jit(solution)/shard_map/ppermute | solution.py:243
  9.0 10.0 %collective-permute-start.2 = (f32[2,6,16,1,256]{4,3,2,1,0:T(1,128)S(1)}, f32[2,6,16,1,256]{4,3,2,1,0:T(1,128)S(1)}, u32[]{:S(2)}, u32[]{:S(2)}) collective-permute-start(f32[2,6,16,1,256]{4,3,2,1,0:T(1,128)S(1)} %pad_maximum_fusion.1), channel_id=1, source_target_pairs={{0,1},{1,0},{2,3},{3,2},{4,5},{5,4},{6,7},{7,6},{8,9},{9,8},{10,11... | collective-permute-start | bytes 589832 | tf_op jit(solution)/shard_map/ppermute | solution.py:240
  19.9 1.0 copy-start.1
  19.9 1.2 copy-start.2
  36.0 41.2 %all-to-all-start = ((f32[32,8,8,128]{3,1,2,0:T(8,128)}), f32[32,8,8,128]{3,1,2,0:T(8,128)S(1)}, u32[]{:S(2)}, u32[]{:S(2)}) async-start(f32[32,8,8,128]{3,1,2,0:T(8,128)} %copy.13), calls=%async_computation | async-start | bytes 2097152 | tf_op jit(solution)/shard_map/all_to_all | solution.py:347
  47.4 11.3 %copy-start.6 = (f32[2,8,1,256]{3,2,1,0:T(1,128)S(1)}, f32[2,8,1,256]{3,2,1,0:T(1,128)}, u32[]{:S(2)}) copy-start(f32[2,8,1,256]{3,2,1,0:T(1,128)} %get-tuple-element.35) | copy-start | bytes 49156
  47.4 11.3 %copy-start.7 = (f32[2,8,1,256]{3,2,1,0:T(1,128)S(1)}, f32[2,8,1,256]{3,2,1,0:T(1,128)}, u32[]{:S(2)}) copy-start(f32[2,8,1,256]{3,2,1,0:T(1,128)} %get-tuple-element.33) | copy-start | bytes 49156
  47.4 13.7 %copy-start.8 = (f32[2,128,256]{2,1,0:T(8,128)S(1)}, f32[2,128,256]{2,1,0:T(8,128)}, u32[]{:S(2)}) copy-start(f32[2,128,256]{2,1,0:T(8,128)} %get-tuple-element.32) | copy-start | bytes 786436
  59.5 5.3 %collective-permute-start.5 = (f32[2,2,16,1,256]{4,3,2,1,0:T(1,128)S(1)}, f32[2,2,16,1,256]{4,3,2,1,0:T(1,128)S(1)}, u32[]{:S(2)}, u32[]{:S(2)}) collective-permute-start(f32[2,2,16,1,256]{4,3,2,1,0:T(1,128)S(1)} %pad_maximum_fusion.2), channel_id=1, source_target_pairs={{0,1},{1,0},{2,3},{3,2},{4,5},{5,4},{6,7},{7,6},{8,9},{9,8},{10,11... | collective-permute-start | bytes 196616 | tf_op jit(solution)/shard_map/ppermute | solution.py:240
  61.1 12.2 %collective-permute-start.4 = (f32[2,128,256]{2,1,0:T(8,128)S(1)}, f32[2,128,256]{2,1,0:T(8,128)S(1)}, u32[]{:S(2)}, u32[]{:S(2)}) collective-permute-start(f32[2,128,256]{2,1,0:T(8,128)S(1)} %copy-done.8), channel_id=1, source_target_pairs={{2,0},{4,2},{6,4},{8,6},{10,8},{12,10},{14,12},{16,14},{18,16},{20... | collective-permute-start | bytes 786440 | tf_op jit(solution)/shard_map/ppermute | solution.py:243
  62.0 13.4 %collective-permute-start.3 = (f32[2,128,256]{2,1,0:T(8,128)}, f32[2,128,256]{2,1,0:T(8,128)S(1)}, u32[]{:S(2)}, u32[]{:S(2)}) collective-permute-start(f32[2,128,256]{2,1,0:T(8,128)} %get-tuple-element.31), channel_id=1, source_target_pairs={{0,2},{2,4},{4,6},{6,8},{8,10},{10,12},{12,14},{14,16},{16,18},{18... | collective-permute-start | bytes 786440 | tf_op jit(solution)/shard_map/ppermute | solution.py:243
  73.3 2.1 %copy-start.4 = (f32[2,128,256]{2,1,0:T(8,128)}, f32[2,128,256]{2,1,0:T(8,128)S(1)}, u32[]{:S(2)}) copy-start(f32[2,128,256]{2,1,0:T(8,128)S(1)} %collective-permute-done.4.y_high_ref) | copy-start | bytes 786436
  75.4 0.7 copy-start.5
  77.2 29.0 %all-to-all-start.1 = ((f32[32,8,8,128]{3,1,2,0:T(8,128)}), f32[32,8,8,128]{3,1,2,0:T(8,128)S(1)}, u32[]{:S(2)}, u32[]{:S(2)}) async-start(f32[32,8,8,128]{3,1,2,0:T(8,128)} %copy.15), calls=%async_computation.1 | async-start | bytes 2097152 | tf_op jit(solution)/shard_map/all_to_all | solution.py:347
  115.3 6.3 %copy-start = (f32[4,16,2,8,2,128]{5,3,4,2,1,0:T(8,128)S(1)}, f32[4,16,2,8,2,128]{5,3,4,2,1,0:T(8,128)}, u32[]{:S(2)}) copy-start(f32[4,16,2,8,2,128]{5,3,4,2,1,0:T(8,128)} %get-tuple-element.44) | copy-start | bytes 3145732
  117.0 29.9 %all-to-all-start.2 = ((f32[32,4,16,128]{3,1,2,0:T(4,128)}), f32[32,4,16,128]{3,1,2,0:T(4,128)S(1)}, u32[]{:S(2)}, u32[]{:S(2)}) async-start(f32[32,4,16,128]{3,1,2,0:T(4,128)} %bitcast.18), calls=%async_computation.2 | async-start | bytes 2097152 | tf_op jit(solution)/shard_map/all_to_all | solution.py:364
  130.8 21.9 %copy-start.3 = (f32[2,8,128,256]{3,2,1,0:T(8,128)S(1)}, f32[2,8,128,256]{3,2,1,0:T(8,128)}, u32[]{:S(2)}) copy-start(f32[2,8,128,256]{3,2,1,0:T(8,128)} %get-tuple-element.29) | copy-start | bytes 6291460
  146.8 30.0 %all-to-all-start.3 = ((f32[32,4,16,128]{3,1,2,0:T(4,128)}), f32[32,4,16,128]{3,1,2,0:T(4,128)}, u32[]{:S(2)}, u32[]{:S(2)}) async-start(f32[32,4,16,128]{3,1,2,0:T(4,128)} %bitcast.27), calls=%async_computation.3 | async-start | bytes 2097152 | tf_op jit(solution)/shard_map/all_to_all | solution.py:364

commit v6 on v4

--- a/solution.py
+++ b/solution.py
@@ -34,9 +34,16 @@
 
 def plane_update(centre, below, above, z_low, z_high):
     length_z, length_x = centre.shape
-    row = lax.broadcasted_iota(jnp.int32, centre.shape, 0)
-    up = jnp.where(row == 0, z_low, pltpu.roll(centre, 1, 0))
-    down = jnp.where(row == length_z - 1, z_high, pltpu.roll(centre, length_z - 1, 0))
+    up = pltpu.roll(centre, 1, 0)
+    down = pltpu.roll(centre, length_z - 1, 0)
+    if length_z > 8:
+        row = lax.broadcasted_iota(jnp.int32, (8, length_x), 0)
+        up = jnp.concatenate([jnp.where(row == 0, z_low, up[:8]), up[8:]], axis=0)
+        down = jnp.concatenate([down[:length_z - 8], jnp.where(row == 7, z_high, down[length_z - 8:])], axis=0)
+    else:
+        row = lax.broadcasted_iota(jnp.int32, centre.shape, 0)
+        up = jnp.where(row == 0, z_low, up)
+        down = jnp.where(row == length_z - 1, z_high, down)
     total = below + above + up + down
     total = total + pltpu.roll(centre, 1, 1) + pltpu.roll(centre, length_x - 1, 1)
     return centre + 0.15 * (total - 6.0 * centre)

time: 183 us -> 183 us (level)
  no operation moved by 1% of the time
where the time goes in v6:
time: 183 us; the launch traced here: 180 us
  waiting for transfers between devices  68.2 us (37%)
  Pallas kernels  36.1 us (20%)
  starting transfers between devices  33.5 us (18%)
  matrix products  23.2 us (13%)
  local copies, waits for them, and re-layouts  14.3 us (8%)
  other arithmetic  3.93 us (2%)
    all_to_all x2, waiting for transfers between devices, dipole_adjoint(): sent.append(lax.all_to_all(spec, ('gy', 'gz'), 0, 0, tiled=True))  36 us
    all_to_all x2, waiting for transfers between devices, dipole_adjoint(): spec = lax.all_to_all(spec, ('gy', 'gz'), 0, 0, tiled=True)  31.3 us
    dot_general x12, matrix products, along(): return jnp.einsum(spec, table, values, precision=lax.Precision.HIGH)  23.2 us
    pallas_call x1, Pallas kernels, backward_sections(): pl.pallas_call(functools.partial(first_kernel, rows=rows), grid=grid, in_...  16.1 us
    all_to_all x2, starting transfers between devices, dipole_adjoint(): sent.append(lax.all_to_all(spec, ('gy', 'gz'), 0, 0, tiled=True))  14.1 us
    all_to_all x2, starting transfers between devices, dipole_adjoint(): spec = lax.all_to_all(spec, ('gy', 'gz'), 0, 0, tiled=True)  9.27 us
    pallas_call x1, Pallas kernels, backward_sections(): pl.pallas_call(functools.partial(factor_kernel, rows=rows), grid=grid, in...  8.52 us
    pallas_call x1, Pallas kernels, finish_lambda(): pl.pallas_call(functools.partial(second_kernel, rows=rows), grid=grid, in...  6.88 us
  transfers between devices with their start and end apart: 10, of which 5 were waited for; matrix products, arithmetic and copies ran while one was open for 18% of the time, Pallas kernels for 9%

profile of v6, /device:TPU:16, one launch (start us, length us, event | category | flops | bytes accessed | tf_op | source)
XLA Modules:
  0.0 180.2 jit_solution(10746572661008564916)
XLA Ops:
  0.6 4.5 %shard_map.69 = (f32[6,128,256]{2,1,0:T(8,128)}, f32[6,128,256]{2,1,0:T(8,128)}, f32[6,16,1,256]{3,2,1,0:T(1,128)}, f32[6,16,1,256]{3,2,1,0:T(1,128)}) custom-call(f32[2,16,128,256]{3,2,1,0:T(8,128)} %refs_2_.3, f32[2,16,128,256]{3,2,1,0:T(8,128)} %refs_2_.3, f32[2,16,128,256]{3,2,1,0:T(8,128)} %refs_2_.3, f32[2,16,128,256]{3,2,1,0:T(8,128)} %refs_2_.3, ...), custom_call_target="tpu_custom_call" | custom-call | tf_op jit(solution)/shard_map/pallas_call | solution.py:268
  5.2 2.6 %collective-permute-start.1 = (f32[6,128,256]{2,1,0:T(8,128)}, f32[6,128,256]{2,1,0:T(8,128)S(1)}, u32[]{:S(2)}, u32[]{:S(2)}) collective-permute-start(f32[6,128,256]{2,1,0:T(8,128)} %get-tuple-element.22), channel_id=1, source_target_pairs={{2,0},{4,2},{6,4},{8,6},{10,8},{12,10},{14,12},{16,14},{18,16},{20... | collective-permute-start | bytes 2359304 | tf_op jit(solution)/shard_map/ppermute | solution.py:251
  7.9 1.1 pad_maximum_fusion
  9.0 1.6 collective-permute-start.2
  10.6 8.5 %shard_map.68 = (f32[2,16,128,256]{3,2,1,0:T(8,128)}, f32[2,16,128,256]{3,2,1,0:T(8,128)}) custom-call(f32[2,16,128,256]{3,2,1,0:T(8,128)} %refs_11_.1, f32[16,128,256]{2,1,0:T(8,128)} %refs_15_.1, s32[16,128,256]{2,1,0:T(8,128)} %refs_19_.1), custom_call_target="tpu_custom_call" | custom-call | tf_op jit(solution)/shard_map/pallas_call | solution.py:276
  19.1 1.1 sine_add_fusion.1
  20.2 0.8 slice_bitcast_fusion
  21.1 1.0 copy-done.1
  22.0 0.2 copy-done.2
  22.2 16.1 %shard_map.70 = (f32[16,128,256]{2,1,0:T(8,128)}, f32[2,16,128,256]{3,2,1,0:T(8,128)}, f32[2,128,256]{2,1,0:T(8,128)}, f32[2,128,256]{2,1,0:T(8,128)}, f32[2,16,...) custom-call(f32[2,16,128,256]{3,2,1,0:T(8,128)} %refs_2_.3, f32[2,16,128,256]{3,2,1,0:T(8,128)} %refs_2_.3, ...), custom_call_target="tpu_custom_call" | custom-call | tf_op jit(solution)/shard_map/pallas_call | solution.py:283
  38.4 0.8 pad_maximum_fusion.1
  39.2 0.6 collective-permute-start.5
  39.8 5.3 %collective-permute-start.3 = (f32[2,128,256]{2,1,0:T(8,128)}, f32[2,128,256]{2,1,0:T(8,128)S(1)}, u32[]{:S(2)}, u32[]{:S(2)}) collective-permute-start(f32[2,128,256]{2,1,0:T(8,128)} %get-tuple-element.26), channel_id=1, source_target_pairs={{0,2},{2,4},{4,6},{6,8},{8,10},{10,12},{12,14},{14,16},{16,18},{18... | collective-permute-start | bytes 786440 | tf_op jit(solution)/shard_map/ppermute | solution.py:251
  45.1 2.8 %fusion.3 = f32[32,4,16,128]{3,0,2,1:T(8,128)S(1)} fusion(f32[16,128,256]{2,1,0:T(8,128)} %get-tuple-element.30, f32[32,2,4,256]{3,0,2,1:T(8,128)S(1)} %sine_add_fusion.1), kind=kOutput, calls=%fused_computation.4 | convolution fusion | flops 402653184 | bytes 3276800 | tf_op jit(solution)/shard_map/sxn,yzn->sxyz/dot_general | solution.py:32
  47.9 0.6 slice_bitcast_fusion.2
  48.5 0.8 collective-permute-done.4.y_high_ref
  49.4 0.7 copy-done.4
  50.1 1.6 copy.13
  51.7 9.5 %all-to-all-start = ((f32[32,4,16,128]{3,2,1,0:T(8,128)}), f32[32,4,16,128]{3,2,1,0:T(8,128)S(1)}, u32[]{:S(2)}, u32[]{:S(2)}) async-start(f32[32,4,16,128]{3,2,1,0:T(8,128)} %copy.13), calls=%async_computation | async-start | bytes 2097152 | tf_op jit(solution)/shard_map/all_to_all | solution.py:332
  61.2 1.2 fusion.1
  62.4 1.6 copy.19
  64.0 22.5 %all-to-all-done = f32[32,4,16,128]{3,2,1,0:T(8,128)S(1)} async-done(((f32[32,4,16,128]{3,2,1,0:T(8,128)}), f32[32,4,16,128]{3,2,1,0:T(8,128)S(1)}, u32[]{:S(2)}, u32[]{:S(2)}) %all-to-all-start) | async-done | bytes 1048608 | tf_op jit(solution)/shard_map/all_to_all | solution.py:332
  86.5 4.6 %all-to-all-start.2 = ((f32[32,4,16,128]{3,2,1,0:T(8,128)}), f32[32,4,16,128]{3,2,1,0:T(8,128)S(1)}, u32[]{:S(2)}, u32[]{:S(2)}) async-start(f32[32,4,16,128]{3,2,1,0:T(8,128)} %copy.19), calls=%async_computation.2 | async-start | bytes 2097152 | tf_op jit(solution)/shard_map/all_to_all | solution.py:332
  91.1 0.8 broadcast_add_fusion
  91.9 0.8 copy.40
  92.7 0.8 reshape.120
  93.6 1.6 fusion.34
  95.2 1.8 fusion.5
  97.0 1.6 convolution_bitcast_fusion.2
  98.7 1.9 %fusion.30 = f32[4,256,256]{2,1,0:T(8,128)S(1)} fusion(f32[4,256,256]{1,2,0:T(8,128)S(1)} %convolution_bitcast_fusion.2), kind=kOutput, calls=%fused_computation.47 | convolution fusion | flops 403636224 | bytes 2097152 | tf_op jit(solution)/shard_map/kz,xyz->xyk/dot_general | solution.py:32
  100.6 0.5 reshape.121
  101.1 1.7 copy.17
  102.8 13.5 %all-to-all-done.2 = f32[32,4,16,128]{3,2,1,0:T(8,128)S(1)} async-done(((f32[32,4,16,128]{3,2,1,0:T(8,128)}), f32[32,4,16,128]{3,2,1,0:T(8,128)S(1)}, u32[]{:S(2)}, u32[]{:S(2)}) %all-to-all-start.2) | async-done | bytes 1048608 | tf_op jit(solution)/shard_map/all_to_all | solution.py:332
  116.3 4.6 %all-to-all-start.1 = ((f32[32,4,16,128]{3,1,2,0:T(4,128)}), f32[32,4,16,128]{3,1,2,0:T(4,128)S(1)}, u32[]{:S(2)}, u32[]{:S(2)}) async-start(f32[32,4,16,128]{3,1,2,0:T(4,128)} %bitcast.18), calls=%async_computation.1 | async-start | bytes 2097152 | tf_op jit(solution)/shard_map/all_to_all | solution.py:349
  121.0 0.8 copy.39
  121.8 0.8 reshape.124
  122.6 1.6 fusion.28
  124.3 1.8 fusion.6
  126.1 1.6 convolution_bitcast_fusion
  127.7 1.9 %fusion.24 = f32[4,256,256]{2,1,0:T(8,128)S(1)} fusion(f32[4,256,256]{1,2,0:T(8,128)S(1)} %convolution_bitcast_fusion), kind=kOutput, calls=%fused_computation.41 | convolution fusion | flops 403636224 | bytes 2097152 | tf_op jit(solution)/shard_map/kz,xyz->xyk/dot_general | solution.py:32
  129.6 0.5 reshape.125
  130.1 1.7 copy.23
  131.8 14.4 %all-to-all-done.1 = f32[32,4,16,128]{3,1,2,0:T(4,128)S(1)} async-done(((f32[32,4,16,128]{3,1,2,0:T(4,128)}), f32[32,4,16,128]{3,1,2,0:T(4,128)S(1)}, u32[]{:S(2)}, u32[]{:S(2)}) %all-to-all-start.1) | async-done | bytes 1048608 | tf_op jit(solution)/shard_map/all_to_all | solution.py:349
  146.2 4.7 %all-to-all-start.3 = ((f32[32,4,16,128]{3,1,2,0:T(4,128)}), f32[32,4,16,128]{3,1,2,0:T(4,128)}, u32[]{:S(2)}, u32[]{:S(2)}) async-start(f32[32,4,16,128]{3,1,2,0:T(4,128)} %bitcast.29), calls=%async_computation.3 | async-start | bytes 2097152 | tf_op jit(solution)/shard_map/all_to_all | solution.py:349
  150.9 6.9 %shard_map.71 = f32[2,16,128,256]{3,2,1,0:T(8,128)} custom-call(f32[2,16,128,256]{3,2,1,0:T(8,128)} %get-tuple-element.25.w_ref.w_prev.w_next, f32[2,16,128,256]{3,2,1,0:T(8,128)} %get-tuple-element.25.w_ref.w_prev.w_next, f32[2,16,128,256]{3,2,1,0:T(8,128)} %get-tuple-element.25.w_ref.w_prev.w_next, f32[2,128,256]{2,1,0:T(8,128)} %copy-done.3, ...), custom_call_target="tpu_custom_call" | custom-call | tf_op jit(solution)/shard_map/pallas_call | solution.py:299
  157.7 1.5 fusion.16
  159.2 16.9 %all-to-all-done.3 = f32[32,4,16,128]{3,1,2,0:T(4,128)} async-done(((f32[32,4,16,128]{3,1,2,0:T(4,128)}), f32[32,4,16,128]{3,1,2,0:T(4,128)}, u32[]{:S(2)}, u32[]{:S(2)}) %all-to-all-start.3) | async-done | bytes 1048608 | tf_op jit(solution)/shard_map/all_to_all | solution.py:349
  176.2 4.0 %fusion = f32[16,128,256]{2,1,0:T(8,128)} fusion(f32[16,128,256,1]{2,1,3,0:T(8,128)S(1)} %fusion.16, f32[32,4,16,128]{3,1,2,0:T(4,128)} %all-to-all-done.3, f32[32,2,4,256]{3,0,2,1:T(8,128)S(1)} %sine_add_fusion.1), kind=kOutput, calls=%fused_computation.1 | convolution fusion | flops 403701760 | bytes 5373952 | tf_op jit(solution)/shard_map/sxn,sxyz->yzn/dot_general | solution.py:32
  (23 shorter events, 0.1 us)
Async XLA Ops:
  5.2 15.9 %collective-permute-start = (f32[6,128,256]{2,1,0:T(8,128)}, f32[6,128,256]{2,1,0:T(8,128)S(1)}, u32[]{:S(2)}, u32[]{:S(2)}) collective-permute-start(f32[6,128,256]{2,1,0:T(8,128)} %get-tuple-element.21), channel_id=1, source_target_pairs={{0,2},{2,4},{4,6},{6,8},{8,10},{10,12},{12,14},{14,16},{16,18},{18... | collective-permute-start | bytes 2359304 | tf_op jit(solution)/shard_map/ppermute | solution.py:251
  5.2 15.8 %collective-permute-start.1 = (f32[6,128,256]{2,1,0:T(8,128)}, f32[6,128,256]{2,1,0:T(8,128)S(1)}, u32[]{:S(2)}, u32[]{:S(2)}) collective-permute-start(f32[6,128,256]{2,1,0:T(8,128)} %get-tuple-element.22), channel_id=1, source_target_pairs={{2,0},{4,2},{6,4},{8,6},{10,8},{12,10},{14,12},{16,14},{18,16},{20... | collective-permute-start | bytes 2359304 | tf_op jit(solution)/shard_map/ppermute | solution.py:251
  9.0 11.2 %collective-permute-start.2 = (f32[2,6,16,1,256]{4,3,2,1,0:T(1,128)S(1)}, f32[2,6,16,1,256]{4,3,2,1,0:T(1,128)S(1)}, u32[]{:S(2)}, u32[]{:S(2)}) collective-permute-start(f32[2,6,16,1,256]{4,3,2,1,0:T(1,128)S(1)} %pad_maximum_fusion), channel_id=1, source_target_pairs={{0,1},{1,0},{2,3},{3,2},{4,5},{5,4},{6,7},{7,6},{8,9},{9,8},{10,11... | collective-permute-start | bytes 589832 | tf_op jit(solution)/shard_map/ppermute | solution.py:248
  21.0 1.0 copy-start.1
  21.1 1.2 copy-start.2
  39.2 8.7 %collective-permute-start.5 = (f32[2,2,16,1,256]{4,3,2,1,0:T(1,128)S(1)}, f32[2,2,16,1,256]{4,3,2,1,0:T(1,128)S(1)}, u32[]{:S(2)}, u32[]{:S(2)}) collective-permute-start(f32[2,2,16,1,256]{4,3,2,1,0:T(1,128)S(1)} %pad_maximum_fusion.1), channel_id=1, source_target_pairs={{0,1},{1,0},{2,3},{3,2},{4,5},{5,4},{6,7},{7,6},{8,9},{9,8},{10,11... | collective-permute-start | bytes 196616 | tf_op jit(solution)/shard_map/ppermute | solution.py:248
  39.8 8.7 %collective-permute-start.3 = (f32[2,128,256]{2,1,0:T(8,128)}, f32[2,128,256]{2,1,0:T(8,128)S(1)}, u32[]{:S(2)}, u32[]{:S(2)}) collective-permute-start(f32[2,128,256]{2,1,0:T(8,128)} %get-tuple-element.26), channel_id=1, source_target_pairs={{0,2},{2,4},{4,6},{6,8},{8,10},{10,12},{12,14},{14,16},{16,18},{18... | collective-permute-start | bytes 786440 | tf_op jit(solution)/shard_map/ppermute | solution.py:251
  45.1 4.3 %collective-permute-start.4 = (f32[2,128,256]{2,1,0:T(8,128)}, f32[2,128,256]{2,1,0:T(8,128)S(1)}, u32[]{:S(2)}, u32[]{:S(2)}) collective-permute-start(f32[2,128,256]{2,1,0:T(8,128)} %get-tuple-element.27), channel_id=1, source_target_pairs={{2,0},{4,2},{6,4},{8,6},{10,8},{12,10},{14,12},{16,14},{18,16},{20... | collective-permute-start | bytes 786440 | tf_op jit(solution)/shard_map/ppermute | solution.py:251
  48.5 0.9 copy-start.3
  49.4 0.7 copy-start.4
  50.1 11.1 %copy-start = (f32[16,128,256]{2,1,0:T(8,128)S(1)}, f32[16,128,256]{2,1,0:T(8,128)}, u32[]{:S(2)}) copy-start(f32[16,128,256]{2,1,0:T(8,128)} %get-tuple-element.30) | copy-start | bytes 6291460
  51.7 34.8 %all-to-all-start = ((f32[32,4,16,128]{3,2,1,0:T(8,128)}), f32[32,4,16,128]{3,2,1,0:T(8,128)S(1)}, u32[]{:S(2)}, u32[]{:S(2)}) async-start(f32[32,4,16,128]{3,2,1,0:T(8,128)} %copy.13), calls=%async_computation | async-start | bytes 2097152 | tf_op jit(solution)/shard_map/all_to_all | solution.py:332
  86.5 29.9 %all-to-all-start.2 = ((f32[32,4,16,128]{3,2,1,0:T(8,128)}), f32[32,4,16,128]{3,2,1,0:T(8,128)S(1)}, u32[]{:S(2)}, u32[]{:S(2)}) async-start(f32[32,4,16,128]{3,2,1,0:T(8,128)} %copy.19), calls=%async_computation.2 | async-start | bytes 2097152 | tf_op jit(solution)/shard_map/all_to_all | solution.py:332
  93.6 1.7 copy-start.5
  116.3 29.9 %all-to-all-start.1 = ((f32[32,4,16,128]{3,1,2,0:T(4,128)}), f32[32,4,16,128]{3,1,2,0:T(4,128)S(1)}, u32[]{:S(2)}, u32[]{:S(2)}) async-start(f32[32,4,16,128]{3,1,2,0:T(4,128)} %bitcast.18), calls=%async_computation.1 | async-start | bytes 2097152 | tf_op jit(solution)/shard_map/all_to_all | solution.py:349
  122.6 1.7 copy-start.6
  146.2 30.0 %all-to-all-start.3 = ((f32[32,4,16,128]{3,1,2,0:T(4,128)}), f32[32,4,16,128]{3,1,2,0:T(4,128)}, u32[]{:S(2)}, u32[]{:S(2)}) async-start(f32[32,4,16,128]{3,1,2,0:T(4,128)} %bitcast.29), calls=%async_computation.3 | async-start | bytes 2097152 | tf_op jit(solution)/shard_map/all_to_all | solution.py:349

commit v7 on v6

--- a/solution.py
+++ b/solution.py
@@ -46,7 +46,7 @@
         down = jnp.where(row == length_z - 1, z_high, down)
     total = below + above + up + down
     total = total + pltpu.roll(centre, 1, 1) + pltpu.roll(centre, length_x - 1, 1)
-    return centre + 0.15 * (total - 6.0 * centre)
+    return 0.1 * centre + 0.15 * total
 
 
 def neighbour_planes(cur_ref, prev_ref, next_ref, y_low_ref, y_high_ref, rows, field, comp, r, step, last):

time: 183 us -> 184 us (level)
  no operation moved by 1% of the time
where the time goes in v7:
time: 184 us; the launch traced here: 181 us
  waiting for transfers between devices  68.2 us (37%)
  Pallas kernels  36.5 us (20%)
  starting transfers between devices  33.5 us (18%)
  matrix products  23.2 us (13%)
  local copies, waits for them, and re-layouts  14.3 us (8%)
  other arithmetic  3.93 us (2%)
    all_to_all x2, waiting for transfers between devices, dipole_adjoint(): sent.append(lax.all_to_all(spec, ('gy', 'gz'), 0, 0, tiled=True))  36 us
    all_to_all x2, waiting for transfers between devices, dipole_adjoint(): spec = lax.all_to_all(spec, ('gy', 'gz'), 0, 0, tiled=True)  31.3 us
    dot_general x12, matrix products, along(): return jnp.einsum(spec, table, values, precision=lax.Precision.HIGH)  23.2 us
    pallas_call x1, Pallas kernels, backward_sections(): pl.pallas_call(functools.partial(first_kernel, rows=rows), grid=grid, in_...  16.6 us
    all_to_all x2, starting transfers between devices, dipole_adjoint(): sent.append(lax.all_to_all(spec, ('gy', 'gz'), 0, 0, tiled=True))  14.1 us
    all_to_all x2, starting transfers between devices, dipole_adjoint(): spec = lax.all_to_all(spec, ('gy', 'gz'), 0, 0, tiled=True)  9.27 us
    pallas_call x1, Pallas kernels, backward_sections(): pl.pallas_call(functools.partial(factor_kernel, rows=rows), grid=grid, in...  8.52 us
    pallas_call x1, Pallas kernels, finish_lambda(): pl.pallas_call(functools.partial(second_kernel, rows=rows), grid=grid, in...  6.84 us
  transfers between devices with their start and end apart: 10, of which 5 were waited for; matrix products, arithmetic and copies ran while one was open for 18% of the time, Pallas kernels for 9%

profile of v7, /device:TPU:16, one launch (start us, length us, event | category | flops | bytes accessed | tf_op | source)
XLA Modules:
  0.0 180.6 jit_solution(10081137533427823238)
XLA Ops:
  0.6 4.5 %shard_map.69 = (f32[6,128,256]{2,1,0:T(8,128)}, f32[6,128,256]{2,1,0:T(8,128)}, f32[6,16,1,256]{3,2,1,0:T(1,128)}, f32[6,16,1,256]{3,2,1,0:T(1,128)}) custom-call(f32[2,16,128,256]{3,2,1,0:T(8,128)} %refs_2_.3, f32[2,16,128,256]{3,2,1,0:T(8,128)} %refs_2_.3, f32[2,16,128,256]{3,2,1,0:T(8,128)} %refs_2_.3, f32[2,16,128,256]{3,2,1,0:T(8,128)} %refs_2_.3, ...), custom_call_target="tpu_custom_call" | custom-call | tf_op jit(solution)/shard_map/pallas_call | solution.py:268
  5.2 2.6 %collective-permute-start.1 = (f32[6,128,256]{2,1,0:T(8,128)}, f32[6,128,256]{2,1,0:T(8,128)S(1)}, u32[]{:S(2)}, u32[]{:S(2)}) collective-permute-start(f32[6,128,256]{2,1,0:T(8,128)} %get-tuple-element.22), channel_id=1, source_target_pairs={{2,0},{4,2},{6,4},{8,6},{10,8},{12,10},{14,12},{16,14},{18,16},{20... | collective-permute-start | bytes 2359304 | tf_op jit(solution)/shard_map/ppermute | solution.py:251
  7.9 1.1 pad_maximum_fusion
  9.0 1.6 collective-permute-start.2
  10.6 8.5 %shard_map.68 = (f32[2,16,128,256]{3,2,1,0:T(8,128)}, f32[2,16,128,256]{3,2,1,0:T(8,128)}) custom-call(f32[2,16,128,256]{3,2,1,0:T(8,128)} %refs_11_.1, f32[16,128,256]{2,1,0:T(8,128)} %refs_15_.1, s32[16,128,256]{2,1,0:T(8,128)} %refs_19_.1), custom_call_target="tpu_custom_call" | custom-call | tf_op jit(solution)/shard_map/pallas_call | solution.py:276
  19.1 1.1 sine_add_fusion.1
  20.2 0.8 slice_bitcast_fusion
  21.1 1.0 copy-done.1
  22.0 0.2 copy-done.2
  22.2 16.6 %shard_map.70 = (f32[16,128,256]{2,1,0:T(8,128)}, f32[2,16,128,256]{3,2,1,0:T(8,128)}, f32[2,128,256]{2,1,0:T(8,128)}, f32[2,128,256]{2,1,0:T(8,128)}, f32[2,16,...) custom-call(f32[2,16,128,256]{3,2,1,0:T(8,128)} %refs_2_.3, f32[2,16,128,256]{3,2,1,0:T(8,128)} %refs_2_.3, ...), custom_call_target="tpu_custom_call" | custom-call | tf_op jit(solution)/shard_map/pallas_call | solution.py:283
  38.8 0.8 pad_maximum_fusion.1
  39.7 0.6 collective-permute-start.5
  40.3 5.3 %collective-permute-start.3 = (f32[2,128,256]{2,1,0:T(8,128)}, f32[2,128,256]{2,1,0:T(8,128)S(1)}, u32[]{:S(2)}, u32[]{:S(2)}) collective-permute-start(f32[2,128,256]{2,1,0:T(8,128)} %get-tuple-element.26), channel_id=1, source_target_pairs={{0,2},{2,4},{4,6},{6,8},{8,10},{10,12},{12,14},{14,16},{16,18},{18... | collective-permute-start | bytes 786440 | tf_op jit(solution)/shard_map/ppermute | solution.py:251
  45.6 2.8 %fusion.3 = f32[32,4,16,128]{3,0,2,1:T(8,128)S(1)} fusion(f32[16,128,256]{2,1,0:T(8,128)} %get-tuple-element.30, f32[32,2,4,256]{3,0,2,1:T(8,128)S(1)} %sine_add_fusion.1), kind=kOutput, calls=%fused_computation.4 | convolution fusion | flops 402653184 | bytes 3276800 | tf_op jit(solution)/shard_map/sxn,yzn->sxyz/dot_general | solution.py:32
  48.4 0.6 slice_bitcast_fusion.2
  49.0 0.9 collective-permute-done.4.y_high_ref
  49.8 0.7 copy-done.4
  50.5 1.6 copy.13
  52.1 9.5 %all-to-all-start = ((f32[32,4,16,128]{3,2,1,0:T(8,128)}), f32[32,4,16,128]{3,2,1,0:T(8,128)S(1)}, u32[]{:S(2)}, u32[]{:S(2)}) async-start(f32[32,4,16,128]{3,2,1,0:T(8,128)} %copy.13), calls=%async_computation | async-start | bytes 2097152 | tf_op jit(solution)/shard_map/all_to_all | solution.py:332
  61.6 1.2 fusion.1
  62.8 1.6 copy.19
  64.4 22.5 %all-to-all-done = f32[32,4,16,128]{3,2,1,0:T(8,128)S(1)} async-done(((f32[32,4,16,128]{3,2,1,0:T(8,128)}), f32[32,4,16,128]{3,2,1,0:T(8,128)S(1)}, u32[]{:S(2)}, u32[]{:S(2)}) %all-to-all-start) | async-done | bytes 1048608 | tf_op jit(solution)/shard_map/all_to_all | solution.py:332
  86.9 4.6 %all-to-all-start.2 = ((f32[32,4,16,128]{3,2,1,0:T(8,128)}), f32[32,4,16,128]{3,2,1,0:T(8,128)S(1)}, u32[]{:S(2)}, u32[]{:S(2)}) async-start(f32[32,4,16,128]{3,2,1,0:T(8,128)} %copy.19), calls=%async_computation.2 | async-start | bytes 2097152 | tf_op jit(solution)/shard_map/all_to_all | solution.py:332
  91.6 0.8 broadcast_add_fusion
  92.4 0.8 copy.40
  93.2 0.8 reshape.120
  94.0 1.6 fusion.34
  95.7 1.8 fusion.5
  97.5 1.6 convolution_bitcast_fusion.2
  99.1 1.9 %fusion.30 = f32[4,256,256]{2,1,0:T(8,128)S(1)} fusion(f32[4,256,256]{1,2,0:T(8,128)S(1)} %convolution_bitcast_fusion.2), kind=kOutput, calls=%fused_computation.47 | convolution fusion | flops 403636224 | bytes 2097152 | tf_op jit(solution)/shard_map/kz,xyz->xyk/dot_general | solution.py:32
  101.0 0.5 reshape.121
  101.6 1.7 copy.17
  103.2 13.5 %all-to-all-done.2 = f32[32,4,16,128]{3,2,1,0:T(8,128)S(1)} async-done(((f32[32,4,16,128]{3,2,1,0:T(8,128)}), f32[32,4,16,128]{3,2,1,0:T(8,128)S(1)}, u32[]{:S(2)}, u32[]{:S(2)}) %all-to-all-start.2) | async-done | bytes 1048608 | tf_op jit(solution)/shard_map/all_to_all | solution.py:332
  116.8 4.6 %all-to-all-start.1 = ((f32[32,4,16,128]{3,1,2,0:T(4,128)}), f32[32,4,16,128]{3,1,2,0:T(4,128)S(1)}, u32[]{:S(2)}, u32[]{:S(2)}) async-start(f32[32,4,16,128]{3,1,2,0:T(4,128)} %bitcast.18), calls=%async_computation.1 | async-start | bytes 2097152 | tf_op jit(solution)/shard_map/all_to_all | solution.py:349
  121.4 0.8 copy.39
  122.2 0.8 reshape.124
  123.1 1.6 fusion.28
  124.7 1.8 fusion.6
  126.5 1.6 convolution_bitcast_fusion
  128.1 1.9 %fusion.24 = f32[4,256,256]{2,1,0:T(8,128)S(1)} fusion(f32[4,256,256]{1,2,0:T(8,128)S(1)} %convolution_bitcast_fusion), kind=kOutput, calls=%fused_computation.41 | convolution fusion | flops 403636224 | bytes 2097152 | tf_op jit(solution)/shard_map/kz,xyz->xyk/dot_general | solution.py:32
  130.0 0.5 reshape.125
  130.6 1.7 copy.23
  132.3 14.3 %all-to-all-done.1 = f32[32,4,16,128]{3,1,2,0:T(4,128)S(1)} async-done(((f32[32,4,16,128]{3,1,2,0:T(4,128)}), f32[32,4,16,128]{3,1,2,0:T(4,128)S(1)}, u32[]{:S(2)}, u32[]{:S(2)}) %all-to-all-start.1) | async-done | bytes 1048608 | tf_op jit(solution)/shard_map/all_to_all | solution.py:349
  146.6 4.7 %all-to-all-start.3 = ((f32[32,4,16,128]{3,1,2,0:T(4,128)}), f32[32,4,16,128]{3,1,2,0:T(4,128)}, u32[]{:S(2)}, u32[]{:S(2)}) async-start(f32[32,4,16,128]{3,1,2,0:T(4,128)} %bitcast.29), calls=%async_computation.3 | async-start | bytes 2097152 | tf_op jit(solution)/shard_map/all_to_all | solution.py:349
  151.3 6.8 %shard_map.71 = f32[2,16,128,256]{3,2,1,0:T(8,128)} custom-call(f32[2,16,128,256]{3,2,1,0:T(8,128)} %get-tuple-element.25.w_ref.w_prev.w_next, f32[2,16,128,256]{3,2,1,0:T(8,128)} %get-tuple-element.25.w_ref.w_prev.w_next, f32[2,16,128,256]{3,2,1,0:T(8,128)} %get-tuple-element.25.w_ref.w_prev.w_next, f32[2,128,256]{2,1,0:T(8,128)} %copy-done.3, ...), custom_call_target="tpu_custom_call" | custom-call | tf_op jit(solution)/shard_map/pallas_call | solution.py:299
  158.1 1.5 fusion.16
  159.6 17.0 %all-to-all-done.3 = f32[32,4,16,128]{3,1,2,0:T(4,128)} async-done(((f32[32,4,16,128]{3,1,2,0:T(4,128)}), f32[32,4,16,128]{3,1,2,0:T(4,128)}, u32[]{:S(2)}, u32[]{:S(2)}) %all-to-all-start.3) | async-done | bytes 1048608 | tf_op jit(solution)/shard_map/all_to_all | solution.py:349
  176.6 4.0 %fusion = f32[16,128,256]{2,1,0:T(8,128)} fusion(f32[16,128,256,1]{2,1,3,0:T(8,128)S(1)} %fusion.16, f32[32,4,16,128]{3,1,2,0:T(4,128)} %all-to-all-done.3, f32[32,2,4,256]{3,0,2,1:T(8,128)S(1)} %sine_add_fusion.1), kind=kOutput, calls=%fused_computation.1 | convolution fusion | flops 403701760 | bytes 5373952 | tf_op jit(solution)/shard_map/sxn,sxyz->yzn/dot_general | solution.py:32
  (23 shorter events, 0.1 us)
Async XLA Ops:
  5.2 15.9 %collective-permute-start = (f32[6,128,256]{2,1,0:T(8,128)}, f32[6,128,256]{2,1,0:T(8,128)S(1)}, u32[]{:S(2)}, u32[]{:S(2)}) collective-permute-start(f32[6,128,256]{2,1,0:T(8,128)} %get-tuple-element.21), channel_id=1, source_target_pairs={{0,2},{2,4},{4,6},{6,8},{8,10},{10,12},{12,14},{14,16},{16,18},{18... | collective-permute-start | bytes 2359304 | tf_op jit(solution)/shard_map/ppermute | solution.py:251
  5.2 15.8 %collective-permute-start.1 = (f32[6,128,256]{2,1,0:T(8,128)}, f32[6,128,256]{2,1,0:T(8,128)S(1)}, u32[]{:S(2)}, u32[]{:S(2)}) collective-permute-start(f32[6,128,256]{2,1,0:T(8,128)} %get-tuple-element.22), channel_id=1, source_target_pairs={{2,0},{4,2},{6,4},{8,6},{10,8},{12,10},{14,12},{16,14},{18,16},{20... | collective-permute-start | bytes 2359304 | tf_op jit(solution)/shard_map/ppermute | solution.py:251
  9.0 11.2 %collective-permute-start.2 = (f32[2,6,16,1,256]{4,3,2,1,0:T(1,128)S(1)}, f32[2,6,16,1,256]{4,3,2,1,0:T(1,128)S(1)}, u32[]{:S(2)}, u32[]{:S(2)}) collective-permute-start(f32[2,6,16,1,256]{4,3,2,1,0:T(1,128)S(1)} %pad_maximum_fusion), channel_id=1, source_target_pairs={{0,1},{1,0},{2,3},{3,2},{4,5},{5,4},{6,7},{7,6},{8,9},{9,8},{10,11... | collective-permute-start | bytes 589832 | tf_op jit(solution)/shard_map/ppermute | solution.py:248
  21.0 1.0 copy-start.1
  21.1 1.2 copy-start.2
  39.7 8.7 %collective-permute-start.5 = (f32[2,2,16,1,256]{4,3,2,1,0:T(1,128)S(1)}, f32[2,2,16,1,256]{4,3,2,1,0:T(1,128)S(1)}, u32[]{:S(2)}, u32[]{:S(2)}) collective-permute-start(f32[2,2,16,1,256]{4,3,2,1,0:T(1,128)S(1)} %pad_maximum_fusion.1), channel_id=1, source_target_pairs={{0,1},{1,0},{2,3},{3,2},{4,5},{5,4},{6,7},{7,6},{8,9},{9,8},{10,11... | collective-permute-start | bytes 196616 | tf_op jit(solution)/shard_map/ppermute | solution.py:248
  40.3 8.7 %collective-permute-start.3 = (f32[2,128,256]{2,1,0:T(8,128)}, f32[2,128,256]{2,1,0:T(8,128)S(1)}, u32[]{:S(2)}, u32[]{:S(2)}) collective-permute-start(f32[2,128,256]{2,1,0:T(8,128)} %get-tuple-element.26), channel_id=1, source_target_pairs={{0,2},{2,4},{4,6},{6,8},{8,10},{10,12},{12,14},{14,16},{16,18},{18... | collective-permute-start | bytes 786440 | tf_op jit(solution)/shard_map/ppermute | solution.py:251
  45.6 4.3 %collective-permute-start.4 = (f32[2,128,256]{2,1,0:T(8,128)}, f32[2,128,256]{2,1,0:T(8,128)S(1)}, u32[]{:S(2)}, u32[]{:S(2)}) collective-permute-start(f32[2,128,256]{2,1,0:T(8,128)} %get-tuple-element.27), channel_id=1, source_target_pairs={{2,0},{4,2},{6,4},{8,6},{10,8},{12,10},{14,12},{16,14},{18,16},{20... | collective-permute-start | bytes 786440 | tf_op jit(solution)/shard_map/ppermute | solution.py:251
  49.0 0.9 copy-start.3
  49.8 0.7 copy-start.4
  50.5 11.1 %copy-start = (f32[16,128,256]{2,1,0:T(8,128)S(1)}, f32[16,128,256]{2,1,0:T(8,128)}, u32[]{:S(2)}) copy-start(f32[16,128,256]{2,1,0:T(8,128)} %get-tuple-element.30) | copy-start | bytes 6291460
  52.1 34.8 %all-to-all-start = ((f32[32,4,16,128]{3,2,1,0:T(8,128)}), f32[32,4,16,128]{3,2,1,0:T(8,128)S(1)}, u32[]{:S(2)}, u32[]{:S(2)}) async-start(f32[32,4,16,128]{3,2,1,0:T(8,128)} %copy.13), calls=%async_computation | async-start | bytes 2097152 | tf_op jit(solution)/shard_map/all_to_all | solution.py:332
  86.9 29.9 %all-to-all-start.2 = ((f32[32,4,16,128]{3,2,1,0:T(8,128)}), f32[32,4,16,128]{3,2,1,0:T(8,128)S(1)}, u32[]{:S(2)}, u32[]{:S(2)}) async-start(f32[32,4,16,128]{3,2,1,0:T(8,128)} %copy.19), calls=%async_computation.2 | async-start | bytes 2097152 | tf_op jit(solution)/shard_map/all_to_all | solution.py:332
  94.0 1.7 copy-start.5
  116.8 29.9 %all-to-all-start.1 = ((f32[32,4,16,128]{3,1,2,0:T(4,128)}), f32[32,4,16,128]{3,1,2,0:T(4,128)S(1)}, u32[]{:S(2)}, u32[]{:S(2)}) async-start(f32[32,4,16,128]{3,1,2,0:T(4,128)} %bitcast.18), calls=%async_computation.1 | async-start | bytes 2097152 | tf_op jit(solution)/shard_map/all_to_all | solution.py:349
  123.1 1.7 copy-start.6
  146.6 30.0 %all-to-all-start.3 = ((f32[32,4,16,128]{3,1,2,0:T(4,128)}), f32[32,4,16,128]{3,1,2,0:T(4,128)}, u32[]{:S(2)}, u32[]{:S(2)}) async-start(f32[32,4,16,128]{3,1,2,0:T(4,128)} %bitcast.29), calls=%async_computation.3 | async-start | bytes 2097152 | tf_op jit(solution)/shard_map/all_to_all | solution.py:349

commit v8 on v6

--- a/solution.py
+++ b/solution.py
@@ -272,7 +272,13 @@
         out_specs=six_specs,
         out_shape=six_shapes,
     )(*[a for a in inputs for _ in range(4)])
-    halos = send_edges(*edges)
+    count_y = lax.axis_size("gy")
+    up = [(i, (i + 1) % count_y) for i in range(count_y)]
+    down = [(j, i) for i, j in up]
+    mag_low = lax.ppermute(jnp.concatenate([mag_middle[:, length_y - 1], mag_start[:, length_y - 1]]), "gy", up)
+    mag_high = lax.ppermute(jnp.concatenate([mag_middle[:, 0], mag_start[:, 0]]), "gy", down)
+    w_low, w_high, z_low, z_high = send_edges(edges[0][4:], edges[1][4:], edges[2], edges[3])
+    halos = [jnp.concatenate([mag_low, w_low]), jnp.concatenate([mag_high, w_high]), z_low, z_high]
     factor, w_first = pl.pallas_call(
         functools.partial(factor_kernel, rows=rows),
         grid=grid,

time: 183 us -> 186 us (1.016)
  local copies, waits for them, and re-layouts: 14.3 us -> 17.4 us
  starting transfers between devices: 33.5 us -> 31.1 us
    ppermute x2, starting transfers between devices: 5.38 us -> 1.64 us  [send_edges(): lax.ppermute(last, axis, up)]
    concatenate x0 -> x4, other arithmetic: none -> 2.04 us  [the longest x1 1.03 us: backward_sections(): jnp.concatenate([mag_low, w_low])]
    slice x0 -> x2, local copies, waits for them, and re-layouts: none -> 1.98 us  [the longest x1 1.01 us: backward_sections(): edges[1][4:]]
  transfers between devices with their start and end apart: 10 -> 12, of which waited for: 5 -> 5; matrix products, arithmetic and copies ran while one was open for 18% -> 20% of each run, Pallas kernels for 9% -> 11%
where the time goes in v8:
time: 186 us; the launch traced here: 183 us
  waiting for transfers between devices  68.3 us (37%)
  Pallas kernels  36.1 us (19%)
  starting transfers between devices  31.1 us (17%)
  matrix products  23.2 us (12%)
  local copies, waits for them, and re-layouts  17.4 us (9%)
  other arithmetic  5.7 us (3%)
    all_to_all x2, waiting for transfers between devices, dipole_adjoint(): sent.append(lax.all_to_all(spec, ('gy', 'gz'), 0, 0, tiled=True))  36 us
    all_to_all x2, waiting for transfers between devices, dipole_adjoint(): spec = lax.all_to_all(spec, ('gy', 'gz'), 0, 0, tiled=True)  31.3 us
    dot_general x12, matrix products, along(): return jnp.einsum(spec, table, values, precision=lax.Precision.HIGH)  23.2 us
    pallas_call x1, Pallas kernels, backward_sections(): pl.pallas_call(functools.partial(first_kernel, rows=rows), grid=grid, in_...  16.1 us
    all_to_all x2, starting transfers between devices, dipole_adjoint(): sent.append(lax.all_to_all(spec, ('gy', 'gz'), 0, 0, tiled=True))  13.8 us
    all_to_all x2, starting transfers between devices, dipole_adjoint(): spec = lax.all_to_all(spec, ('gy', 'gz'), 0, 0, tiled=True)  9.27 us
    pallas_call x1, Pallas kernels, backward_sections(): pl.pallas_call(functools.partial(factor_kernel, rows=rows), grid=grid, in...  8.58 us
    pallas_call x1, Pallas kernels, finish_lambda(): pl.pallas_call(functools.partial(second_kernel, rows=rows), grid=grid, in...  6.88 us
  transfers between devices with their start and end apart: 12, of which 5 were waited for; matrix products, arithmetic and copies ran while one was open for 20% of the time, Pallas kernels for 11%

profile of v8, /device:TPU:16, one launch (start us, length us, event | category | flops | bytes accessed | tf_op | source)
XLA Modules:
  0.0 182.9 jit_solution(17391423284576835156)
XLA Ops:
  0.6 1.3 slice_bitcast_fusion
  2.0 4.5 %shard_map.69 = (f32[6,128,256]{2,1,0:T(8,128)}, f32[6,128,256]{2,1,0:T(8,128)}, f32[6,16,1,256]{3,2,1,0:T(1,128)}, f32[6,16,1,256]{3,2,1,0:T(1,128)}) custom-call(f32[2,16,128,256]{3,2,1,0:T(8,128)} %refs_2_.3, f32[2,16,128,256]{3,2,1,0:T(8,128)} %refs_2_.3, f32[2,16,128,256]{3,2,1,0:T(8,128)} %refs_2_.3, f32[2,16,128,256]{3,2,1,0:T(8,128)} %refs_2_.3, ...), custom_call_target="tpu_custom_call" | custom-call | tf_op jit(solution)/shard_map/pallas_call | solution.py:268
  6.6 1.0 slice.44
  7.6 1.6 collective-permute-start.1
  9.3 1.1 collective-permute-start.2
  10.4 1.0 slice.47
  11.9 0.9 pad_maximum_fusion.4
  12.8 1.5 collective-permute-start.4
  14.3 1.1 sine_add_fusion.1
  15.4 8.6 %shard_map.68 = (f32[2,16,128,256]{3,2,1,0:T(8,128)}, f32[2,16,128,256]{3,2,1,0:T(8,128)}) custom-call(f32[2,16,128,256]{3,2,1,0:T(8,128)} %refs_11_.1, f32[16,128,256]{2,1,0:T(8,128)} %refs_15_.1, s32[16,128,256]{2,1,0:T(8,128)} %refs_19_.1), custom_call_target="tpu_custom_call" | custom-call | tf_op jit(solution)/shard_map/pallas_call | solution.py:282
  24.0 1.8 slice_bitcast_fusion.4
  25.7 1.0 pad_maximum_fusion.refs_10_
  26.8 0.9 pad_maximum_fusion.1.refs_11_
  27.7 16.1 %shard_map.70 = (f32[16,128,256]{2,1,0:T(8,128)}, f32[2,16,128,256]{3,2,1,0:T(8,128)}, f32[2,128,256]{2,1,0:T(8,128)}, f32[2,128,256]{2,1,0:T(8,128)}, f32[2,16,...) custom-call(f32[2,16,128,256]{3,2,1,0:T(8,128)} %refs_2_.3, f32[2,16,128,256]{3,2,1,0:T(8,128)} %refs_2_.3, ...), custom_call_target="tpu_custom_call" | custom-call | tf_op jit(solution)/shard_map/pallas_call | solution.py:289
  43.8 0.8 pad_maximum_fusion.5
  45.3 2.6 %collective-permute-start.6 = (f32[2,128,256]{2,1,0:T(8,128)}, f32[2,128,256]{2,1,0:T(8,128)S(1)}, u32[]{:S(2)}, u32[]{:S(2)}) collective-permute-start(f32[2,128,256]{2,1,0:T(8,128)} %get-tuple-element.27), channel_id=1, source_target_pairs={{2,0},{4,2},{6,4},{8,6},{10,8},{12,10},{14,12},{16,14},{18,16},{20... | collective-permute-start | bytes 786440 | tf_op jit(solution)/shard_map/ppermute | solution.py:251
  47.9 2.8 %fusion.3 = f32[32,4,16,128]{3,0,2,1:T(8,128)S(1)} fusion(f32[16,128,256]{2,1,0:T(8,128)} %get-tuple-element.30, f32[32,2,4,256]{3,0,2,1:T(8,128)S(1)} %sine_add_fusion.1), kind=kOutput, calls=%fused_computation.4 | convolution fusion | flops 402653184 | bytes 3276800 | tf_op jit(solution)/shard_map/sxn,yzn->sxyz/dot_general | solution.py:32
  51.3 0.9 collective-permute-done.5.y_low_ref
  52.3 0.7 copy-done.1
  53.1 1.6 copy.25
  54.7 9.2 %all-to-all-start = ((f32[32,4,16,128]{3,2,1,0:T(8,128)}), f32[32,4,16,128]{3,2,1,0:T(8,128)S(1)}, u32[]{:S(2)}, u32[]{:S(2)}) async-start(f32[32,4,16,128]{3,2,1,0:T(8,128)} %copy.25), calls=%async_computation | async-start | bytes 2097152 | tf_op jit(solution)/shard_map/all_to_all | solution.py:338
  63.9 1.2 fusion.1
  65.1 1.6 copy.31
  66.7 22.5 %all-to-all-done = f32[32,4,16,128]{3,2,1,0:T(8,128)S(1)} async-done(((f32[32,4,16,128]{3,2,1,0:T(8,128)}), f32[32,4,16,128]{3,2,1,0:T(8,128)S(1)}, u32[]{:S(2)}, u32[]{:S(2)}) %all-to-all-start) | async-done | bytes 1048608 | tf_op jit(solution)/shard_map/all_to_all | solution.py:338
  89.2 4.6 %all-to-all-start.2 = ((f32[32,4,16,128]{3,2,1,0:T(8,128)}), f32[32,4,16,128]{3,2,1,0:T(8,128)S(1)}, u32[]{:S(2)}, u32[]{:S(2)}) async-start(f32[32,4,16,128]{3,2,1,0:T(8,128)} %copy.31), calls=%async_computation.2 | async-start | bytes 2097152 | tf_op jit(solution)/shard_map/all_to_all | solution.py:338
  93.8 0.8 broadcast_add_fusion
  94.6 0.8 copy.56
  95.4 0.8 reshape.120
  96.3 1.6 fusion.34
  98.0 1.8 fusion.5
  99.7 1.6 convolution_bitcast_fusion.2
  101.4 1.9 %fusion.30 = f32[4,256,256]{2,1,0:T(8,128)S(1)} fusion(f32[4,256,256]{1,2,0:T(8,128)S(1)} %convolution_bitcast_fusion.2), kind=kOutput, calls=%fused_computation.51 | convolution fusion | flops 403636224 | bytes 2097152 | tf_op jit(solution)/shard_map/kz,xyz->xyk/dot_general | solution.py:32
  103.8 1.7 copy.29
  105.5 13.5 %all-to-all-done.2 = f32[32,4,16,128]{3,2,1,0:T(8,128)S(1)} async-done(((f32[32,4,16,128]{3,2,1,0:T(8,128)}), f32[32,4,16,128]{3,2,1,0:T(8,128)S(1)}, u32[]{:S(2)}, u32[]{:S(2)}) %all-to-all-start.2) | async-done | bytes 1048608 | tf_op jit(solution)/shard_map/all_to_all | solution.py:338
  119.0 4.6 %all-to-all-start.1 = ((f32[32,4,16,128]{3,1,2,0:T(4,128)}), f32[32,4,16,128]{3,1,2,0:T(4,128)S(1)}, u32[]{:S(2)}, u32[]{:S(2)}) async-start(f32[32,4,16,128]{3,1,2,0:T(4,128)} %bitcast.22), calls=%async_computation.1 | async-start | bytes 2097152 | tf_op jit(solution)/shard_map/all_to_all | solution.py:355
  123.7 0.8 copy.55
  124.5 0.8 reshape.124
  125.3 1.6 fusion.28
  127.0 1.8 fusion.6
  128.8 1.6 convolution_bitcast_fusion
  130.4 1.9 %fusion.24 = f32[4,256,256]{2,1,0:T(8,128)S(1)} fusion(f32[4,256,256]{1,2,0:T(8,128)S(1)} %convolution_bitcast_fusion), kind=kOutput, calls=%fused_computation.45 | convolution fusion | flops 403636224 | bytes 2097152 | tf_op jit(solution)/shard_map/kz,xyz->xyk/dot_general | solution.py:32
  132.9 1.7 copy.35
  134.5 14.4 %all-to-all-done.1 = f32[32,4,16,128]{3,1,2,0:T(4,128)S(1)} async-done(((f32[32,4,16,128]{3,1,2,0:T(4,128)}), f32[32,4,16,128]{3,1,2,0:T(4,128)S(1)}, u32[]{:S(2)}, u32[]{:S(2)}) %all-to-all-start.1) | async-done | bytes 1048608 | tf_op jit(solution)/shard_map/all_to_all | solution.py:355
  148.9 4.7 %all-to-all-start.3 = ((f32[32,4,16,128]{3,1,2,0:T(4,128)}), f32[32,4,16,128]{3,1,2,0:T(4,128)}, u32[]{:S(2)}, u32[]{:S(2)}) async-start(f32[32,4,16,128]{3,1,2,0:T(4,128)} %bitcast.33), calls=%async_computation.3 | async-start | bytes 2097152 | tf_op jit(solution)/shard_map/all_to_all | solution.py:355
  153.6 6.9 %shard_map.71 = f32[2,16,128,256]{3,2,1,0:T(8,128)} custom-call(f32[2,16,128,256]{3,2,1,0:T(8,128)} %get-tuple-element.25.w_ref.w_prev.w_next, f32[2,16,128,256]{3,2,1,0:T(8,128)} %get-tuple-element.25.w_ref.w_prev.w_next, f32[2,16,128,256]{3,2,1,0:T(8,128)} %get-tuple-element.25.w_ref.w_prev.w_next, f32[2,128,256]{2,1,0:T(8,128)} %copy-done.1, ...), custom_call_target="tpu_custom_call" | custom-call | tf_op jit(solution)/shard_map/pallas_call | solution.py:305
  160.5 1.5 fusion.16
  161.9 16.9 %all-to-all-done.3 = f32[32,4,16,128]{3,1,2,0:T(4,128)} async-done(((f32[32,4,16,128]{3,1,2,0:T(4,128)}), f32[32,4,16,128]{3,1,2,0:T(4,128)}, u32[]{:S(2)}, u32[]{:S(2)}) %all-to-all-start.3) | async-done | bytes 1048608 | tf_op jit(solution)/shard_map/all_to_all | solution.py:355
  178.9 4.0 %fusion = f32[16,128,256]{2,1,0:T(8,128)} fusion(f32[16,128,256,1]{2,1,3,0:T(8,128)S(1)} %fusion.16, f32[32,4,16,128]{3,1,2,0:T(4,128)} %all-to-all-done.3, f32[32,2,4,256]{3,0,2,1:T(8,128)S(1)} %sine_add_fusion.1), kind=kOutput, calls=%fused_computation.1 | convolution fusion | flops 403701760 | bytes 5373952 | tf_op jit(solution)/shard_map/sxn,sxyz->yzn/dot_general | solution.py:32
  (34 shorter events, 3.2 us)
Async XLA Ops:
  2.0 23.8 %collective-permute-start = (f32[4,128,256]{2,1,0:T(8,128)S(1)}, f32[4,128,256]{2,1,0:T(8,128)S(1)}, u32[]{:S(2)}, u32[]{:S(2)}) collective-permute-start(f32[4,128,256]{2,1,0:T(8,128)S(1)} %pad_maximum_fusion.2), channel_id=1, source_target_pairs={{0,2},{2,4},{4,6},{6,8},{8,10},{10,12},{12,14},{14,16},{16,18},{18... | collective-permute-start | bytes 1572872 | tf_op jit(solution)/shard_map/ppermute | solution.py:278
  6.6 5.3 %copy-start.5 = (f32[6,16,1,256]{3,2,1,0:T(1,128)S(1)}, f32[6,16,1,256]{3,2,1,0:T(1,128)}, u32[]{:S(2)}) copy-start(f32[6,16,1,256]{3,2,1,0:T(1,128)} %get-tuple-element.24) | copy-start | bytes 294916
  6.6 5.3 %copy-start.6 = (f32[6,16,1,256]{3,2,1,0:T(1,128)S(1)}, f32[6,16,1,256]{3,2,1,0:T(1,128)}, u32[]{:S(2)}) copy-start(f32[6,16,1,256]{3,2,1,0:T(1,128)} %get-tuple-element.23) | copy-start | bytes 294916
  7.6 18.1 %collective-permute-start.1 = (f32[2,128,256]{2,1,0:T(8,128)S(1)}, f32[2,128,256]{2,1,0:T(8,128)S(1)}, u32[]{:S(2)}, u32[]{:S(2)}) collective-permute-start(f32[2,128,256]{2,1,0:T(8,128)S(1)} %slice.44), channel_id=1, source_target_pairs={{0,2},{2,4},{4,6},{6,8},{8,10},{10,12},{12,14},{14,16},{16,18},{18... | collective-permute-start | bytes 786440 | tf_op jit(solution)/shard_map/ppermute | solution.py:251
  9.3 17.5 %collective-permute-start.2 = (f32[4,128,256]{2,1,0:T(8,128)S(1)}, f32[4,128,256]{2,1,0:T(8,128)S(1)}, u32[]{:S(2)}, u32[]{:S(2)}) collective-permute-start(f32[4,128,256]{2,1,0:T(8,128)S(1)} %pad_maximum_fusion.3), channel_id=1, source_target_pairs={{2,0},{4,2},{6,4},{8,6},{10,8},{12,10},{14,12},{16,14},{18,16},{20... | collective-permute-start | bytes 1572872 | tf_op jit(solution)/shard_map/ppermute | solution.py:279
  11.4 15.4 %collective-permute-start.3 = (f32[2,128,256]{2,1,0:T(8,128)S(1)}, f32[2,128,256]{2,1,0:T(8,128)S(1)}, u32[]{:S(2)}, u32[]{:S(2)}) collective-permute-start(f32[2,128,256]{2,1,0:T(8,128)S(1)} %slice.47), channel_id=1, source_target_pairs={{2,0},{4,2},{6,4},{8,6},{10,8},{12,10},{14,12},{16,14},{18,16},{20... | collective-permute-start | bytes 786440 | tf_op jit(solution)/shard_map/ppermute | solution.py:251
  12.8 11.2 %collective-permute-start.4 = (f32[2,6,16,1,256]{4,3,2,1,0:T(1,128)}, f32[2,6,16,1,256]{4,3,2,1,0:T(1,128)}, u32[]{:S(2)}, u32[]{:S(2)}) collective-permute-start(f32[2,6,16,1,256]{4,3,2,1,0:T(1,128)} %pad_maximum_fusion.4), channel_id=1, source_target_pairs={{0,1},{1,0},{2,3},{3,2},{4,5},{5,4},{6,7},{7,6},{8,9},{9,8},{10,11... | collective-permute-start | bytes 589832 | tf_op jit(solution)/shard_map/ppermute | solution.py:248
  44.7 6.0 %collective-permute-start.7 = (f32[2,2,16,1,256]{4,3,2,1,0:T(1,128)S(1)}, f32[2,2,16,1,256]{4,3,2,1,0:T(1,128)S(1)}, u32[]{:S(2)}, u32[]{:S(2)}) collective-permute-start(f32[2,2,16,1,256]{4,3,2,1,0:T(1,128)S(1)} %pad_maximum_fusion.5), channel_id=1, source_target_pairs={{0,1},{1,0},{2,3},{3,2},{4,5},{5,4},{6,7},{7,6},{8,9},{9,8},{10,11... | collective-permute-start | bytes 196616 | tf_op jit(solution)/shard_map/ppermute | solution.py:248
  45.3 7.0 %collective-permute-start.5 = (f32[2,128,256]{2,1,0:T(8,128)}, f32[2,128,256]{2,1,0:T(8,128)S(1)}, u32[]{:S(2)}, u32[]{:S(2)}) collective-permute-start(f32[2,128,256]{2,1,0:T(8,128)} %get-tuple-element.26), channel_id=1, source_target_pairs={{0,2},{2,4},{4,6},{6,8},{8,10},{10,12},{12,14},{14,16},{16,18},{18... | collective-permute-start | bytes 786440 | tf_op jit(solution)/shard_map/ppermute | solution.py:251
  45.3 7.0 %collective-permute-start.6 = (f32[2,128,256]{2,1,0:T(8,128)}, f32[2,128,256]{2,1,0:T(8,128)S(1)}, u32[]{:S(2)}, u32[]{:S(2)}) collective-permute-start(f32[2,128,256]{2,1,0:T(8,128)} %get-tuple-element.27), channel_id=1, source_target_pairs={{2,0},{4,2},{6,4},{8,6},{10,8},{12,10},{14,12},{16,14},{18,16},{20... | collective-permute-start | bytes 786440 | tf_op jit(solution)/shard_map/ppermute | solution.py:251
  52.3 0.7 copy-start.1
  52.3 0.8 copy-start.2
  53.1 10.8 %copy-start = (f32[16,128,256]{2,1,0:T(8,128)S(1)}, f32[16,128,256]{2,1,0:T(8,128)}, u32[]{:S(2)}) copy-start(f32[16,128,256]{2,1,0:T(8,128)} %get-tuple-element.30) | copy-start | bytes 6291460
  54.7 34.5 %all-to-all-start = ((f32[32,4,16,128]{3,2,1,0:T(8,128)}), f32[32,4,16,128]{3,2,1,0:T(8,128)S(1)}, u32[]{:S(2)}, u32[]{:S(2)}) async-start(f32[32,4,16,128]{3,2,1,0:T(8,128)} %copy.25), calls=%async_computation | async-start | bytes 2097152 | tf_op jit(solution)/shard_map/all_to_all | solution.py:338
  89.2 29.9 %all-to-all-start.2 = ((f32[32,4,16,128]{3,2,1,0:T(8,128)}), f32[32,4,16,128]{3,2,1,0:T(8,128)S(1)}, u32[]{:S(2)}, u32[]{:S(2)}) async-start(f32[32,4,16,128]{3,2,1,0:T(8,128)} %copy.31), calls=%async_computation.2 | async-start | bytes 2097152 | tf_op jit(solution)/shard_map/all_to_all | solution.py:338
  96.3 1.7 copy-start.3
  119.0 29.9 %all-to-all-start.1 = ((f32[32,4,16,128]{3,1,2,0:T(4,128)}), f32[32,4,16,128]{3,1,2,0:T(4,128)S(1)}, u32[]{:S(2)}, u32[]{:S(2)}) async-start(f32[32,4,16,128]{3,1,2,0:T(4,128)} %bitcast.22), calls=%async_computation.1 | async-start | bytes 2097152 | tf_op jit(solution)/shard_map/all_to_all | solution.py:355
  125.3 1.7 copy-start.4
  148.9 30.0 %all-to-all-start.3 = ((f32[32,4,16,128]{3,1,2,0:T(4,128)}), f32[32,4,16,128]{3,1,2,0:T(4,128)}, u32[]{:S(2)}, u32[]{:S(2)}) async-start(f32[32,4,16,128]{3,1,2,0:T(4,128)} %bitcast.33), calls=%async_computation.3 | async-start | bytes 2097152 | tf_op jit(solution)/shard_map/all_to_all | solution.py:355

commit v9 on v6

--- a/solution.py
+++ b/solution.py
@@ -265,10 +265,12 @@
     edge_shapes, edge_specs = edge_outputs(2, length_y, length_z, length_x, rows)
     six_shapes, six_specs = edge_outputs(6, length_y, length_z, length_x, rows)
     inputs = (mag_middle, mag_start, adjoint_end, phase, labels)
+    edge_rows = length_y
+    six_shapes, six_specs = edge_outputs(6, length_y, length_z, length_x, edge_rows)
     edges = pl.pallas_call(
-        functools.partial(edges_kernel, rows=rows),
-        grid=grid,
-        in_specs=[s for a in inputs for s in edge_specs_of(a.ndim, length_y, length_z, length_x, rows)],
+        functools.partial(edges_kernel, rows=edge_rows),
+        grid=(1,),
+        in_specs=[s for a in inputs for s in edge_specs_of(a.ndim, length_y, length_z, length_x, edge_rows)],
         out_specs=six_specs,
         out_shape=six_shapes,
     )(*[a for a in inputs for _ in range(4)])

time: 183 us -> 183 us (level)
  no operation moved by 1% of the time
where the time goes in v9:
time: 183 us; the launch traced here: 180 us
  waiting for transfers between devices  68.2 us (37%)
  Pallas kernels  36.1 us (20%)
  starting transfers between devices  33.5 us (18%)
  matrix products  23.2 us (13%)
  local copies, waits for them, and re-layouts  14.3 us (8%)
  other arithmetic  3.93 us (2%)
    all_to_all x2, waiting for transfers between devices, dipole_adjoint(): sent.append(lax.all_to_all(spec, ('gy', 'gz'), 0, 0, tiled=True))  36 us
    all_to_all x2, waiting for transfers between devices, dipole_adjoint(): spec = lax.all_to_all(spec, ('gy', 'gz'), 0, 0, tiled=True)  31.3 us
    dot_general x12, matrix products, along(): return jnp.einsum(spec, table, values, precision=lax.Precision.HIGH)  23.2 us
    pallas_call x1, Pallas kernels, backward_sections(): pl.pallas_call(functools.partial(first_kernel, rows=rows), grid=grid, in_...  16.1 us
    all_to_all x2, starting transfers between devices, dipole_adjoint(): sent.append(lax.all_to_all(spec, ('gy', 'gz'), 0, 0, tiled=True))  14.1 us
    all_to_all x2, starting transfers between devices, dipole_adjoint(): spec = lax.all_to_all(spec, ('gy', 'gz'), 0, 0, tiled=True)  9.27 us
    pallas_call x1, Pallas kernels, backward_sections(): pl.pallas_call(functools.partial(factor_kernel, rows=rows), grid=grid, in...  8.52 us
    pallas_call x1, Pallas kernels, finish_lambda(): pl.pallas_call(functools.partial(second_kernel, rows=rows), grid=grid, in...  6.88 us
  transfers between devices with their start and end apart: 10, of which 5 were waited for; matrix products, arithmetic and copies ran while one was open for 18% of the time, Pallas kernels for 9%

profile of v9, /device:TPU:16, one launch (start us, length us, event | category | flops | bytes accessed | tf_op | source)
XLA Modules:
  0.0 180.2 jit_solution(11350880775437290860)
XLA Ops:
  0.6 4.6 %shard_map.69 = (f32[6,128,256]{2,1,0:T(8,128)}, f32[6,128,256]{2,1,0:T(8,128)}, f32[6,16,1,256]{3,2,1,0:T(1,128)}, f32[6,16,1,256]{3,2,1,0:T(1,128)}) custom-call(f32[2,16,128,256]{3,2,1,0:T(8,128)} %refs_2_.3, f32[2,16,128,256]{3,2,1,0:T(8,128)} %refs_2_.3, f32[2,16,128,256]{3,2,1,0:T(8,128)} %refs_2_.3, f32[2,16,128,256]{3,2,1,0:T(8,128)} %refs_2_.3, ...), custom_call_target="tpu_custom_call" | custom-call | tf_op jit(solution)/shard_map/pallas_call | solution.py:270
  5.3 2.6 %collective-permute-start.1 = (f32[6,128,256]{2,1,0:T(8,128)}, f32[6,128,256]{2,1,0:T(8,128)S(1)}, u32[]{:S(2)}, u32[]{:S(2)}) collective-permute-start(f32[6,128,256]{2,1,0:T(8,128)} %get-tuple-element.22), channel_id=1, source_target_pairs={{2,0},{4,2},{6,4},{8,6},{10,8},{12,10},{14,12},{16,14},{18,16},{20... | collective-permute-start | bytes 2359304 | tf_op jit(solution)/shard_map/ppermute | solution.py:251
  7.9 1.1 pad_maximum_fusion
  9.0 1.6 collective-permute-start.2
  10.6 8.5 %shard_map.68 = (f32[2,16,128,256]{3,2,1,0:T(8,128)}, f32[2,16,128,256]{3,2,1,0:T(8,128)}) custom-call(f32[2,16,128,256]{3,2,1,0:T(8,128)} %refs_11_.1, f32[16,128,256]{2,1,0:T(8,128)} %refs_15_.1, s32[16,128,256]{2,1,0:T(8,128)} %refs_19_.1), custom_call_target="tpu_custom_call" | custom-call | tf_op jit(solution)/shard_map/pallas_call | solution.py:278
  19.1 1.1 sine_add_fusion.1
  20.3 0.8 slice_bitcast_fusion
  21.1 1.0 copy-done.1
  22.0 0.2 copy-done.2
  22.3 16.1 %shard_map.70 = (f32[16,128,256]{2,1,0:T(8,128)}, f32[2,16,128,256]{3,2,1,0:T(8,128)}, f32[2,128,256]{2,1,0:T(8,128)}, f32[2,128,256]{2,1,0:T(8,128)}, f32[2,16,...) custom-call(f32[2,16,128,256]{3,2,1,0:T(8,128)} %refs_2_.3, f32[2,16,128,256]{3,2,1,0:T(8,128)} %refs_2_.3, ...), custom_call_target="tpu_custom_call" | custom-call | tf_op jit(solution)/shard_map/pallas_call | solution.py:285
  38.4 0.8 pad_maximum_fusion.1
  39.2 0.6 collective-permute-start.5
  39.8 5.3 %collective-permute-start.3 = (f32[2,128,256]{2,1,0:T(8,128)}, f32[2,128,256]{2,1,0:T(8,128)S(1)}, u32[]{:S(2)}, u32[]{:S(2)}) collective-permute-start(f32[2,128,256]{2,1,0:T(8,128)} %get-tuple-element.26), channel_id=1, source_target_pairs={{0,2},{2,4},{4,6},{6,8},{8,10},{10,12},{12,14},{14,16},{16,18},{18... | collective-permute-start | bytes 786440 | tf_op jit(solution)/shard_map/ppermute | solution.py:251
  45.2 2.8 %fusion.3 = f32[32,4,16,128]{3,0,2,1:T(8,128)S(1)} fusion(f32[16,128,256]{2,1,0:T(8,128)} %get-tuple-element.30, f32[32,2,4,256]{3,0,2,1:T(8,128)S(1)} %sine_add_fusion.1), kind=kOutput, calls=%fused_computation.4 | convolution fusion | flops 402653184 | bytes 3276800 | tf_op jit(solution)/shard_map/sxn,yzn->sxyz/dot_general | solution.py:32
  47.9 0.6 slice_bitcast_fusion.2
  48.6 0.8 collective-permute-done.4.y_high_ref
  49.4 0.7 copy-done.4
  50.1 1.6 copy.13
  51.7 9.5 %all-to-all-start = ((f32[32,4,16,128]{3,2,1,0:T(8,128)}), f32[32,4,16,128]{3,2,1,0:T(8,128)S(1)}, u32[]{:S(2)}, u32[]{:S(2)}) async-start(f32[32,4,16,128]{3,2,1,0:T(8,128)} %copy.13), calls=%async_computation | async-start | bytes 2097152 | tf_op jit(solution)/shard_map/all_to_all | solution.py:334
  61.2 1.2 fusion.1
  62.4 1.6 copy.19
  64.0 22.5 %all-to-all-done = f32[32,4,16,128]{3,2,1,0:T(8,128)S(1)} async-done(((f32[32,4,16,128]{3,2,1,0:T(8,128)}), f32[32,4,16,128]{3,2,1,0:T(8,128)S(1)}, u32[]{:S(2)}, u32[]{:S(2)}) %all-to-all-start) | async-done | bytes 1048608 | tf_op jit(solution)/shard_map/all_to_all | solution.py:334
  86.5 4.6 %all-to-all-start.2 = ((f32[32,4,16,128]{3,2,1,0:T(8,128)}), f32[32,4,16,128]{3,2,1,0:T(8,128)S(1)}, u32[]{:S(2)}, u32[]{:S(2)}) async-start(f32[32,4,16,128]{3,2,1,0:T(8,128)} %copy.19), calls=%async_computation.2 | async-start | bytes 2097152 | tf_op jit(solution)/shard_map/all_to_all | solution.py:334
  91.1 0.8 broadcast_add_fusion
  91.9 0.8 copy.40
  92.8 0.8 reshape.120
  93.6 1.6 fusion.34
  95.3 1.8 fusion.5
  97.0 1.6 convolution_bitcast_fusion.2
  98.7 1.9 %fusion.30 = f32[4,256,256]{2,1,0:T(8,128)S(1)} fusion(f32[4,256,256]{1,2,0:T(8,128)S(1)} %convolution_bitcast_fusion.2), kind=kOutput, calls=%fused_computation.47 | convolution fusion | flops 403636224 | bytes 2097152 | tf_op jit(solution)/shard_map/kz,xyz->xyk/dot_general | solution.py:32
  100.6 0.5 reshape.121
  101.1 1.7 copy.17
  102.8 13.5 %all-to-all-done.2 = f32[32,4,16,128]{3,2,1,0:T(8,128)S(1)} async-done(((f32[32,4,16,128]{3,2,1,0:T(8,128)}), f32[32,4,16,128]{3,2,1,0:T(8,128)S(1)}, u32[]{:S(2)}, u32[]{:S(2)}) %all-to-all-start.2) | async-done | bytes 1048608 | tf_op jit(solution)/shard_map/all_to_all | solution.py:334
  116.3 4.6 %all-to-all-start.1 = ((f32[32,4,16,128]{3,1,2,0:T(4,128)}), f32[32,4,16,128]{3,1,2,0:T(4,128)S(1)}, u32[]{:S(2)}, u32[]{:S(2)}) async-start(f32[32,4,16,128]{3,1,2,0:T(4,128)} %bitcast.18), calls=%async_computation.1 | async-start | bytes 2097152 | tf_op jit(solution)/shard_map/all_to_all | solution.py:351
  121.0 0.8 copy.39
  121.8 0.8 reshape.124
  122.7 1.6 fusion.28
  124.3 1.8 fusion.6
  126.1 1.6 convolution_bitcast_fusion
  127.7 1.9 %fusion.24 = f32[4,256,256]{2,1,0:T(8,128)S(1)} fusion(f32[4,256,256]{1,2,0:T(8,128)S(1)} %convolution_bitcast_fusion), kind=kOutput, calls=%fused_computation.41 | convolution fusion | flops 403636224 | bytes 2097152 | tf_op jit(solution)/shard_map/kz,xyz->xyk/dot_general | solution.py:32
  129.6 0.5 reshape.125
  130.2 1.7 copy.23
  131.9 14.3 %all-to-all-done.1 = f32[32,4,16,128]{3,1,2,0:T(4,128)S(1)} async-done(((f32[32,4,16,128]{3,1,2,0:T(4,128)}), f32[32,4,16,128]{3,1,2,0:T(4,128)S(1)}, u32[]{:S(2)}, u32[]{:S(2)}) %all-to-all-start.1) | async-done | bytes 1048608 | tf_op jit(solution)/shard_map/all_to_all | solution.py:351
  146.2 4.7 %all-to-all-start.3 = ((f32[32,4,16,128]{3,1,2,0:T(4,128)}), f32[32,4,16,128]{3,1,2,0:T(4,128)}, u32[]{:S(2)}, u32[]{:S(2)}) async-start(f32[32,4,16,128]{3,1,2,0:T(4,128)} %bitcast.29), calls=%async_computation.3 | async-start | bytes 2097152 | tf_op jit(solution)/shard_map/all_to_all | solution.py:351
  150.9 6.9 %shard_map.71 = f32[2,16,128,256]{3,2,1,0:T(8,128)} custom-call(f32[2,16,128,256]{3,2,1,0:T(8,128)} %get-tuple-element.25.w_ref.w_prev.w_next, f32[2,16,128,256]{3,2,1,0:T(8,128)} %get-tuple-element.25.w_ref.w_prev.w_next, f32[2,16,128,256]{3,2,1,0:T(8,128)} %get-tuple-element.25.w_ref.w_prev.w_next, f32[2,128,256]{2,1,0:T(8,128)} %copy-done.3, ...), custom_call_target="tpu_custom_call" | custom-call | tf_op jit(solution)/shard_map/pallas_call | solution.py:301
  157.8 1.5 fusion.16
  159.2 16.9 %all-to-all-done.3 = f32[32,4,16,128]{3,1,2,0:T(4,128)} async-done(((f32[32,4,16,128]{3,1,2,0:T(4,128)}), f32[32,4,16,128]{3,1,2,0:T(4,128)}, u32[]{:S(2)}, u32[]{:S(2)}) %all-to-all-start.3) | async-done | bytes 1048608 | tf_op jit(solution)/shard_map/all_to_all | solution.py:351
  176.2 4.0 %fusion = f32[16,128,256]{2,1,0:T(8,128)} fusion(f32[16,128,256,1]{2,1,3,0:T(8,128)S(1)} %fusion.16, f32[32,4,16,128]{3,1,2,0:T(4,128)} %all-to-all-done.3, f32[32,2,4,256]{3,0,2,1:T(8,128)S(1)} %sine_add_fusion.1), kind=kOutput, calls=%fused_computation.1 | convolution fusion | flops 403701760 | bytes 5373952 | tf_op jit(solution)/shard_map/sxn,sxyz->yzn/dot_general | solution.py:32
  (23 shorter events, 0.1 us)
Async XLA Ops:
  5.2 15.8 %collective-permute-start = (f32[6,128,256]{2,1,0:T(8,128)}, f32[6,128,256]{2,1,0:T(8,128)S(1)}, u32[]{:S(2)}, u32[]{:S(2)}) collective-permute-start(f32[6,128,256]{2,1,0:T(8,128)} %get-tuple-element.21), channel_id=1, source_target_pairs={{0,2},{2,4},{4,6},{6,8},{8,10},{10,12},{12,14},{14,16},{16,18},{18... | collective-permute-start | bytes 2359304 | tf_op jit(solution)/shard_map/ppermute | solution.py:251
  5.3 15.8 %collective-permute-start.1 = (f32[6,128,256]{2,1,0:T(8,128)}, f32[6,128,256]{2,1,0:T(8,128)S(1)}, u32[]{:S(2)}, u32[]{:S(2)}) collective-permute-start(f32[6,128,256]{2,1,0:T(8,128)} %get-tuple-element.22), channel_id=1, source_target_pairs={{2,0},{4,2},{6,4},{8,6},{10,8},{12,10},{14,12},{16,14},{18,16},{20... | collective-permute-start | bytes 2359304 | tf_op jit(solution)/shard_map/ppermute | solution.py:251
  9.0 11.2 %collective-permute-start.2 = (f32[2,6,16,1,256]{4,3,2,1,0:T(1,128)S(1)}, f32[2,6,16,1,256]{4,3,2,1,0:T(1,128)S(1)}, u32[]{:S(2)}, u32[]{:S(2)}) collective-permute-start(f32[2,6,16,1,256]{4,3,2,1,0:T(1,128)S(1)} %pad_maximum_fusion), channel_id=1, source_target_pairs={{0,1},{1,0},{2,3},{3,2},{4,5},{5,4},{6,7},{7,6},{8,9},{9,8},{10,11... | collective-permute-start | bytes 589832 | tf_op jit(solution)/shard_map/ppermute | solution.py:248
  21.1 1.0 copy-start.1
  21.1 1.2 copy-start.2
  39.2 8.7 %collective-permute-start.5 = (f32[2,2,16,1,256]{4,3,2,1,0:T(1,128)S(1)}, f32[2,2,16,1,256]{4,3,2,1,0:T(1,128)S(1)}, u32[]{:S(2)}, u32[]{:S(2)}) collective-permute-start(f32[2,2,16,1,256]{4,3,2,1,0:T(1,128)S(1)} %pad_maximum_fusion.1), channel_id=1, source_target_pairs={{0,1},{1,0},{2,3},{3,2},{4,5},{5,4},{6,7},{7,6},{8,9},{9,8},{10,11... | collective-permute-start | bytes 196616 | tf_op jit(solution)/shard_map/ppermute | solution.py:248
  39.8 8.7 %collective-permute-start.3 = (f32[2,128,256]{2,1,0:T(8,128)}, f32[2,128,256]{2,1,0:T(8,128)S(1)}, u32[]{:S(2)}, u32[]{:S(2)}) collective-permute-start(f32[2,128,256]{2,1,0:T(8,128)} %get-tuple-element.26), channel_id=1, source_target_pairs={{0,2},{2,4},{4,6},{6,8},{8,10},{10,12},{12,14},{14,16},{16,18},{18... | collective-permute-start | bytes 786440 | tf_op jit(solution)/shard_map/ppermute | solution.py:251
  45.2 4.3 %collective-permute-start.4 = (f32[2,128,256]{2,1,0:T(8,128)}, f32[2,128,256]{2,1,0:T(8,128)S(1)}, u32[]{:S(2)}, u32[]{:S(2)}) collective-permute-start(f32[2,128,256]{2,1,0:T(8,128)} %get-tuple-element.27), channel_id=1, source_target_pairs={{2,0},{4,2},{6,4},{8,6},{10,8},{12,10},{14,12},{16,14},{18,16},{20... | collective-permute-start | bytes 786440 | tf_op jit(solution)/shard_map/ppermute | solution.py:251
  48.6 0.9 copy-start.3
  49.4 0.7 copy-start.4
  50.1 11.1 %copy-start = (f32[16,128,256]{2,1,0:T(8,128)S(1)}, f32[16,128,256]{2,1,0:T(8,128)}, u32[]{:S(2)}) copy-start(f32[16,128,256]{2,1,0:T(8,128)} %get-tuple-element.30) | copy-start | bytes 6291460
  51.7 34.8 %all-to-all-start = ((f32[32,4,16,128]{3,2,1,0:T(8,128)}), f32[32,4,16,128]{3,2,1,0:T(8,128)S(1)}, u32[]{:S(2)}, u32[]{:S(2)}) async-start(f32[32,4,16,128]{3,2,1,0:T(8,128)} %copy.13), calls=%async_computation | async-start | bytes 2097152 | tf_op jit(solution)/shard_map/all_to_all | solution.py:334
  86.5 29.9 %all-to-all-start.2 = ((f32[32,4,16,128]{3,2,1,0:T(8,128)}), f32[32,4,16,128]{3,2,1,0:T(8,128)S(1)}, u32[]{:S(2)}, u32[]{:S(2)}) async-start(f32[32,4,16,128]{3,2,1,0:T(8,128)} %copy.19), calls=%async_computation.2 | async-start | bytes 2097152 | tf_op jit(solution)/shard_map/all_to_all | solution.py:334
  93.6 1.7 copy-start.5
  116.3 29.9 %all-to-all-start.1 = ((f32[32,4,16,128]{3,1,2,0:T(4,128)}), f32[32,4,16,128]{3,1,2,0:T(4,128)S(1)}, u32[]{:S(2)}, u32[]{:S(2)}) async-start(f32[32,4,16,128]{3,1,2,0:T(4,128)} %bitcast.18), calls=%async_computation.1 | async-start | bytes 2097152 | tf_op jit(solution)/shard_map/all_to_all | solution.py:351
  122.6 1.7 copy-start.6
  146.2 30.0 %all-to-all-start.3 = ((f32[32,4,16,128]{3,1,2,0:T(4,128)}), f32[32,4,16,128]{3,1,2,0:T(4,128)}, u32[]{:S(2)}, u32[]{:S(2)}) async-start(f32[32,4,16,128]{3,1,2,0:T(4,128)} %bitcast.29), calls=%async_computation.3 | async-start | bytes 2097152 | tf_op jit(solution)/shard_map/all_to_all | solution.py:351

commit v10 on v6

--- a/solution.py
+++ b/solution.py
@@ -222,7 +222,7 @@
 
 
 def block_rows(length_y):
-    rows = 8
+    rows = 4
     while length_y % rows:
         rows //= 2
     return rows

time: 183 us -> 184 us (level)
  no operation moved by 1% of the time
where the time goes in v10:
time: 184 us; the launch traced here: 180 us
  waiting for transfers between devices  67.8 us (37%)
  Pallas kernels  37.2 us (20%)
  starting transfers between devices  33 us (18%)
  matrix products  23.2 us (13%)
  local copies, waits for them, and re-layouts  14.3 us (8%)
  other arithmetic  3.93 us (2%)
    all_to_all x2, waiting for transfers between devices, dipole_adjoint(): sent.append(lax.all_to_all(spec, ('gy', 'gz'), 0, 0, tiled=True))  36 us
    all_to_all x2, waiting for transfers between devices, dipole_adjoint(): spec = lax.all_to_all(spec, ('gy', 'gz'), 0, 0, tiled=True)  30.9 us
    dot_general x12, matrix products, along(): return jnp.einsum(spec, table, values, precision=lax.Precision.HIGH)  23.2 us
    pallas_call x1, Pallas kernels, backward_sections(): pl.pallas_call(functools.partial(first_kernel, rows=rows), grid=grid, in_...  15.3 us
    all_to_all x2, starting transfers between devices, dipole_adjoint(): sent.append(lax.all_to_all(spec, ('gy', 'gz'), 0, 0, tiled=True))  14.1 us
    all_to_all x2, starting transfers between devices, dipole_adjoint(): spec = lax.all_to_all(spec, ('gy', 'gz'), 0, 0, tiled=True)  9.27 us
    pallas_call x1, Pallas kernels, backward_sections(): pl.pallas_call(functools.partial(factor_kernel, rows=rows), grid=grid, in...  9.14 us
    pallas_call x1, Pallas kernels, finish_lambda(): pl.pallas_call(functools.partial(second_kernel, rows=rows), grid=grid, in...  7.22 us
  transfers between devices with their start and end apart: 10, of which 5 were waited for; matrix products, arithmetic and copies ran while one was open for 18% of the time, Pallas kernels for 9%

profile of v10, /device:TPU:16, one launch (start us, length us, event | category | flops | bytes accessed | tf_op | source)
XLA Modules:
  0.0 180.3 jit_solution(628967682446561672)
XLA Ops:
  0.6 5.5 %shard_map.69 = (f32[6,128,256]{2,1,0:T(8,128)}, f32[6,128,256]{2,1,0:T(8,128)}, f32[6,16,1,256]{3,2,1,0:T(1,128)}, f32[6,16,1,256]{3,2,1,0:T(1,128)}) custom-call(f32[2,16,128,256]{3,2,1,0:T(8,128)} %refs_2_.3, f32[2,16,128,256]{3,2,1,0:T(8,128)} %refs_2_.3, f32[2,16,128,256]{3,2,1,0:T(8,128)} %refs_2_.3, f32[2,16,128,256]{3,2,1,0:T(8,128)} %refs_2_.3, ...), custom_call_target="tpu_custom_call" | custom-call | tf_op jit(solution)/shard_map/pallas_call | solution.py:268
  6.2 2.6 %collective-permute-start.1 = (f32[6,128,256]{2,1,0:T(8,128)}, f32[6,128,256]{2,1,0:T(8,128)S(1)}, u32[]{:S(2)}, u32[]{:S(2)}) collective-permute-start(f32[6,128,256]{2,1,0:T(8,128)} %get-tuple-element.22), channel_id=1, source_target_pairs={{2,0},{4,2},{6,4},{8,6},{10,8},{12,10},{14,12},{16,14},{18,16},{20... | collective-permute-start | bytes 2359304 | tf_op jit(solution)/shard_map/ppermute | solution.py:251
  8.9 1.1 pad_maximum_fusion
  10.0 1.6 collective-permute-start.2
  11.6 9.1 %shard_map.68 = (f32[2,16,128,256]{3,2,1,0:T(8,128)}, f32[2,16,128,256]{3,2,1,0:T(8,128)}) custom-call(f32[2,16,128,256]{3,2,1,0:T(8,128)} %refs_11_.1, f32[16,128,256]{2,1,0:T(8,128)} %refs_15_.1, s32[16,128,256]{2,1,0:T(8,128)} %refs_19_.1), custom_call_target="tpu_custom_call" | custom-call | tf_op jit(solution)/shard_map/pallas_call | solution.py:276
  20.7 1.1 sine_add_fusion.1
  21.8 0.8 slice_bitcast_fusion
  22.7 1.0 copy-done.1
  23.6 0.2 copy-done.2
  23.8 15.3 %shard_map.70 = (f32[16,128,256]{2,1,0:T(8,128)}, f32[2,16,128,256]{3,2,1,0:T(8,128)}, f32[2,128,256]{2,1,0:T(8,128)}, f32[2,128,256]{2,1,0:T(8,128)}, f32[2,16,...) custom-call(f32[2,16,128,256]{3,2,1,0:T(8,128)} %refs_2_.3, f32[2,16,128,256]{3,2,1,0:T(8,128)} %refs_2_.3, ...), custom_call_target="tpu_custom_call" | custom-call | tf_op jit(solution)/shard_map/pallas_call | solution.py:283
  39.1 0.8 pad_maximum_fusion.1
  40.0 0.6 collective-permute-start.5
  40.6 4.7 %collective-permute-start.3 = (f32[2,128,256]{2,1,0:T(8,128)}, f32[2,128,256]{2,1,0:T(8,128)S(1)}, u32[]{:S(2)}, u32[]{:S(2)}) collective-permute-start(f32[2,128,256]{2,1,0:T(8,128)} %get-tuple-element.26), channel_id=1, source_target_pairs={{0,2},{2,4},{4,6},{6,8},{8,10},{10,12},{12,14},{14,16},{16,18},{18... | collective-permute-start | bytes 786440 | tf_op jit(solution)/shard_map/ppermute | solution.py:251
  45.3 2.8 %fusion.3 = f32[32,4,16,128]{3,0,2,1:T(8,128)S(1)} fusion(f32[16,128,256]{2,1,0:T(8,128)} %get-tuple-element.30, f32[32,2,4,256]{3,0,2,1:T(8,128)S(1)} %sine_add_fusion.1), kind=kOutput, calls=%fused_computation.4 | convolution fusion | flops 402653184 | bytes 3276800 | tf_op jit(solution)/shard_map/sxn,yzn->sxyz/dot_general | solution.py:32
  48.1 0.6 slice_bitcast_fusion.2
  48.7 0.8 collective-permute-done.4.y_high_ref
  49.5 0.7 copy-done.4
  50.2 1.6 copy.13
  51.8 9.5 %all-to-all-start = ((f32[32,4,16,128]{3,2,1,0:T(8,128)}), f32[32,4,16,128]{3,2,1,0:T(8,128)S(1)}, u32[]{:S(2)}, u32[]{:S(2)}) async-start(f32[32,4,16,128]{3,2,1,0:T(8,128)} %copy.13), calls=%async_computation | async-start | bytes 2097152 | tf_op jit(solution)/shard_map/all_to_all | solution.py:332
  61.4 1.2 fusion.1
  62.5 1.6 copy.19
  64.2 22.5 %all-to-all-done = f32[32,4,16,128]{3,2,1,0:T(8,128)S(1)} async-done(((f32[32,4,16,128]{3,2,1,0:T(8,128)}), f32[32,4,16,128]{3,2,1,0:T(8,128)S(1)}, u32[]{:S(2)}, u32[]{:S(2)}) %all-to-all-start) | async-done | bytes 1048608 | tf_op jit(solution)/shard_map/all_to_all | solution.py:332
  86.6 4.6 %all-to-all-start.2 = ((f32[32,4,16,128]{3,2,1,0:T(8,128)}), f32[32,4,16,128]{3,2,1,0:T(8,128)S(1)}, u32[]{:S(2)}, u32[]{:S(2)}) async-start(f32[32,4,16,128]{3,2,1,0:T(8,128)} %copy.19), calls=%async_computation.2 | async-start | bytes 2097152 | tf_op jit(solution)/shard_map/all_to_all | solution.py:332
  91.3 0.8 broadcast_add_fusion
  92.1 0.8 copy.40
  92.9 0.8 reshape.120
  93.8 1.6 fusion.34
  95.4 1.8 fusion.5
  97.2 1.6 convolution_bitcast_fusion.2
  98.8 1.9 %fusion.30 = f32[4,256,256]{2,1,0:T(8,128)S(1)} fusion(f32[4,256,256]{1,2,0:T(8,128)S(1)} %convolution_bitcast_fusion.2), kind=kOutput, calls=%fused_computation.47 | convolution fusion | flops 403636224 | bytes 2097152 | tf_op jit(solution)/shard_map/kz,xyz->xyk/dot_general | solution.py:32
  100.7 0.5 reshape.121
  101.3 1.7 copy.17
  102.9 13.5 %all-to-all-done.2 = f32[32,4,16,128]{3,2,1,0:T(8,128)S(1)} async-done(((f32[32,4,16,128]{3,2,1,0:T(8,128)}), f32[32,4,16,128]{3,2,1,0:T(8,128)S(1)}, u32[]{:S(2)}, u32[]{:S(2)}) %all-to-all-start.2) | async-done | bytes 1048608 | tf_op jit(solution)/shard_map/all_to_all | solution.py:332
  116.5 4.6 %all-to-all-start.1 = ((f32[32,4,16,128]{3,1,2,0:T(4,128)}), f32[32,4,16,128]{3,1,2,0:T(4,128)S(1)}, u32[]{:S(2)}, u32[]{:S(2)}) async-start(f32[32,4,16,128]{3,1,2,0:T(4,128)} %bitcast.18), calls=%async_computation.1 | async-start | bytes 2097152 | tf_op jit(solution)/shard_map/all_to_all | solution.py:349
  121.1 0.8 copy.39
  121.9 0.8 reshape.124
  122.8 1.6 fusion.28
  124.5 1.8 fusion.6
  126.2 1.6 convolution_bitcast_fusion
  127.9 1.9 %fusion.24 = f32[4,256,256]{2,1,0:T(8,128)S(1)} fusion(f32[4,256,256]{1,2,0:T(8,128)S(1)} %convolution_bitcast_fusion), kind=kOutput, calls=%fused_computation.41 | convolution fusion | flops 403636224 | bytes 2097152 | tf_op jit(solution)/shard_map/kz,xyz->xyk/dot_general | solution.py:32
  129.8 0.5 reshape.125
  130.3 1.7 copy.23
  132.0 14.3 %all-to-all-done.1 = f32[32,4,16,128]{3,1,2,0:T(4,128)S(1)} async-done(((f32[32,4,16,128]{3,1,2,0:T(4,128)}), f32[32,4,16,128]{3,1,2,0:T(4,128)S(1)}, u32[]{:S(2)}, u32[]{:S(2)}) %all-to-all-start.1) | async-done | bytes 1048608 | tf_op jit(solution)/shard_map/all_to_all | solution.py:349
  146.4 4.7 %all-to-all-start.3 = ((f32[32,4,16,128]{3,1,2,0:T(4,128)}), f32[32,4,16,128]{3,1,2,0:T(4,128)}, u32[]{:S(2)}, u32[]{:S(2)}) async-start(f32[32,4,16,128]{3,1,2,0:T(4,128)} %bitcast.29), calls=%async_computation.3 | async-start | bytes 2097152 | tf_op jit(solution)/shard_map/all_to_all | solution.py:349
  151.0 7.2 %shard_map.71 = f32[2,16,128,256]{3,2,1,0:T(8,128)} custom-call(f32[2,16,128,256]{3,2,1,0:T(8,128)} %get-tuple-element.25.w_ref.w_prev.w_next, f32[2,16,128,256]{3,2,1,0:T(8,128)} %get-tuple-element.25.w_ref.w_prev.w_next, f32[2,16,128,256]{3,2,1,0:T(8,128)} %get-tuple-element.25.w_ref.w_prev.w_next, f32[2,128,256]{2,1,0:T(8,128)} %copy-done.3, ...), custom_call_target="tpu_custom_call" | custom-call | tf_op jit(solution)/shard_map/pallas_call | solution.py:299
  158.3 1.5 fusion.16
  159.7 16.6 %all-to-all-done.3 = f32[32,4,16,128]{3,1,2,0:T(4,128)} async-done(((f32[32,4,16,128]{3,1,2,0:T(4,128)}), f32[32,4,16,128]{3,1,2,0:T(4,128)}, u32[]{:S(2)}, u32[]{:S(2)}) %all-to-all-start.3) | async-done | bytes 1048608 | tf_op jit(solution)/shard_map/all_to_all | solution.py:349
  176.3 4.0 %fusion = f32[16,128,256]{2,1,0:T(8,128)} fusion(f32[16,128,256,1]{2,1,3,0:T(8,128)S(1)} %fusion.16, f32[32,4,16,128]{3,1,2,0:T(4,128)} %all-to-all-done.3, f32[32,2,4,256]{3,0,2,1:T(8,128)S(1)} %sine_add_fusion.1), kind=kOutput, calls=%fused_computation.1 | convolution fusion | flops 403701760 | bytes 5373952 | tf_op jit(solution)/shard_map/sxn,sxyz->yzn/dot_general | solution.py:32
  (23 shorter events, 0.1 us)
Async XLA Ops:
  6.2 16.5 %collective-permute-start = (f32[6,128,256]{2,1,0:T(8,128)}, f32[6,128,256]{2,1,0:T(8,128)S(1)}, u32[]{:S(2)}, u32[]{:S(2)}) collective-permute-start(f32[6,128,256]{2,1,0:T(8,128)} %get-tuple-element.21), channel_id=1, source_target_pairs={{0,2},{2,4},{4,6},{6,8},{8,10},{10,12},{12,14},{14,16},{16,18},{18... | collective-permute-start | bytes 2359304 | tf_op jit(solution)/shard_map/ppermute | solution.py:251
  6.2 16.4 %collective-permute-start.1 = (f32[6,128,256]{2,1,0:T(8,128)}, f32[6,128,256]{2,1,0:T(8,128)S(1)}, u32[]{:S(2)}, u32[]{:S(2)}) collective-permute-start(f32[6,128,256]{2,1,0:T(8,128)} %get-tuple-element.22), channel_id=1, source_target_pairs={{2,0},{4,2},{6,4},{8,6},{10,8},{12,10},{14,12},{16,14},{18,16},{20... | collective-permute-start | bytes 2359304 | tf_op jit(solution)/shard_map/ppermute | solution.py:251
  10.0 11.8 %collective-permute-start.2 = (f32[2,6,16,1,256]{4,3,2,1,0:T(1,128)S(1)}, f32[2,6,16,1,256]{4,3,2,1,0:T(1,128)S(1)}, u32[]{:S(2)}, u32[]{:S(2)}) collective-permute-start(f32[2,6,16,1,256]{4,3,2,1,0:T(1,128)S(1)} %pad_maximum_fusion), channel_id=1, source_target_pairs={{0,1},{1,0},{2,3},{3,2},{4,5},{5,4},{6,7},{7,6},{8,9},{9,8},{10,11... | collective-permute-start | bytes 589832 | tf_op jit(solution)/shard_map/ppermute | solution.py:248
  22.6 1.0 copy-start.1
  22.6 1.2 copy-start.2
  40.0 8.1 %collective-permute-start.5 = (f32[2,2,16,1,256]{4,3,2,1,0:T(1,128)S(1)}, f32[2,2,16,1,256]{4,3,2,1,0:T(1,128)S(1)}, u32[]{:S(2)}, u32[]{:S(2)}) collective-permute-start(f32[2,2,16,1,256]{4,3,2,1,0:T(1,128)S(1)} %pad_maximum_fusion.1), channel_id=1, source_target_pairs={{0,1},{1,0},{2,3},{3,2},{4,5},{5,4},{6,7},{7,6},{8,9},{9,8},{10,11... | collective-permute-start | bytes 196616 | tf_op jit(solution)/shard_map/ppermute | solution.py:248
  40.6 8.1 %collective-permute-start.3 = (f32[2,128,256]{2,1,0:T(8,128)}, f32[2,128,256]{2,1,0:T(8,128)S(1)}, u32[]{:S(2)}, u32[]{:S(2)}) collective-permute-start(f32[2,128,256]{2,1,0:T(8,128)} %get-tuple-element.26), channel_id=1, source_target_pairs={{0,2},{2,4},{4,6},{6,8},{8,10},{10,12},{12,14},{14,16},{16,18},{18... | collective-permute-start | bytes 786440 | tf_op jit(solution)/shard_map/ppermute | solution.py:251
  45.3 4.3 %collective-permute-start.4 = (f32[2,128,256]{2,1,0:T(8,128)}, f32[2,128,256]{2,1,0:T(8,128)S(1)}, u32[]{:S(2)}, u32[]{:S(2)}) collective-permute-start(f32[2,128,256]{2,1,0:T(8,128)} %get-tuple-element.27), channel_id=1, source_target_pairs={{2,0},{4,2},{6,4},{8,6},{10,8},{12,10},{14,12},{16,14},{18,16},{20... | collective-permute-start | bytes 786440 | tf_op jit(solution)/shard_map/ppermute | solution.py:251
  48.7 0.9 copy-start.3
  49.5 0.7 copy-start.4
  50.2 11.1 %copy-start = (f32[16,128,256]{2,1,0:T(8,128)S(1)}, f32[16,128,256]{2,1,0:T(8,128)}, u32[]{:S(2)}) copy-start(f32[16,128,256]{2,1,0:T(8,128)} %get-tuple-element.30) | copy-start | bytes 6291460
  51.8 34.8 %all-to-all-start = ((f32[32,4,16,128]{3,2,1,0:T(8,128)}), f32[32,4,16,128]{3,2,1,0:T(8,128)S(1)}, u32[]{:S(2)}, u32[]{:S(2)}) async-start(f32[32,4,16,128]{3,2,1,0:T(8,128)} %copy.13), calls=%async_computation | async-start | bytes 2097152 | tf_op jit(solution)/shard_map/all_to_all | solution.py:332
  86.6 29.9 %all-to-all-start.2 = ((f32[32,4,16,128]{3,2,1,0:T(8,128)}), f32[32,4,16,128]{3,2,1,0:T(8,128)S(1)}, u32[]{:S(2)}, u32[]{:S(2)}) async-start(f32[32,4,16,128]{3,2,1,0:T(8,128)} %copy.19), calls=%async_computation.2 | async-start | bytes 2097152 | tf_op jit(solution)/shard_map/all_to_all | solution.py:332
  93.7 1.7 copy-start.5
  116.5 29.9 %all-to-all-start.1 = ((f32[32,4,16,128]{3,1,2,0:T(4,128)}), f32[32,4,16,128]{3,1,2,0:T(4,128)S(1)}, u32[]{:S(2)}, u32[]{:S(2)}) async-start(f32[32,4,16,128]{3,1,2,0:T(4,128)} %bitcast.18), calls=%async_computation.1 | async-start | bytes 2097152 | tf_op jit(solution)/shard_map/all_to_all | solution.py:349
  122.8 1.7 copy-start.6
  146.4 30.0 %all-to-all-start.3 = ((f32[32,4,16,128]{3,1,2,0:T(4,128)}), f32[32,4,16,128]{3,1,2,0:T(4,128)}, u32[]{:S(2)}, u32[]{:S(2)}) async-start(f32[32,4,16,128]{3,1,2,0:T(4,128)} %bitcast.29), calls=%async_computation.3 | async-start | bytes 2097152 | tf_op jit(solution)/shard_map/all_to_all | solution.py:349

commit v11 on v6

--- a/solution.py
+++ b/solution.py
@@ -347,7 +347,9 @@
         spec = spec.reshape(piece_x, count_y, block_y, count_z, block_z)
         spec = spec.transpose(1, 3, 0, 2, 4).reshape(parts, piece_x, block_y, block_z)
         spec = lax.all_to_all(spec, ("gy", "gz"), 0, 0, tiled=True)
-        part = along("sxn,sxyz->yzn", table_x[:, p], spec)
+        rows_in = spec.reshape(parts * piece_x, block_y * block_z)
+        part = along("kn,km->mn", table_x[:, p].reshape(parts * piece_x, length_x), rows_in)
+        part = part.reshape(block_y, block_z, length_x)
         result = part if result is None else result + part
     return result * scale, lam
 

time: 183 us -> 179 us (0.978)
  matrix products: 23.2 us -> 21.1 us
  starting transfers between devices: 33.5 us -> 31.5 us
    all_to_all x2, waiting for transfers between devices: 36 us -> 14.1 us  [dipole_adjoint(): sent.append(lax.all_to_all(spec, ('gy', 'gz'), 0, 0, tiled=True))]
    ppermute x2, waiting for transfers between devices: 0.01 us -> 17.5 us  [send_edges(): lax.ppermute(last, axis, up)]
    ppermute x2, starting transfers between devices: 5.38 us -> 0.06 us  [send_edges(): lax.ppermute(last, axis, up)]
    ppermute x2, waiting for transfers between devices: 0.01 us -> 4.56 us  [send_edges(): both = lax.ppermute(jnp.stack([last, first]), axis, up)]
    transpose x2 -> x0, local copies, waits for them, and re-layouts: 3.37 us -> none  [dipole_adjoint(): spec.transpose(1, 3, 0, 2, 4).reshape(parts, piece_x, block_y, block_z)]
    ppermute x2, starting transfers between devices: 2.63 us -> 5.27 us  [send_edges(): lax.ppermute(first, axis, down)]
    reshape x2 -> x4, local copies, waits for them, and re-layouts: 1.08 us -> 3.29 us  [dipole_adjoint(): spec = spec.reshape(piece_x, count_y, block_y, count_z, block_z)]
    dot_general x12, matrix products: 23.2 us -> 21.1 us  [along(): return jnp.einsum(spec, table, values, precision=lax.Precision.HIGH)]
  transfers between devices with their start and end apart: 10 -> 10, of which waited for: 5 -> 5; matrix products, arithmetic and copies ran while one was open for 18% -> 17% of each run, Pallas kernels for 9% -> 9%
where the time goes in v11:
time: 179 us; the launch traced here: 176 us
  waiting for transfers between devices  67.5 us (38%)
  Pallas kernels  36.1 us (20%)
  starting transfers between devices  31.5 us (18%)
  matrix products  21.1 us (12%)
  local copies, waits for them, and re-layouts  16.1 us (9%)
  other arithmetic  3.15 us (2%)
    all_to_all x2, waiting for transfers between devices, dipole_adjoint(): spec = lax.all_to_all(spec, ('gy', 'gz'), 0, 0, tiled=True)  31.3 us
    dot_general x12, matrix products, along(): return jnp.einsum(spec, table, values, precision=lax.Precision.HIGH)  21.1 us
    ppermute x2, waiting for transfers between devices, send_edges(): lax.ppermute(last, axis, up)  17.5 us
    pallas_call x1, Pallas kernels, backward_sections(): pl.pallas_call(functools.partial(first_kernel, rows=rows), grid=grid, in_...  16.1 us
    all_to_all x2, waiting for transfers between devices, dipole_adjoint(): sent.append(lax.all_to_all(spec, ('gy', 'gz'), 0, 0, tiled=True))  14.1 us
    all_to_all x2, starting transfers between devices, dipole_adjoint(): sent.append(lax.all_to_all(spec, ('gy', 'gz'), 0, 0, tiled=True))  13.9 us
    all_to_all x2, starting transfers between devices, dipole_adjoint(): spec = lax.all_to_all(spec, ('gy', 'gz'), 0, 0, tiled=True)  9.21 us
    pallas_call x1, Pallas kernels, backward_sections(): pl.pallas_call(functools.partial(factor_kernel, rows=rows), grid=grid, in...  8.56 us
  transfers between devices with their start and end apart: 10, of which 5 were waited for; matrix products, arithmetic and copies ran while one was open for 17% of the time, Pallas kernels for 9%

profile of v11, /device:TPU:16, one launch (start us, length us, event | category | flops | bytes accessed | tf_op | source)
XLA Modules:
  0.0 176.4 jit_solution(7008253025518410567)
XLA Ops:
  0.6 4.5 %shard_map.69 = (f32[6,128,256]{2,1,0:T(8,128)}, f32[6,128,256]{2,1,0:T(8,128)}, f32[6,16,1,256]{3,2,1,0:T(1,128)}, f32[6,16,1,256]{3,2,1,0:T(1,128)}) custom-call(f32[2,16,128,256]{3,2,1,0:T(8,128)} %refs_2_.3, f32[2,16,128,256]{3,2,1,0:T(8,128)} %refs_2_.3, f32[2,16,128,256]{3,2,1,0:T(8,128)} %refs_2_.3, f32[2,16,128,256]{3,2,1,0:T(8,128)} %refs_2_.3, ...), custom_call_target="tpu_custom_call" | custom-call | tf_op jit(solution)/shard_map/pallas_call | solution.py:268
  5.2 2.6 %collective-permute-start.1 = (f32[6,128,256]{2,1,0:T(8,128)}, f32[6,128,256]{2,1,0:T(8,128)S(1)}, u32[]{:S(2)}, u32[]{:S(2)}) collective-permute-start(f32[6,128,256]{2,1,0:T(8,128)} %get-tuple-element.22), channel_id=1, source_target_pairs={{2,0},{4,2},{6,4},{8,6},{10,8},{12,10},{14,12},{16,14},{18,16},{20... | collective-permute-start | bytes 2359304 | tf_op jit(solution)/shard_map/ppermute | solution.py:251
  7.9 1.1 pad_maximum_fusion
  9.0 1.6 collective-permute-start.2
  10.6 8.6 %shard_map.68 = (f32[2,16,128,256]{3,2,1,0:T(8,128)}, f32[2,16,128,256]{3,2,1,0:T(8,128)}) custom-call(f32[2,16,128,256]{3,2,1,0:T(8,128)} %refs_11_.1, f32[16,128,256]{2,1,0:T(8,128)} %refs_15_.1, s32[16,128,256]{2,1,0:T(8,128)} %refs_19_.1), custom_call_target="tpu_custom_call" | custom-call | tf_op jit(solution)/shard_map/pallas_call | solution.py:276
  19.1 1.1 sine_add_fusion.1
  20.3 0.8 slice_bitcast_fusion
  21.1 1.0 copy-done.2
  22.3 16.1 %shard_map.70 = (f32[16,128,256]{2,1,0:T(8,128)}, f32[2,16,128,256]{3,2,1,0:T(8,128)}, f32[2,128,256]{2,1,0:T(8,128)}, f32[2,128,256]{2,1,0:T(8,128)}, f32[2,16,...) custom-call(f32[2,16,128,256]{3,2,1,0:T(8,128)} %refs_2_.3, f32[2,16,128,256]{3,2,1,0:T(8,128)} %refs_2_.3, ...), custom_call_target="tpu_custom_call" | custom-call | tf_op jit(solution)/shard_map/pallas_call | solution.py:283
  38.4 2.8 %fusion = f32[32,4,16,128]{3,0,2,1:T(8,128)S(1)} fusion(f32[16,128,256]{2,1,0:T(8,128)} %get-tuple-element.30, f32[32,2,4,256]{3,0,2,1:T(8,128)S(1)} %sine_add_fusion.1), kind=kOutput, calls=%fused_computation | convolution fusion | flops 402653184 | bytes 3276800 | tf_op jit(solution)/shard_map/sxn,yzn->sxyz/dot_general | solution.py:32
  41.2 1.6 copy.22
  42.8 10.1 %all-to-all-start.2 = ((f32[32,4,16,128]{3,2,1,0:T(8,128)}), f32[32,4,16,128]{3,2,1,0:T(8,128)S(1)}, u32[]{:S(2)}, u32[]{:S(2)}) async-start(f32[32,4,16,128]{3,2,1,0:T(8,128)} %copy.22), calls=%async_computation.2 | async-start | bytes 2097152 | tf_op jit(solution)/shard_map/all_to_all | solution.py:332
  53.0 1.5 collective-permute-start.5
  54.6 2.6 %collective-permute-start.4 = (f32[2,128,256]{2,1,0:T(8,128)}, f32[2,128,256]{2,1,0:T(8,128)S(1)}, u32[]{:S(2)}, u32[]{:S(2)}) collective-permute-start(f32[2,128,256]{2,1,0:T(8,128)} %get-tuple-element.27), channel_id=1, source_target_pairs={{2,0},{4,2},{6,4},{8,6},{10,8},{12,10},{14,12},{16,14},{18,16},{20... | collective-permute-start | bytes 786440 | tf_op jit(solution)/shard_map/ppermute | solution.py:251
  57.2 1.2 fusion.2
  58.4 4.6 %collective-permute-done.5 = f32[2,2,16,1,256]{4,3,2,1,0:T(1,128)S(1)} collective-permute-done((f32[2,2,16,1,256]{4,3,2,1,0:T(1,128)S(1)}, f32[2,2,16,1,256]{4,3,2,1,0:T(1,128)S(1)}, u32[]{:S(2)}, u32[]{:S(2)}) %collective-permute-start.5) | collective-permute-done | bytes 65568 | tf_op jit(solution)/shard_map/ppermute | solution.py:248
  62.9 0.6 slice_bitcast_fusion.2
  63.6 17.4 %collective-permute-done.3.y_low_ref = f32[2,128,256]{2,1,0:T(8,128)S(1)} collective-permute-done((f32[2,128,256]{2,1,0:T(8,128)}, f32[2,128,256]{2,1,0:T(8,128)S(1)}, u32[]{:S(2)}, u32[]{:S(2)}) %collective-permute-start.3) | collective-permute-done | bytes 262176 | tf_op jit(solution)/shard_map/ppermute | solution.py:251
  81.0 0.7 copy-done.4
  81.8 1.6 copy.15
  83.4 3.7 %all-to-all-start = ((f32[32,4,16,128]{3,2,1,0:T(8,128)}), f32[32,4,16,128]{3,2,1,0:T(8,128)S(1)}, u32[]{:S(2)}, u32[]{:S(2)}) async-start(f32[32,4,16,128]{3,2,1,0:T(8,128)} %copy.15), calls=%async_computation | async-start | bytes 2097152 | tf_op jit(solution)/shard_map/all_to_all | solution.py:332
  87.2 0.8 broadcast_add_fusion
  88.0 0.8 copy.43
  88.8 0.8 reshape.135
  89.7 1.6 fusion.24
  91.3 1.8 %fusion.5 = f32[4,256,256]{1,2,0:T(8,128)S(1)} fusion(f32[4,256,256]{1,2,0:T(8,128)S(1)} %fusion.24, s32[4]{0:T(128)S(1)} %fusion.42, f32[256]{0:T(256)S(1)} %fusion.43, s32[256,256]{0,1:T(8,128)S(1)} %copy-done.6), kind=kOutput, calls=%fused_computation.14 | convolution fusion | flops 405733376 | bytes 2360336 | tf_op jit(solution)/shard_map/ky,xyz->xkz/dot_general | solution.py:32
  93.1 1.6 convolution_bitcast_fusion
  94.8 1.9 %fusion.20 = f32[4,256,256]{2,1,0:T(8,128)S(1)} fusion(f32[4,256,256]{1,2,0:T(8,128)S(1)} %convolution_bitcast_fusion), kind=kOutput, calls=%fused_computation.39 | convolution fusion | flops 403636224 | bytes 2097152 | tf_op jit(solution)/shard_map/kz,xyz->xyk/dot_general | solution.py:32
  96.6 0.5 reshape.136
  97.2 1.1 copy.26
  98.3 14.1 %all-to-all-done = f32[32,4,16,128]{3,2,1,0:T(8,128)S(1)} async-done(((f32[32,4,16,128]{3,2,1,0:T(8,128)}), f32[32,4,16,128]{3,2,1,0:T(8,128)S(1)}, u32[]{:S(2)}, u32[]{:S(2)}) %all-to-all-start) | async-done | bytes 1048608 | tf_op jit(solution)/shard_map/all_to_all | solution.py:332
  112.4 4.6 %all-to-all-start.3 = ((f32[32,4,16,128]{3,2,1,0:T(8,128)}), f32[32,4,16,128]{3,2,1,0:T(8,128)S(1)}, u32[]{:S(2)}, u32[]{:S(2)}) async-start(f32[32,4,16,128]{3,2,1,0:T(8,128)} %bitcast.29), calls=%async_computation.3 | async-start | bytes 2097152 | tf_op jit(solution)/shard_map/all_to_all | solution.py:349
  117.0 0.8 copy.44
  117.9 0.8 reshape.130
  118.7 1.6 fusion.30
  120.4 1.8 %fusion.4 = f32[4,256,256]{1,2,0:T(8,128)S(1)} fusion(f32[4,256,256]{1,2,0:T(8,128)S(1)} %fusion.30, f32[256]{0:T(256)S(1)} %fusion.43, s32[4]{0:T(128)S(1)} %fusion.41, s32[256,256]{0,1:T(8,128)S(1)} %copy-done.7), kind=kOutput, calls=%fused_computation.13 | convolution fusion | flops 405733376 | bytes 2360336 | tf_op jit(solution)/shard_map/ky,xyz->xkz/dot_general | solution.py:32
  122.1 1.6 convolution_bitcast_fusion.2
  123.8 1.9 %fusion.26 = f32[4,256,256]{2,1,0:T(8,128)S(1)} fusion(f32[4,256,256]{1,2,0:T(8,128)S(1)} %convolution_bitcast_fusion.2), kind=kOutput, calls=%fused_computation.45 | convolution fusion | flops 403636224 | bytes 2097152 | tf_op jit(solution)/shard_map/kz,xyz->xyk/dot_general | solution.py:32
  125.7 0.5 reshape.131
  126.2 1.1 copy.19
  127.3 14.9 %all-to-all-done.3 = f32[32,4,16,128]{3,2,1,0:T(8,128)S(1)} async-done(((f32[32,4,16,128]{3,2,1,0:T(8,128)}), f32[32,4,16,128]{3,2,1,0:T(8,128)S(1)}, u32[]{:S(2)}, u32[]{:S(2)}) %all-to-all-start.3) | async-done | bytes 1048608 | tf_op jit(solution)/shard_map/all_to_all | solution.py:349
  142.3 4.6 %all-to-all-start.1 = ((f32[32,4,16,128]{3,2,1,0:T(8,128)}), f32[32,4,16,128]{3,2,1,0:T(8,128)S(1)}, u32[]{:S(2)}, u32[]{:S(2)}) async-start(f32[32,4,16,128]{3,2,1,0:T(8,128)} %bitcast.18), calls=%async_computation.1 | async-start | bytes 2097152 | tf_op jit(solution)/shard_map/all_to_all | solution.py:349
  147.2 6.9 %shard_map.71 = f32[2,16,128,256]{3,2,1,0:T(8,128)} custom-call(f32[2,16,128,256]{3,2,1,0:T(8,128)} %get-tuple-element.25.w_ref.w_prev.w_next, f32[2,16,128,256]{3,2,1,0:T(8,128)} %get-tuple-element.25.w_ref.w_prev.w_next, f32[2,16,128,256]{3,2,1,0:T(8,128)} %get-tuple-element.25.w_ref.w_prev.w_next, f32[2,128,256]{2,1,0:T(8,128)} %copy-done.4, ...), custom_call_target="tpu_custom_call" | custom-call | tf_op jit(solution)/shard_map/pallas_call | solution.py:299
  154.1 0.3 copy.41
  154.4 1.3 copy.27
  155.8 16.4 %all-to-all-done.1 = f32[32,4,16,128]{3,2,1,0:T(8,128)S(1)} async-done(((f32[32,4,16,128]{3,2,1,0:T(8,128)}), f32[32,4,16,128]{3,2,1,0:T(8,128)S(1)}, u32[]{:S(2)}, u32[]{:S(2)}) %all-to-all-start.1) | async-done | bytes 1048608 | tf_op jit(solution)/shard_map/all_to_all | solution.py:349
  172.8 1.0 fusion.79
  174.0 2.4 %add_multiply_fusion = f32[16,128,256]{2,1,0:T(8,128)} fusion(f32[16,128,256]{2,1,0:T(8,128)S(1)} %fusion.79, f32[16,128,128]{2,1,0:T(8,128)S(1)} %bitcast.115, f32[128,256,1]{1,0,2:T(8,128)S(1)} %reshape.144), kind=kOutput, calls=%fused_computation.4 | convolution fusion | flops 403701760 | bytes 5373952 | tf_op jit(solution)/shard_map/kn,km->mn/dot_general | solution.py:32
  (38 shorter events, 1.7 us)
Async XLA Ops:
  5.2 15.9 %collective-permute-start = (f32[6,128,256]{2,1,0:T(8,128)}, f32[6,128,256]{2,1,0:T(8,128)S(1)}, u32[]{:S(2)}, u32[]{:S(2)}) collective-permute-start(f32[6,128,256]{2,1,0:T(8,128)} %get-tuple-element.21), channel_id=1, source_target_pairs={{0,2},{2,4},{4,6},{6,8},{8,10},{10,12},{12,14},{14,16},{16,18},{18... | collective-permute-start | bytes 2359304 | tf_op jit(solution)/shard_map/ppermute | solution.py:251
  5.2 15.9 %collective-permute-start.1 = (f32[6,128,256]{2,1,0:T(8,128)}, f32[6,128,256]{2,1,0:T(8,128)S(1)}, u32[]{:S(2)}, u32[]{:S(2)}) collective-permute-start(f32[6,128,256]{2,1,0:T(8,128)} %get-tuple-element.22), channel_id=1, source_target_pairs={{2,0},{4,2},{6,4},{8,6},{10,8},{12,10},{14,12},{16,14},{18,16},{20... | collective-permute-start | bytes 2359304 | tf_op jit(solution)/shard_map/ppermute | solution.py:251
  9.0 11.2 %collective-permute-start.2 = (f32[2,6,16,1,256]{4,3,2,1,0:T(1,128)S(1)}, f32[2,6,16,1,256]{4,3,2,1,0:T(1,128)S(1)}, u32[]{:S(2)}, u32[]{:S(2)}) collective-permute-start(f32[2,6,16,1,256]{4,3,2,1,0:T(1,128)S(1)} %pad_maximum_fusion), channel_id=1, source_target_pairs={{0,1},{1,0},{2,3},{3,2},{4,5},{5,4},{6,7},{7,6},{8,9},{9,8},{10,11... | collective-permute-start | bytes 589832 | tf_op jit(solution)/shard_map/ppermute | solution.py:248
  21.1 1.0 copy-start.2
  21.1 1.2 copy-start.3
  41.2 11.7 %copy-start.8 = (f32[2,16,1,256]{3,2,1,0:T(1,128)S(1)}, f32[2,16,1,256]{3,2,1,0:T(1,128)}, u32[]{:S(2)}) copy-start(f32[2,16,1,256]{3,2,1,0:T(1,128)} %get-tuple-element.29) | copy-start | bytes 98308
  41.2 11.7 %copy-start.9 = (f32[2,16,1,256]{3,2,1,0:T(1,128)S(1)}, f32[2,16,1,256]{3,2,1,0:T(1,128)}, u32[]{:S(2)}) copy-start(f32[2,16,1,256]{3,2,1,0:T(1,128)} %get-tuple-element.28) | copy-start | bytes 98308
  41.2 16.0 %copy-start = (f32[16,128,256]{2,1,0:T(8,128)S(1)}, f32[16,128,256]{2,1,0:T(8,128)}, u32[]{:S(2)}) copy-start(f32[16,128,256]{2,1,0:T(8,128)} %get-tuple-element.30) | copy-start | bytes 6291460
  42.8 40.6 %all-to-all-start.2 = ((f32[32,4,16,128]{3,2,1,0:T(8,128)}), f32[32,4,16,128]{3,2,1,0:T(8,128)S(1)}, u32[]{:S(2)}, u32[]{:S(2)}) async-start(f32[32,4,16,128]{3,2,1,0:T(8,128)} %copy.22), calls=%async_computation.2 | async-start | bytes 2097152 | tf_op jit(solution)/shard_map/all_to_all | solution.py:332
  53.0 9.9 %collective-permute-start.5 = (f32[2,2,16,1,256]{4,3,2,1,0:T(1,128)S(1)}, f32[2,2,16,1,256]{4,3,2,1,0:T(1,128)S(1)}, u32[]{:S(2)}, u32[]{:S(2)}) collective-permute-start(f32[2,2,16,1,256]{4,3,2,1,0:T(1,128)S(1)} %pad_maximum_fusion.1), channel_id=1, source_target_pairs={{0,1},{1,0},{2,3},{3,2},{4,5},{5,4},{6,7},{7,6},{8,9},{9,8},{10,11... | collective-permute-start | bytes 196616 | tf_op jit(solution)/shard_map/ppermute | solution.py:248
  54.6 26.5 %collective-permute-start.3 = (f32[2,128,256]{2,1,0:T(8,128)}, f32[2,128,256]{2,1,0:T(8,128)S(1)}, u32[]{:S(2)}, u32[]{:S(2)}) collective-permute-start(f32[2,128,256]{2,1,0:T(8,128)} %get-tuple-element.26), channel_id=1, source_target_pairs={{0,2},{2,4},{4,6},{6,8},{8,10},{10,12},{12,14},{14,16},{16,18},{18... | collective-permute-start | bytes 786440 | tf_op jit(solution)/shard_map/ppermute | solution.py:251
  54.6 26.5 %collective-permute-start.4 = (f32[2,128,256]{2,1,0:T(8,128)}, f32[2,128,256]{2,1,0:T(8,128)S(1)}, u32[]{:S(2)}, u32[]{:S(2)}) collective-permute-start(f32[2,128,256]{2,1,0:T(8,128)} %get-tuple-element.27), channel_id=1, source_target_pairs={{2,0},{4,2},{6,4},{8,6},{10,8},{12,10},{14,12},{16,14},{18,16},{20... | collective-permute-start | bytes 786440 | tf_op jit(solution)/shard_map/ppermute | solution.py:251
  81.0 0.7 copy-start.4
  81.0 0.8 copy-start.5
  83.4 29.0 %all-to-all-start = ((f32[32,4,16,128]{3,2,1,0:T(8,128)}), f32[32,4,16,128]{3,2,1,0:T(8,128)S(1)}, u32[]{:S(2)}, u32[]{:S(2)}) async-start(f32[32,4,16,128]{3,2,1,0:T(8,128)} %copy.15), calls=%async_computation | async-start | bytes 2097152 | tf_op jit(solution)/shard_map/all_to_all | solution.py:332
  89.7 1.7 copy-start.6
  112.4 29.9 %all-to-all-start.3 = ((f32[32,4,16,128]{3,2,1,0:T(8,128)}), f32[32,4,16,128]{3,2,1,0:T(8,128)S(1)}, u32[]{:S(2)}, u32[]{:S(2)}) async-start(f32[32,4,16,128]{3,2,1,0:T(8,128)} %bitcast.29), calls=%async_computation.3 | async-start | bytes 2097152 | tf_op jit(solution)/shard_map/all_to_all | solution.py:349
  118.7 1.7 copy-start.7
  142.3 29.9 %all-to-all-start.1 = ((f32[32,4,16,128]{3,2,1,0:T(8,128)}), f32[32,4,16,128]{3,2,1,0:T(8,128)S(1)}, u32[]{:S(2)}, u32[]{:S(2)}) async-start(f32[32,4,16,128]{3,2,1,0:T(8,128)} %bitcast.18), calls=%async_computation.1 | async-start | bytes 2097152 | tf_op jit(solution)/shard_map/all_to_all | solution.py:349
  172.8 1.2 copy-start.1

commit v12 on v11

--- a/solution.py
+++ b/solution.py
@@ -348,10 +348,10 @@
         spec = spec.transpose(1, 3, 0, 2, 4).reshape(parts, piece_x, block_y, block_z)
         spec = lax.all_to_all(spec, ("gy", "gz"), 0, 0, tiled=True)
         rows_in = spec.reshape(parts * piece_x, block_y * block_z)
-        part = along("kn,km->mn", table_x[:, p].reshape(parts * piece_x, length_x), rows_in)
+        part = along("kn,km->mn", (table_x[:, p] * scale).reshape(parts * piece_x, length_x), rows_in)
         part = part.reshape(block_y, block_z, length_x)
         result = part if result is None else result + part
-    return result * scale, lam
+    return result, lam
 
 
 def per_device(mag_start, mag_middle, adjoint_end, phase, labels):

time: 179 us -> 179 us (level)
  no operation moved by 1% of the time
where the time goes in v12:
time: 179 us; the launch traced here: 176 us
  waiting for transfers between devices  67.5 us (38%)
  Pallas kernels  36.1 us (20%)
  starting transfers between devices  31.5 us (18%)
  matrix products  21.1 us (12%)
  local copies, waits for them, and re-layouts  16 us (9%)
  other arithmetic  3.18 us (2%)
    all_to_all x2, waiting for transfers between devices, dipole_adjoint(): spec = lax.all_to_all(spec, ('gy', 'gz'), 0, 0, tiled=True)  31.3 us
    dot_general x12, matrix products, along(): return jnp.einsum(spec, table, values, precision=lax.Precision.HIGH)  21.1 us
    ppermute x2, waiting for transfers between devices, send_edges(): lax.ppermute(last, axis, up)  17.5 us
    pallas_call x1, Pallas kernels, backward_sections(): pl.pallas_call(functools.partial(first_kernel, rows=rows), grid=grid, in_...  16.1 us
    all_to_all x2, waiting for transfers between devices, dipole_adjoint(): sent.append(lax.all_to_all(spec, ('gy', 'gz'), 0, 0, tiled=True))  14.1 us
    all_to_all x2, starting transfers between devices, dipole_adjoint(): sent.append(lax.all_to_all(spec, ('gy', 'gz'), 0, 0, tiled=True))  13.9 us
    all_to_all x2, starting transfers between devices, dipole_adjoint(): spec = lax.all_to_all(spec, ('gy', 'gz'), 0, 0, tiled=True)  9.21 us
    pallas_call x1, Pallas kernels, backward_sections(): pl.pallas_call(functools.partial(factor_kernel, rows=rows), grid=grid, in...  8.56 us
  transfers between devices with their start and end apart: 10, of which 5 were waited for; matrix products, arithmetic and copies ran while one was open for 17% of the time, Pallas kernels for 9%

profile of v12, /device:TPU:16, one launch (start us, length us, event | category | flops | bytes accessed | tf_op | source)
XLA Modules:
  0.0 176.4 jit_solution(17150828778318988149)
XLA Ops:
  0.6 4.5 %shard_map.69 = (f32[6,128,256]{2,1,0:T(8,128)}, f32[6,128,256]{2,1,0:T(8,128)}, f32[6,16,1,256]{3,2,1,0:T(1,128)}, f32[6,16,1,256]{3,2,1,0:T(1,128)}) custom-call(f32[2,16,128,256]{3,2,1,0:T(8,128)} %refs_2_.3, f32[2,16,128,256]{3,2,1,0:T(8,128)} %refs_2_.3, f32[2,16,128,256]{3,2,1,0:T(8,128)} %refs_2_.3, f32[2,16,128,256]{3,2,1,0:T(8,128)} %refs_2_.3, ...), custom_call_target="tpu_custom_call" | custom-call | tf_op jit(solution)/shard_map/pallas_call | solution.py:268
  5.2 2.6 %collective-permute-start.1 = (f32[6,128,256]{2,1,0:T(8,128)}, f32[6,128,256]{2,1,0:T(8,128)S(1)}, u32[]{:S(2)}, u32[]{:S(2)}) collective-permute-start(f32[6,128,256]{2,1,0:T(8,128)} %get-tuple-element.22), channel_id=1, source_target_pairs={{2,0},{4,2},{6,4},{8,6},{10,8},{12,10},{14,12},{16,14},{18,16},{20... | collective-permute-start | bytes 2359304 | tf_op jit(solution)/shard_map/ppermute | solution.py:251
  7.9 1.1 pad_maximum_fusion
  9.0 1.6 collective-permute-start.2
  10.6 8.6 %shard_map.68 = (f32[2,16,128,256]{3,2,1,0:T(8,128)}, f32[2,16,128,256]{3,2,1,0:T(8,128)}) custom-call(f32[2,16,128,256]{3,2,1,0:T(8,128)} %refs_11_.1, f32[16,128,256]{2,1,0:T(8,128)} %refs_15_.1, s32[16,128,256]{2,1,0:T(8,128)} %refs_19_.1), custom_call_target="tpu_custom_call" | custom-call | tf_op jit(solution)/shard_map/pallas_call | solution.py:276
  19.1 1.1 sine_add_fusion.1
  20.3 0.8 slice_bitcast_fusion
  21.1 1.0 copy-done.2
  22.3 16.1 %shard_map.70 = (f32[16,128,256]{2,1,0:T(8,128)}, f32[2,16,128,256]{3,2,1,0:T(8,128)}, f32[2,128,256]{2,1,0:T(8,128)}, f32[2,128,256]{2,1,0:T(8,128)}, f32[2,16,...) custom-call(f32[2,16,128,256]{3,2,1,0:T(8,128)} %refs_2_.3, f32[2,16,128,256]{3,2,1,0:T(8,128)} %refs_2_.3, ...), custom_call_target="tpu_custom_call" | custom-call | tf_op jit(solution)/shard_map/pallas_call | solution.py:283
  38.4 2.8 %fusion = f32[32,4,16,128]{3,0,2,1:T(8,128)S(1)} fusion(f32[16,128,256]{2,1,0:T(8,128)} %get-tuple-element.30, f32[32,2,4,256]{3,0,2,1:T(8,128)S(1)} %sine_add_fusion.1), kind=kOutput, calls=%fused_computation | convolution fusion | flops 402653184 | bytes 3276800 | tf_op jit(solution)/shard_map/sxn,yzn->sxyz/dot_general | solution.py:32
  41.2 1.6 copy.22
  42.8 10.1 %all-to-all-start.2 = ((f32[32,4,16,128]{3,2,1,0:T(8,128)}), f32[32,4,16,128]{3,2,1,0:T(8,128)S(1)}, u32[]{:S(2)}, u32[]{:S(2)}) async-start(f32[32,4,16,128]{3,2,1,0:T(8,128)} %copy.22), calls=%async_computation.2 | async-start | bytes 2097152 | tf_op jit(solution)/shard_map/all_to_all | solution.py:332
  53.0 1.5 collective-permute-start.5
  54.6 2.6 %collective-permute-start.4 = (f32[2,128,256]{2,1,0:T(8,128)}, f32[2,128,256]{2,1,0:T(8,128)S(1)}, u32[]{:S(2)}, u32[]{:S(2)}) collective-permute-start(f32[2,128,256]{2,1,0:T(8,128)} %get-tuple-element.27), channel_id=1, source_target_pairs={{2,0},{4,2},{6,4},{8,6},{10,8},{12,10},{14,12},{16,14},{18,16},{20... | collective-permute-start | bytes 786440 | tf_op jit(solution)/shard_map/ppermute | solution.py:251
  57.2 1.2 fusion.2
  58.4 4.6 %collective-permute-done.5 = f32[2,2,16,1,256]{4,3,2,1,0:T(1,128)S(1)} collective-permute-done((f32[2,2,16,1,256]{4,3,2,1,0:T(1,128)S(1)}, f32[2,2,16,1,256]{4,3,2,1,0:T(1,128)S(1)}, u32[]{:S(2)}, u32[]{:S(2)}) %collective-permute-start.5) | collective-permute-done | bytes 65568 | tf_op jit(solution)/shard_map/ppermute | solution.py:248
  62.9 0.6 slice_bitcast_fusion.2
  63.6 17.4 %collective-permute-done.3.y_low_ref = f32[2,128,256]{2,1,0:T(8,128)S(1)} collective-permute-done((f32[2,128,256]{2,1,0:T(8,128)}, f32[2,128,256]{2,1,0:T(8,128)S(1)}, u32[]{:S(2)}, u32[]{:S(2)}) %collective-permute-start.3) | collective-permute-done | bytes 262176 | tf_op jit(solution)/shard_map/ppermute | solution.py:251
  81.0 0.7 copy-done.4
  81.8 1.6 copy.15
  83.4 3.7 %all-to-all-start = ((f32[32,4,16,128]{3,2,1,0:T(8,128)}), f32[32,4,16,128]{3,2,1,0:T(8,128)S(1)}, u32[]{:S(2)}, u32[]{:S(2)}) async-start(f32[32,4,16,128]{3,2,1,0:T(8,128)} %copy.15), calls=%async_computation | async-start | bytes 2097152 | tf_op jit(solution)/shard_map/all_to_all | solution.py:332
  87.2 0.8 broadcast_add_fusion
  88.0 0.8 copy.43
  88.8 0.8 reshape.141
  89.7 1.6 fusion.24
  91.3 1.8 %fusion.5 = f32[4,256,256]{1,2,0:T(8,128)S(1)} fusion(f32[4,256,256]{1,2,0:T(8,128)S(1)} %fusion.24, s32[4]{0:T(128)S(1)} %fusion.44, f32[256]{0:T(256)S(1)} %fusion.45, s32[256,256]{0,1:T(8,128)S(1)} %copy-done.6), kind=kOutput, calls=%fused_computation.14 | convolution fusion | flops 405733376 | bytes 2360336 | tf_op jit(solution)/shard_map/ky,xyz->xkz/dot_general | solution.py:32
  93.1 1.6 convolution_bitcast_fusion
  94.8 1.9 %fusion.20 = f32[4,256,256]{2,1,0:T(8,128)S(1)} fusion(f32[4,256,256]{1,2,0:T(8,128)S(1)} %convolution_bitcast_fusion), kind=kOutput, calls=%fused_computation.39 | convolution fusion | flops 403636224 | bytes 2097152 | tf_op jit(solution)/shard_map/kz,xyz->xyk/dot_general | solution.py:32
  96.6 0.5 reshape.142
  97.2 1.1 copy.26
  98.3 14.1 %all-to-all-done = f32[32,4,16,128]{3,2,1,0:T(8,128)S(1)} async-done(((f32[32,4,16,128]{3,2,1,0:T(8,128)}), f32[32,4,16,128]{3,2,1,0:T(8,128)S(1)}, u32[]{:S(2)}, u32[]{:S(2)}) %all-to-all-start) | async-done | bytes 1048608 | tf_op jit(solution)/shard_map/all_to_all | solution.py:332
  112.4 4.6 %all-to-all-start.3 = ((f32[32,4,16,128]{3,2,1,0:T(8,128)}), f32[32,4,16,128]{3,2,1,0:T(8,128)S(1)}, u32[]{:S(2)}, u32[]{:S(2)}) async-start(f32[32,4,16,128]{3,2,1,0:T(8,128)} %bitcast.29), calls=%async_computation.3 | async-start | bytes 2097152 | tf_op jit(solution)/shard_map/all_to_all | solution.py:349
  117.0 0.8 copy.44
  117.9 0.8 reshape.136
  118.7 1.6 fusion.30
  120.4 1.8 %fusion.4 = f32[4,256,256]{1,2,0:T(8,128)S(1)} fusion(f32[4,256,256]{1,2,0:T(8,128)S(1)} %fusion.30, f32[256]{0:T(256)S(1)} %fusion.45, s32[4]{0:T(128)S(1)} %fusion.43, s32[256,256]{0,1:T(8,128)S(1)} %copy-done.7), kind=kOutput, calls=%fused_computation.13 | convolution fusion | flops 405733376 | bytes 2360336 | tf_op jit(solution)/shard_map/ky,xyz->xkz/dot_general | solution.py:32
  122.1 1.6 convolution_bitcast_fusion.2
  123.8 1.9 %fusion.26 = f32[4,256,256]{2,1,0:T(8,128)S(1)} fusion(f32[4,256,256]{1,2,0:T(8,128)S(1)} %convolution_bitcast_fusion.2), kind=kOutput, calls=%fused_computation.45 | convolution fusion | flops 403636224 | bytes 2097152 | tf_op jit(solution)/shard_map/kz,xyz->xyk/dot_general | solution.py:32
  125.7 0.5 reshape.137
  126.2 1.1 copy.19
  127.3 14.9 %all-to-all-done.3 = f32[32,4,16,128]{3,2,1,0:T(8,128)S(1)} async-done(((f32[32,4,16,128]{3,2,1,0:T(8,128)}), f32[32,4,16,128]{3,2,1,0:T(8,128)S(1)}, u32[]{:S(2)}, u32[]{:S(2)}) %all-to-all-start.3) | async-done | bytes 1048608 | tf_op jit(solution)/shard_map/all_to_all | solution.py:349
  142.3 4.6 %all-to-all-start.1 = ((f32[32,4,16,128]{3,2,1,0:T(8,128)}), f32[32,4,16,128]{3,2,1,0:T(8,128)S(1)}, u32[]{:S(2)}, u32[]{:S(2)}) async-start(f32[32,4,16,128]{3,2,1,0:T(8,128)} %bitcast.18), calls=%async_computation.1 | async-start | bytes 2097152 | tf_op jit(solution)/shard_map/all_to_all | solution.py:349
  147.2 6.9 %shard_map.71 = f32[2,16,128,256]{3,2,1,0:T(8,128)} custom-call(f32[2,16,128,256]{3,2,1,0:T(8,128)} %get-tuple-element.25.w_ref.w_prev.w_next, f32[2,16,128,256]{3,2,1,0:T(8,128)} %get-tuple-element.25.w_ref.w_prev.w_next, f32[2,16,128,256]{3,2,1,0:T(8,128)} %get-tuple-element.25.w_ref.w_prev.w_next, f32[2,128,256]{2,1,0:T(8,128)} %copy-done.4, ...), custom_call_target="tpu_custom_call" | custom-call | tf_op jit(solution)/shard_map/pallas_call | solution.py:299
  154.1 0.3 copy.41
  154.4 1.3 copy.27
  155.8 16.4 %all-to-all-done.1 = f32[32,4,16,128]{3,2,1,0:T(8,128)S(1)} async-done(((f32[32,4,16,128]{3,2,1,0:T(8,128)}), f32[32,4,16,128]{3,2,1,0:T(8,128)S(1)}, u32[]{:S(2)}, u32[]{:S(2)}) %all-to-all-start.1) | async-done | bytes 1048608 | tf_op jit(solution)/shard_map/all_to_all | solution.py:349
  172.8 1.0 fusion.78
  174.0 2.3 %convolution_add_fusion = f32[16,128,256]{2,1,0:T(8,128)} fusion(f32[16,128,256]{2,1,0:T(8,128)S(1)} %fusion.78, f32[16,128,128]{2,1,0:T(8,128)S(1)} %bitcast.115, f32[128,256,1]{1,0,2:T(8,128)S(1)} %reshape.150), kind=kOutput, calls=%fused_computation.4 | convolution fusion | flops 403177472 | bytes 5373952 | tf_op jit(solution)/shard_map/kn,km->mn/dot_general | solution.py:32
  (38 shorter events, 1.7 us)
Async XLA Ops:
  5.2 15.9 %collective-permute-start = (f32[6,128,256]{2,1,0:T(8,128)}, f32[6,128,256]{2,1,0:T(8,128)S(1)}, u32[]{:S(2)}, u32[]{:S(2)}) collective-permute-start(f32[6,128,256]{2,1,0:T(8,128)} %get-tuple-element.21), channel_id=1, source_target_pairs={{0,2},{2,4},{4,6},{6,8},{8,10},{10,12},{12,14},{14,16},{16,18},{18... | collective-permute-start | bytes 2359304 | tf_op jit(solution)/shard_map/ppermute | solution.py:251
  5.2 15.9 %collective-permute-start.1 = (f32[6,128,256]{2,1,0:T(8,128)}, f32[6,128,256]{2,1,0:T(8,128)S(1)}, u32[]{:S(2)}, u32[]{:S(2)}) collective-permute-start(f32[6,128,256]{2,1,0:T(8,128)} %get-tuple-element.22), channel_id=1, source_target_pairs={{2,0},{4,2},{6,4},{8,6},{10,8},{12,10},{14,12},{16,14},{18,16},{20... | collective-permute-start | bytes 2359304 | tf_op jit(solution)/shard_map/ppermute | solution.py:251
  9.0 11.2 %collective-permute-start.2 = (f32[2,6,16,1,256]{4,3,2,1,0:T(1,128)S(1)}, f32[2,6,16,1,256]{4,3,2,1,0:T(1,128)S(1)}, u32[]{:S(2)}, u32[]{:S(2)}) collective-permute-start(f32[2,6,16,1,256]{4,3,2,1,0:T(1,128)S(1)} %pad_maximum_fusion), channel_id=1, source_target_pairs={{0,1},{1,0},{2,3},{3,2},{4,5},{5,4},{6,7},{7,6},{8,9},{9,8},{10,11... | collective-permute-start | bytes 589832 | tf_op jit(solution)/shard_map/ppermute | solution.py:248
  21.1 1.0 copy-start.2
  21.1 1.2 copy-start.3
  41.2 11.7 %copy-start.8 = (f32[2,16,1,256]{3,2,1,0:T(1,128)S(1)}, f32[2,16,1,256]{3,2,1,0:T(1,128)}, u32[]{:S(2)}) copy-start(f32[2,16,1,256]{3,2,1,0:T(1,128)} %get-tuple-element.29) | copy-start | bytes 98308
  41.2 11.7 %copy-start.9 = (f32[2,16,1,256]{3,2,1,0:T(1,128)S(1)}, f32[2,16,1,256]{3,2,1,0:T(1,128)}, u32[]{:S(2)}) copy-start(f32[2,16,1,256]{3,2,1,0:T(1,128)} %get-tuple-element.28) | copy-start | bytes 98308
  41.2 16.0 %copy-start = (f32[16,128,256]{2,1,0:T(8,128)S(1)}, f32[16,128,256]{2,1,0:T(8,128)}, u32[]{:S(2)}) copy-start(f32[16,128,256]{2,1,0:T(8,128)} %get-tuple-element.30) | copy-start | bytes 6291460
  42.8 40.6 %all-to-all-start.2 = ((f32[32,4,16,128]{3,2,1,0:T(8,128)}), f32[32,4,16,128]{3,2,1,0:T(8,128)S(1)}, u32[]{:S(2)}, u32[]{:S(2)}) async-start(f32[32,4,16,128]{3,2,1,0:T(8,128)} %copy.22), calls=%async_computation.2 | async-start | bytes 2097152 | tf_op jit(solution)/shard_map/all_to_all | solution.py:332
  53.0 9.9 %collective-permute-start.5 = (f32[2,2,16,1,256]{4,3,2,1,0:T(1,128)S(1)}, f32[2,2,16,1,256]{4,3,2,1,0:T(1,128)S(1)}, u32[]{:S(2)}, u32[]{:S(2)}) collective-permute-start(f32[2,2,16,1,256]{4,3,2,1,0:T(1,128)S(1)} %pad_maximum_fusion.1), channel_id=1, source_target_pairs={{0,1},{1,0},{2,3},{3,2},{4,5},{5,4},{6,7},{7,6},{8,9},{9,8},{10,11... | collective-permute-start | bytes 196616 | tf_op jit(solution)/shard_map/ppermute | solution.py:248
  54.6 26.5 %collective-permute-start.3 = (f32[2,128,256]{2,1,0:T(8,128)}, f32[2,128,256]{2,1,0:T(8,128)S(1)}, u32[]{:S(2)}, u32[]{:S(2)}) collective-permute-start(f32[2,128,256]{2,1,0:T(8,128)} %get-tuple-element.26), channel_id=1, source_target_pairs={{0,2},{2,4},{4,6},{6,8},{8,10},{10,12},{12,14},{14,16},{16,18},{18... | collective-permute-start | bytes 786440 | tf_op jit(solution)/shard_map/ppermute | solution.py:251
  54.6 26.5 %collective-permute-start.4 = (f32[2,128,256]{2,1,0:T(8,128)}, f32[2,128,256]{2,1,0:T(8,128)S(1)}, u32[]{:S(2)}, u32[]{:S(2)}) collective-permute-start(f32[2,128,256]{2,1,0:T(8,128)} %get-tuple-element.27), channel_id=1, source_target_pairs={{2,0},{4,2},{6,4},{8,6},{10,8},{12,10},{14,12},{16,14},{18,16},{20... | collective-permute-start | bytes 786440 | tf_op jit(solution)/shard_map/ppermute | solution.py:251
  81.0 0.7 copy-start.4
  81.0 0.8 copy-start.5
  83.4 29.0 %all-to-all-start = ((f32[32,4,16,128]{3,2,1,0:T(8,128)}), f32[32,4,16,128]{3,2,1,0:T(8,128)S(1)}, u32[]{:S(2)}, u32[]{:S(2)}) async-start(f32[32,4,16,128]{3,2,1,0:T(8,128)} %copy.15), calls=%async_computation | async-start | bytes 2097152 | tf_op jit(solution)/shard_map/all_to_all | solution.py:332
  89.7 1.7 copy-start.6
  112.4 29.9 %all-to-all-start.3 = ((f32[32,4,16,128]{3,2,1,0:T(8,128)}), f32[32,4,16,128]{3,2,1,0:T(8,128)S(1)}, u32[]{:S(2)}, u32[]{:S(2)}) async-start(f32[32,4,16,128]{3,2,1,0:T(8,128)} %bitcast.29), calls=%async_computation.3 | async-start | bytes 2097152 | tf_op jit(solution)/shard_map/all_to_all | solution.py:349
  118.7 1.7 copy-start.7
  142.3 29.9 %all-to-all-start.1 = ((f32[32,4,16,128]{3,2,1,0:T(8,128)}), f32[32,4,16,128]{3,2,1,0:T(8,128)S(1)}, u32[]{:S(2)}, u32[]{:S(2)}) async-start(f32[32,4,16,128]{3,2,1,0:T(8,128)} %bitcast.18), calls=%async_computation.1 | async-start | bytes 2097152 | tf_op jit(solution)/shard_map/all_to_all | solution.py:349
  172.8 1.2 copy-start.1

commit v13 on v11

--- a/solution.py
+++ b/solution.py
@@ -326,10 +326,12 @@
     index = lax.axis_index("gy") * count_z + lax.axis_index("gz")
     sent = []
     for p in range(pieces):
-        spec = along("sxn,yzn->sxyz", table_x[:, p], phase_grad)
+        flat = along("kn,mn->km", table_x[:, p].reshape(parts * piece_x, length_x),
+                     phase_grad.reshape(block_y * block_z, length_x))
         if p == 0:
-            halos, spec = lax.optimization_barrier((halos, spec))
-        sent.append(lax.all_to_all(spec, ("gy", "gz"), 0, 0, tiled=True))
+            halos, flat = lax.optimization_barrier((halos, flat))
+        spec = lax.all_to_all(flat, ("gy", "gz"), 0, 0, tiled=True)
+        sent.append(spec.reshape(parts, piece_x, block_y, block_z))
         if p == 0:
             lam = finish(halos)
     result = None

time: 179 us -> 178 us (level)
  waiting for transfers between devices: 67.5 us -> 65.1 us
    another operation x0 -> x3, local copies, waits for them, and re-layouts: none -> 3.11 us  [dipole_adjoint(): spec = sent[p].reshape(count_y, count_z, piece_x, block_y, block_z)]
where the time goes in v13:
time: 178 us; the launch traced here: 175 us
  waiting for transfers between devices  65.1 us (37%)
  Pallas kernels  36.1 us (20%)
  starting transfers between devices  31.6 us (18%)
  matrix products  21.1 us (12%)
  local copies, waits for them, and re-layouts  17.4 us (10%)
  other arithmetic  3.14 us (2%)
    all_to_all x2, waiting for transfers between devices, dipole_adjoint(): spec = lax.all_to_all(spec, ('gy', 'gz'), 0, 0, tiled=True)  30.9 us
    dot_general x12, matrix products, along(): return jnp.einsum(spec, table, values, precision=lax.Precision.HIGH)  21.1 us
    ppermute x2, waiting for transfers between devices, send_edges(): lax.ppermute(last, axis, up)  17.6 us
    pallas_call x1, Pallas kernels, backward_sections(): pl.pallas_call(functools.partial(first_kernel, rows=rows), grid=grid, in_...  16.1 us
    all_to_all x2, starting transfers between devices, dipole_adjoint(): spec = lax.all_to_all(flat, ('gy', 'gz'), 0, 0, tiled=True)  14 us
    all_to_all x2, waiting for transfers between devices, dipole_adjoint(): spec = lax.all_to_all(flat, ('gy', 'gz'), 0, 0, tiled=True)  12.3 us
    all_to_all x2, starting transfers between devices, dipole_adjoint(): spec = lax.all_to_all(spec, ('gy', 'gz'), 0, 0, tiled=True)  9.21 us
    pallas_call x1, Pallas kernels, backward_sections(): pl.pallas_call(functools.partial(factor_kernel, rows=rows), grid=grid, in...  8.53 us
  transfers between devices with their start and end apart: 10, of which 5 were waited for; matrix products, arithmetic and copies ran while one was open for 17% of the time, Pallas kernels for 9%

profile of v13, /device:TPU:16, one launch (start us, length us, event | category | flops | bytes accessed | tf_op | source)
XLA Modules:
  0.0 175.4 jit_solution(530529957741006163)
XLA Ops:
  0.6 4.5 %shard_map.69 = (f32[6,128,256]{2,1,0:T(8,128)}, f32[6,128,256]{2,1,0:T(8,128)}, f32[6,16,1,256]{3,2,1,0:T(1,128)}, f32[6,16,1,256]{3,2,1,0:T(1,128)}) custom-call(f32[2,16,128,256]{3,2,1,0:T(8,128)} %refs_2_.3, f32[2,16,128,256]{3,2,1,0:T(8,128)} %refs_2_.3, f32[2,16,128,256]{3,2,1,0:T(8,128)} %refs_2_.3, f32[2,16,128,256]{3,2,1,0:T(8,128)} %refs_2_.3, ...), custom_call_target="tpu_custom_call" | custom-call | tf_op jit(solution)/shard_map/pallas_call | solution.py:268
  5.2 2.6 %collective-permute-start.1 = (f32[6,128,256]{2,1,0:T(8,128)}, f32[6,128,256]{2,1,0:T(8,128)S(1)}, u32[]{:S(2)}, u32[]{:S(2)}) collective-permute-start(f32[6,128,256]{2,1,0:T(8,128)} %get-tuple-element.22), channel_id=1, source_target_pairs={{2,0},{4,2},{6,4},{8,6},{10,8},{12,10},{14,12},{16,14},{18,16},{20... | collective-permute-start | bytes 2359304 | tf_op jit(solution)/shard_map/ppermute | solution.py:251
  7.9 1.1 pad_maximum_fusion
  9.0 1.6 collective-permute-start.2
  10.6 8.5 %shard_map.68 = (f32[2,16,128,256]{3,2,1,0:T(8,128)}, f32[2,16,128,256]{3,2,1,0:T(8,128)}) custom-call(f32[2,16,128,256]{3,2,1,0:T(8,128)} %refs_11_.1, f32[16,128,256]{2,1,0:T(8,128)} %refs_15_.1, s32[16,128,256]{2,1,0:T(8,128)} %refs_19_.1), custom_call_target="tpu_custom_call" | custom-call | tf_op jit(solution)/shard_map/pallas_call | solution.py:276
  19.1 1.1 sine_add_fusion.1
  20.2 0.8 slice_bitcast_fusion
  21.1 1.0 copy-done.2
  22.3 16.1 %shard_map.70 = (f32[16,128,256]{2,1,0:T(8,128)}, f32[2,16,128,256]{3,2,1,0:T(8,128)}, f32[2,128,256]{2,1,0:T(8,128)}, f32[2,128,256]{2,1,0:T(8,128)}, f32[2,16,...) custom-call(f32[2,16,128,256]{3,2,1,0:T(8,128)} %refs_2_.3, f32[2,16,128,256]{3,2,1,0:T(8,128)} %refs_2_.3, ...), custom_call_target="tpu_custom_call" | custom-call | tf_op jit(solution)/shard_map/pallas_call | solution.py:283
  38.4 2.8 %fusion.34 = f32[32,4,2048]{2,0,1:T(8,128)S(1)} fusion(f32[2048,256,1]{1,0,2:T(8,128)} %bitcast.97, f32[32,2,4,256]{3,0,2,1:T(8,128)S(1)} %sine_add_fusion.1), kind=kOutput, calls=%fused_computation.55 | convolution fusion | flops 402653184 | bytes 3276800 | tf_op jit(solution)/shard_map/kn,mn->km/dot_general | solution.py:32
  41.2 1.6 copy.35
  42.8 10.2 %all-to-all-start.2 = ((f32[32,4,2048]{2,1,0:T(4,128)}), f32[32,4,2048]{2,1,0:T(4,128)}, u32[]{:S(2)}, u32[]{:S(2)}) async-start(f32[32,4,2048]{2,1,0:T(4,128)} %copy.35), calls=%async_computation.2 | async-start | bytes 2097152 | tf_op jit(solution)/shard_map/all_to_all | solution.py:333
  53.3 1.5 collective-permute-start.5
  54.8 2.6 %collective-permute-start.4 = (f32[2,128,256]{2,1,0:T(8,128)}, f32[2,128,256]{2,1,0:T(8,128)}, u32[]{:S(2)}, u32[]{:S(2)}) collective-permute-start(f32[2,128,256]{2,1,0:T(8,128)} %get-tuple-element.27), channel_id=1, source_target_pairs={{2,0},{4,2},{6,4},{8,6},{10,8},{12,10},{14,12},{16,14},{18,16},{20... | collective-permute-start | bytes 786440 | tf_op jit(solution)/shard_map/ppermute | solution.py:251
  57.5 1.2 fusion.74
  58.6 4.3 %collective-permute-done.5 = f32[2,2,16,1,256]{4,3,2,1,0:T(1,128)S(1)} collective-permute-done((f32[2,2,16,1,256]{4,3,2,1,0:T(1,128)S(1)}, f32[2,2,16,1,256]{4,3,2,1,0:T(1,128)S(1)}, u32[]{:S(2)}, u32[]{:S(2)}) %collective-permute-start.5) | collective-permute-done | bytes 65568 | tf_op jit(solution)/shard_map/ppermute | solution.py:248
  63.0 0.6 slice_bitcast_fusion.2
  63.6 17.6 %collective-permute-done.3.y_low_ref = f32[2,128,256]{2,1,0:T(8,128)} collective-permute-done((f32[2,128,256]{2,1,0:T(8,128)}, f32[2,128,256]{2,1,0:T(8,128)}, u32[]{:S(2)}, u32[]{:S(2)}) %collective-permute-start.3) | collective-permute-done | bytes 262176 | tf_op jit(solution)/shard_map/ppermute | solution.py:251
  81.2 1.3 all_to_all.16
  82.4 3.7 %all-to-all-start = ((f32[32,4,2048]{2,1,0:T(4,128)}), f32[32,4,2048]{2,1,0:T(4,128)S(1)}, u32[]{:S(2)}, u32[]{:S(2)}) async-start(f32[32,4,2048]{2,1,0:T(4,128)} %all_to_all.16), calls=%async_computation | async-start | bytes 2097152 | tf_op jit(solution)/shard_map/all_to_all | solution.py:333
  86.2 0.8 broadcast_add_fusion
  87.0 1.8 %reshape_reshape.7 = f32[16,2,4,16,128]{4,3,2,1,0:T(8,128)S(1)} reshape(f32[32,4,2048]{2,1,0:T(4,128)} %all-to-all-done.2) | data formatting | bytes 2097152 | tf_op jit(solution)/shard_map/reshape;reshape | solution.py:339
  88.8 0.8 copy.55
  89.6 0.8 reshape.140
  90.5 1.6 fusion.20
  92.1 1.8 %fusion.1 = f32[4,256,256]{1,2,0:T(8,128)S(1)} fusion(f32[4,256,256]{1,2,0:T(8,128)S(1)} %fusion.20, s32[4]{0:T(128)S(1)} %fusion.38, f32[256]{0:T(256)S(1)} %fusion.39, s32[256,256]{0,1:T(8,128)S(1)} %copy-done.4), kind=kOutput, calls=%fused_computation.10 | convolution fusion | flops 405733376 | bytes 2360336 | tf_op jit(solution)/shard_map/ky,xyz->xkz/dot_general | solution.py:32
  93.9 1.6 convolution_bitcast_fusion
  95.6 1.9 %fusion.16 = f32[4,256,256]{2,1,0:T(8,128)S(1)} fusion(f32[4,256,256]{1,2,0:T(8,128)S(1)} %convolution_bitcast_fusion), kind=kOutput, calls=%fused_computation.34 | convolution fusion | flops 403636224 | bytes 2097152 | tf_op jit(solution)/shard_map/kz,xyz->xyk/dot_general | solution.py:32
  97.5 0.5 reshape.141
  98.0 1.1 copy.39
  99.1 12.3 %all-to-all-done = f32[32,4,2048]{2,1,0:T(4,128)S(1)} async-done(((f32[32,4,2048]{2,1,0:T(4,128)}), f32[32,4,2048]{2,1,0:T(4,128)S(1)}, u32[]{:S(2)}, u32[]{:S(2)}) %all-to-all-start) | async-done | bytes 1048608 | tf_op jit(solution)/shard_map/all_to_all | solution.py:333
  111.5 4.6 %all-to-all-start.3 = ((f32[32,4,16,128]{3,2,1,0:T(8,128)}), f32[32,4,16,128]{3,2,1,0:T(8,128)S(1)}, u32[]{:S(2)}, u32[]{:S(2)}) async-start(f32[32,4,16,128]{3,2,1,0:T(8,128)} %bitcast.24), calls=%async_computation.3 | async-start | bytes 2097152 | tf_op jit(solution)/shard_map/all_to_all | solution.py:351
  116.1 0.5 reshape.148
  116.6 0.8 copy.30
  117.4 0.8 reshape.136
  118.3 1.6 fusion.26
  120.0 1.8 %fusion = f32[4,256,256]{1,2,0:T(8,128)S(1)} fusion(f32[4,256,256]{1,2,0:T(8,128)S(1)} %fusion.26, f32[256]{0:T(256)S(1)} %fusion.39, s32[4]{0:T(128)S(1)} %fusion.37, s32[256,256]{0,1:T(8,128)S(1)} %copy-done.5), kind=kOutput, calls=%fused_computation.9 | convolution fusion | flops 405733376 | bytes 2360336 | tf_op jit(solution)/shard_map/ky,xyz->xkz/dot_general | solution.py:32
  121.7 1.6 convolution_bitcast_fusion.2
  123.4 1.9 %fusion.22 = f32[4,256,256]{2,1,0:T(8,128)S(1)} fusion(f32[4,256,256]{1,2,0:T(8,128)S(1)} %convolution_bitcast_fusion.2), kind=kOutput, calls=%fused_computation.40 | convolution fusion | flops 403636224 | bytes 2097152 | tf_op jit(solution)/shard_map/kz,xyz->xyk/dot_general | solution.py:32
  125.3 0.5 reshape.137
  125.8 1.1 copy.33
  126.9 14.4 %all-to-all-done.3 = f32[32,4,16,128]{3,2,1,0:T(8,128)S(1)} async-done(((f32[32,4,16,128]{3,2,1,0:T(8,128)}), f32[32,4,16,128]{3,2,1,0:T(8,128)S(1)}, u32[]{:S(2)}, u32[]{:S(2)}) %all-to-all-start.3) | async-done | bytes 1048608 | tf_op jit(solution)/shard_map/all_to_all | solution.py:351
  141.3 4.6 %all-to-all-start.1 = ((f32[32,4,16,128]{3,2,1,0:T(8,128)}), f32[32,4,16,128]{3,2,1,0:T(8,128)S(1)}, u32[]{:S(2)}, u32[]{:S(2)}) async-start(f32[32,4,16,128]{3,2,1,0:T(8,128)} %bitcast.15), calls=%async_computation.1 | async-start | bytes 2097152 | tf_op jit(solution)/shard_map/all_to_all | solution.py:351
  146.1 6.9 %shard_map.71 = f32[2,16,128,256]{3,2,1,0:T(8,128)} custom-call(f32[2,16,128,256]{3,2,1,0:T(8,128)} %get-tuple-element.25.w_ref.w_prev.w_next, f32[2,16,128,256]{3,2,1,0:T(8,128)} %get-tuple-element.25.w_ref.w_prev.w_next, f32[2,16,128,256]{3,2,1,0:T(8,128)} %get-tuple-element.25.w_ref.w_prev.w_next, f32[2,128,256]{2,1,0:T(8,128)} %collective-permute-done.3.y_low_ref, ...), custom_call_target="tpu_custom_call" | custom-call | tf_op jit(solution)/shard_map/pallas_call | solution.py:299
  153.4 1.3 copy.40
  154.7 16.5 %all-to-all-done.1 = f32[32,4,16,128]{3,2,1,0:T(8,128)S(1)} async-done(((f32[32,4,16,128]{3,2,1,0:T(8,128)}), f32[32,4,16,128]{3,2,1,0:T(8,128)S(1)}, u32[]{:S(2)}, u32[]{:S(2)}) %all-to-all-start.1) | async-done | bytes 1048608 | tf_op jit(solution)/shard_map/all_to_all | solution.py:351
  171.9 1.0 fusion.75
  173.1 2.4 %add_multiply_fusion = f32[16,128,256]{2,1,0:T(8,128)} fusion(f32[16,128,256]{2,1,0:T(8,128)S(1)} %fusion.75, f32[16,128,128]{2,1,0:T(8,128)S(1)} %bitcast.106, f32[128,256,1]{1,0,2:T(8,128)S(1)} %reshape.147), kind=kOutput, calls=%fused_computation | convolution fusion | flops 403701760 | bytes 5373952 | tf_op jit(solution)/shard_map/kn,km->mn/dot_general | solution.py:32
  (37 shorter events, 2.0 us)
Async XLA Ops:
  5.2 15.9 %collective-permute-start = (f32[6,128,256]{2,1,0:T(8,128)}, f32[6,128,256]{2,1,0:T(8,128)S(1)}, u32[]{:S(2)}, u32[]{:S(2)}) collective-permute-start(f32[6,128,256]{2,1,0:T(8,128)} %get-tuple-element.21), channel_id=1, source_target_pairs={{0,2},{2,4},{4,6},{6,8},{8,10},{10,12},{12,14},{14,16},{16,18},{18... | collective-permute-start | bytes 2359304 | tf_op jit(solution)/shard_map/ppermute | solution.py:251
  5.2 15.8 %collective-permute-start.1 = (f32[6,128,256]{2,1,0:T(8,128)}, f32[6,128,256]{2,1,0:T(8,128)S(1)}, u32[]{:S(2)}, u32[]{:S(2)}) collective-permute-start(f32[6,128,256]{2,1,0:T(8,128)} %get-tuple-element.22), channel_id=1, source_target_pairs={{2,0},{4,2},{6,4},{8,6},{10,8},{12,10},{14,12},{16,14},{18,16},{20... | collective-permute-start | bytes 2359304 | tf_op jit(solution)/shard_map/ppermute | solution.py:251
  9.0 11.2 %collective-permute-start.2 = (f32[2,6,16,1,256]{4,3,2,1,0:T(1,128)S(1)}, f32[2,6,16,1,256]{4,3,2,1,0:T(1,128)S(1)}, u32[]{:S(2)}, u32[]{:S(2)}) collective-permute-start(f32[2,6,16,1,256]{4,3,2,1,0:T(1,128)S(1)} %pad_maximum_fusion), channel_id=1, source_target_pairs={{0,1},{1,0},{2,3},{3,2},{4,5},{5,4},{6,7},{7,6},{8,9},{9,8},{10,11... | collective-permute-start | bytes 589832 | tf_op jit(solution)/shard_map/ppermute | solution.py:248
  21.1 1.0 copy-start.2
  21.1 1.2 copy-start.3
  42.8 10.4 %copy-start.6 = (f32[2,16,1,256]{3,2,1,0:T(1,128)S(1)}, f32[2,16,1,256]{3,2,1,0:T(1,128)}, u32[]{:S(2)}) copy-start(f32[2,16,1,256]{3,2,1,0:T(1,128)} %get-tuple-element.29) | copy-start | bytes 98308
  42.8 10.4 %copy-start.7 = (f32[2,16,1,256]{3,2,1,0:T(1,128)S(1)}, f32[2,16,1,256]{3,2,1,0:T(1,128)}, u32[]{:S(2)}) copy-start(f32[2,16,1,256]{3,2,1,0:T(1,128)} %get-tuple-element.28) | copy-start | bytes 98308
  42.8 14.7 %copy-start = (f32[16,128,256]{2,1,0:T(8,128)S(1)}, f32[16,128,256]{2,1,0:T(8,128)}, u32[]{:S(2)}) copy-start(f32[16,128,256]{2,1,0:T(8,128)} %get-tuple-element.30) | copy-start | bytes 6291460
  42.8 39.6 %all-to-all-start.2 = ((f32[32,4,2048]{2,1,0:T(4,128)}), f32[32,4,2048]{2,1,0:T(4,128)}, u32[]{:S(2)}, u32[]{:S(2)}) async-start(f32[32,4,2048]{2,1,0:T(4,128)} %copy.35), calls=%async_computation.2 | async-start | bytes 2097152 | tf_op jit(solution)/shard_map/all_to_all | solution.py:333
  53.3 9.7 %collective-permute-start.5 = (f32[2,2,16,1,256]{4,3,2,1,0:T(1,128)S(1)}, f32[2,2,16,1,256]{4,3,2,1,0:T(1,128)S(1)}, u32[]{:S(2)}, u32[]{:S(2)}) collective-permute-start(f32[2,2,16,1,256]{4,3,2,1,0:T(1,128)S(1)} %pad_maximum_fusion.1), channel_id=1, source_target_pairs={{0,1},{1,0},{2,3},{3,2},{4,5},{5,4},{6,7},{7,6},{8,9},{9,8},{10,11... | collective-permute-start | bytes 196616 | tf_op jit(solution)/shard_map/ppermute | solution.py:248
  54.8 26.3 %collective-permute-start.3 = (f32[2,128,256]{2,1,0:T(8,128)}, f32[2,128,256]{2,1,0:T(8,128)}, u32[]{:S(2)}, u32[]{:S(2)}) collective-permute-start(f32[2,128,256]{2,1,0:T(8,128)} %get-tuple-element.26), channel_id=1, source_target_pairs={{0,2},{2,4},{4,6},{6,8},{8,10},{10,12},{12,14},{14,16},{16,18},{18... | collective-permute-start | bytes 786440 | tf_op jit(solution)/shard_map/ppermute | solution.py:251
  54.8 26.3 %collective-permute-start.4 = (f32[2,128,256]{2,1,0:T(8,128)}, f32[2,128,256]{2,1,0:T(8,128)}, u32[]{:S(2)}, u32[]{:S(2)}) collective-permute-start(f32[2,128,256]{2,1,0:T(8,128)} %get-tuple-element.27), channel_id=1, source_target_pairs={{2,0},{4,2},{6,4},{8,6},{10,8},{12,10},{14,12},{16,14},{18,16},{20... | collective-permute-start | bytes 786440 | tf_op jit(solution)/shard_map/ppermute | solution.py:251
  82.4 29.0 %all-to-all-start = ((f32[32,4,2048]{2,1,0:T(4,128)}), f32[32,4,2048]{2,1,0:T(4,128)S(1)}, u32[]{:S(2)}, u32[]{:S(2)}) async-start(f32[32,4,2048]{2,1,0:T(4,128)} %all_to_all.16), calls=%async_computation | async-start | bytes 2097152 | tf_op jit(solution)/shard_map/all_to_all | solution.py:333
  90.5 1.7 copy-start.4
  111.5 29.9 %all-to-all-start.3 = ((f32[32,4,16,128]{3,2,1,0:T(8,128)}), f32[32,4,16,128]{3,2,1,0:T(8,128)S(1)}, u32[]{:S(2)}, u32[]{:S(2)}) async-start(f32[32,4,16,128]{3,2,1,0:T(8,128)} %bitcast.24), calls=%async_computation.3 | async-start | bytes 2097152 | tf_op jit(solution)/shard_map/all_to_all | solution.py:351
  118.3 1.7 copy-start.5
  141.3 29.9 %all-to-all-start.1 = ((f32[32,4,16,128]{3,2,1,0:T(8,128)}), f32[32,4,16,128]{3,2,1,0:T(8,128)S(1)}, u32[]{:S(2)}, u32[]{:S(2)}) async-start(f32[32,4,16,128]{3,2,1,0:T(8,128)} %bitcast.15), calls=%async_computation.1 | async-start | bytes 2097152 | tf_op jit(solution)/shard_map/all_to_all | solution.py:351
  171.9 1.2 copy-start.1
